TPU v7x, 256 devices: a whole 4x4x8 slice. The times are simulated.
256 devices in a mesh: dp: 8 (over y, core), seq: 32 (over x, z).
Axes of the slice: x: 4, y: 4, z: 8, core: 2. Of those that a mesh axis runs over, the one named last changes fastest.
Arguments:
- queries: bfloat16 [16, 2048, 1536], P('dp', 'seq'), may hold values from -6 to 6
- key_rows: bfloat16 [16, 2048, 1536], P('dp', 'seq'), may hold values from -6 to 6
- value_rows: bfloat16 [16, 2048, 1536], P('dp', 'seq'), may hold values from -6 to 6
- layer_input: bfloat16 [16, 2048, 1536], P('dp', 'seq'), may hold values from -6 to 6
- utt_lengths: int32 [16], P('dp'), may hold values from 512 to 2048, as said below
- out_weight: bfloat16 [1536, 1536], replicated, may hold values from -0.15625 to 0.15625
- conv_kernel: bfloat16 [31, 1536], replicated, may hold values from -1 to 1
- conv_cotangent: bfloat16 [16, 2048, 1536], P('dp', 'seq'), may hold values from -6 to 6
- pick_weight: int32 [23592], replicated, may hold values from 0 to 2359295
- pick_kernel: int32 [476], replicated, may hold values from 0 to 47615
Outputs:
- conv_out: bfloat16 [16, 2048, 1536], P('dp', 'seq')
- context_grad: bfloat16 [16, 2048, 1536], P('dp', 'seq')
- weight_picks: float32 [23592], replicated
- kernel_picks: float32 [476], replicated
Inputs may be any that keep to these rules, and one draw needn't show every extreme that they name: `utt_lengths`: the first utterance fills all 2048 slots and the last has 512 valid frames.
All inputs are finite; a program needn't handle non-finite values.
Results may differ from a plain program's by a relative error of at most 0.0056.
Values may be sent and summed in bfloat16 or wider, within the bound.
No kernel may reach another device: no remote copies, remote signals or barrier semaphores. Data moves between devices by JAX's collectives and lax.ppermute only.
A program may use at most 128 MiB of HBM per device.

v0:
```python
import math

import jax
import jax.numpy as jnp
from jax import lax
from jax.sharding import PartitionSpec as P

HEADS = 16


neg_big = -1e30


def padded(value, sides, width):
    for axis, dim in sides:
        count, length = (lax.axis_size(axis), value.shape[dim])
        up = [(i, (i + 1) % count) for i in range(count - 1)]
        down = [(j, i) for i, j in up]
        last = lax.slice_in_dim(value, length - width, length, axis=dim)
        leading = lax.slice_in_dim(value, 0, width, axis=dim)
        before = lax.ppermute(last, axis, up)
        after = lax.ppermute(leading, axis, down)
        value = jnp.concatenate([before, value, after], axis=dim)
    return value


def softmax_rows(scores, key_ok):
    scores = jnp.where(key_ok, scores, neg_big)
    row_max = jnp.max(scores, axis=-1, keepdims=True)
    probs = jnp.exp(scores - row_max)
    return (probs.astype(jnp.bfloat16), jnp.sum(probs, axis=-1))


def pick_entries(table, picks):
    flat = table.reshape(-1)
    lane = math.gcd(flat.shape[0], 128)
    blocks = flat.reshape(flat.shape[0] // lane, lane)
    chosen = jnp.take(blocks, picks // lane, axis=0)
    lane_ids = jnp.arange(lane, dtype=jnp.int32)
    hit = lane_ids[None, :] == (picks % lane)[:, None]
    return jnp.sum(jnp.where(hit, chosen, jnp.float32(0.0)), axis=1)

def group_picks(context_flat, grad_flat, picks, axis, levels):
    count = lax.axis_size(axis)
    levels = min(levels, count.bit_length() - 1)
    group = 1 << levels
    pair = jnp.stack([context_flat, grad_flat])
    for level in range(levels):
        step = 1 << level
        other = lax.ppermute(pair, axis, [(i, i ^ step) for i in range(count)])
        pair = jnp.concatenate([pair, other], axis=1)
    table = lax.dot_general(
        pair[0], pair[1], (((0,), (0,)), ((), ())), preferred_element_type=jnp.float32
    )
    total = picks.shape[0]
    rows = -(-total // group)
    padded_picks = jnp.pad(picks, (0, rows * group - total))
    first = (lax.axis_index(axis) % group) * rows
    mine = lax.dynamic_slice(padded_picks, (first,), (rows,))
    values = pick_entries(table, mine)
    spread = lax.dynamic_update_slice(jnp.zeros((rows * group,), jnp.float32), values, (first,))
    return spread[:total]


def butterfly_sum(value, axes):
    for axis in axes:
        count = lax.axis_size(axis)
        step = 1
        while step < count:
            pairs = [(i, i ^ step) for i in range(count)]
            value = value + lax.ppermute(value, axis, pairs)
            step *= 2
    return value


def attend(query, key, value, key_ok, score_scale):
    scores = jnp.dot(query, key.T, preferred_element_type=jnp.float32) * score_scale
    weights, denom = softmax_rows(scores, key_ok[None, :])
    out_rows = jnp.dot(weights, value, preferred_element_type=jnp.float32)
    return (out_rows / denom[:, None]).astype(jnp.bfloat16)


def head_attention(queries, key_rows, value_rows, utt_lengths, seq_index, score_scale, later):
    local_utts, frames_dev, width = queries.shape
    head_size = width // HEADS
    seq_count = HEADS * local_utts
    full_frames = frames_dev * seq_count
    stacked = jnp.stack([queries, key_rows, value_rows])
    stacked = stacked.reshape(3, local_utts, frames_dev, HEADS, head_size)
    stacked = stacked.transpose(3, 1, 0, 2, 4).reshape(seq_count, 3, frames_dev, head_size)
    gathered = lax.all_to_all(stacked, "seq", 0, 0, tiled=True)
    gathered, later = lax.optimization_barrier((gathered, later))
    gathered = gathered.transpose(1, 0, 2, 3).reshape(3, full_frames, head_size)
    length = utt_lengths[seq_index % local_utts]
    key_ok = jnp.arange(full_frames, dtype=jnp.int32) < length
    out_rows = attend(gathered[0], gathered[1], gathered[2], key_ok, score_scale)
    out_rows = out_rows.reshape(seq_count, frames_dev, head_size)
    back = lax.all_to_all(out_rows, "seq", 0, 0, tiled=True)
    back = back.reshape(HEADS, local_utts, frames_dev, head_size).transpose(1, 2, 0, 3)
    return back.reshape(local_utts, frames_dev, width), later


def frame_attention(queries, key_rows, value_rows, utt_lengths, score_scale):
    local_utts, frames_dev, width = queries.shape
    head_size = width // HEADS
    all_keys = lax.all_gather(key_rows, "seq", axis=1, tiled=True)
    all_values = lax.all_gather(value_rows, "seq", axis=1, tiled=True)
    full_frames = all_keys.shape[1]
    full_ids = jnp.arange(full_frames, dtype=jnp.int32)

    def one_utt(item):
        query_utt, key_utt, value_utt, length_utt = item
        query_heads = query_utt.reshape(frames_dev, HEADS, head_size)
        key_heads = key_utt.reshape(full_frames, HEADS, head_size)
        value_heads = value_utt.reshape(full_frames, HEADS, head_size)
        scores = (
            jnp.einsum("qhd,khd->hqk", query_heads, key_heads, preferred_element_type=jnp.float32)
            * score_scale
        )
        weights, denom = softmax_rows(scores, (full_ids < length_utt)[None, None, :])
        out_rows = jnp.einsum(
            "hqk,khd->qhd", weights, value_heads, preferred_element_type=jnp.float32
        )
        out_rows = out_rows / denom.transpose(1, 0)[:, :, None]
        return out_rows.astype(jnp.bfloat16).reshape(frames_dev, width)

    return lax.map(one_utt, (queries, all_keys, all_values, utt_lengths))


def on_device(
    queries,
    key_rows,
    value_rows,
    layer_input,
    utt_lengths,
    out_weight,
    conv_kernel,
    conv_cotangent,
    pick_weight,
    pick_kernel,
):
    local_utts, frames_dev, width = queries.shape
    seq_count = lax.axis_size("seq")
    full_frames = frames_dev * seq_count
    head_size = width // HEADS
    score_scale = 1.0 / math.sqrt(head_size)
    first_frame = lax.axis_index("seq") * frames_dev
    local_ids = first_frame + jnp.arange(frames_dev, dtype=jnp.int32)
    valid_rows = (local_ids[None, :] < utt_lengths[:, None]).astype(jnp.float32)
    seq_index = lax.axis_index("seq")
    if HEADS * local_utts == seq_count:
        context, conv_cotangent = head_attention(
            queries, key_rows, value_rows, utt_lengths, seq_index, score_scale, conv_cotangent
        )
    else:
        context = frame_attention(queries, key_rows, value_rows, utt_lengths, score_scale)
    context_flat = context.reshape(local_utts * frames_dev, width)
    projected = jnp.dot(context_flat, out_weight, preferred_element_type=jnp.float32).reshape(
        local_utts, frames_dev, width
    )
    hidden = ((layer_input.astype(jnp.float32) + projected) * valid_rows[:, :, None]).astype(
        jnp.bfloat16
    )
    tap_count = conv_kernel.shape[0]
    half_taps = (tap_count - 1) // 2
    kernel_f = conv_kernel.astype(jnp.float32)
    hidden_pad = padded(hidden, (("seq", 1),), half_taps)
    cot_f = conv_cotangent.astype(jnp.float32)
    conv_sum = jnp.zeros((local_utts, frames_dev, width), jnp.float32)
    kernel_rows = []
    for offset in range(tap_count):
        window = hidden_pad[:, offset : offset + frames_dev].astype(jnp.float32)
        conv_sum = conv_sum + kernel_f[offset] * window
        kernel_rows.append(jnp.sum(window * cot_f, axis=(0, 1)))
    conv_out = conv_sum.astype(jnp.bfloat16)
    kernel_grad = jnp.stack(kernel_rows)
    cot_pad = padded(conv_cotangent, (("seq", 1),), half_taps).astype(jnp.float32)
    back_sum = jnp.zeros((local_utts, frames_dev, width), jnp.float32)
    for offset in range(tap_count):
        begin = 2 * half_taps - offset
        back_sum = back_sum + kernel_f[offset] * cot_pad[:, begin : begin + frames_dev]
    hidden_grad = (back_sum * valid_rows[:, :, None]).astype(jnp.bfloat16)
    grad_flat = hidden_grad.reshape(local_utts * frames_dev, width)
    context_grad = lax.dot_general(
        grad_flat, out_weight, (((1,), (1,)), ((), ())), preferred_element_type=jnp.float32
    )
    context_grad = context_grad.reshape(local_utts, frames_dev, width).astype(jnp.bfloat16)
    weight_vals = group_picks(context_flat, grad_flat, pick_weight, "dp", 1)
    kernel_vals = pick_entries(kernel_grad, pick_kernel)
    joined = butterfly_sum(jnp.concatenate([weight_vals, kernel_vals]), ("dp", "seq"))
    weight_sum, kernel_sum = joined[: weight_vals.shape[0]], joined[weight_vals.shape[0] :]
    total_slots = local_utts * lax.axis_size("dp") * full_frames
    norm_factor = 1.0 / math.sqrt(total_slots)
    return (conv_out, context_grad, weight_sum * norm_factor, kernel_sum * norm_factor)


def solution(mesh):
    placed = (
        P("dp", "seq", None),
        P("dp", "seq", None),
        P("dp", "seq", None),
        P("dp", "seq", None),
        P("dp"),
        P(),
        P(),
        P("dp", "seq", None),
        P(),
        P(),
    )
    return jax.shard_map(
        on_device,
        mesh=mesh,
        in_specs=placed,
        out_specs=(P("dp", "seq", None), P("dp", "seq", None), P(), P()),
        check_vma=False,
    )
```

profile of v0, /device:TPU:16, one launch (start us, length us, event | category | flops | bytes accessed | tf_op | source)
XLA Modules:
  0.0 225.5 jit_solution(18418555050744117391)
XLA Ops:
  7.0 11.3 %all-to-all-start = ((bf16[32,3,64,96]{3,2,1,0:T(8,128)(2,1)}), bf16[32,3,64,96]{3,2,1,0:T(8,128)(2,1)S(1)}, u32[]{:S(2)}, u32[]{:S(2)}) async-start(bf16[32,3,64,96]{3,2,1,0:T(8,128)(2,1)} %bitcast.45), calls=%async_computation | async-start | bytes 3145728 | tf_op jit(solution)/shard_map/all_to_all | solution.py:91
  23.7 33.9 %all-to-all-done = bf16[32,3,64,96]{3,2,1,0:T(8,128)(2,1)S(1)} async-done(((bf16[32,3,64,96]{3,2,1,0:T(8,128)(2,1)}), bf16[32,3,64,96]{3,2,1,0:T(8,128)(2,1)S(1)}, u32[]{:S(2)}, u32[]{:S(2)}) %all-to-all-start) | async-done | bytes 1179680 | tf_op jit(solution)/shard_map/all_to_all | solution.py:91
  59.1 4.6 %collective-permute-start.2 = (bf16[2,15,1536]{2,1,0:T(8,128)(2,1)S(1)}, bf16[2,15,1536]{2,1,0:T(8,128)(2,1)S(1)}, u32[]{:S(2)}, u32[]{:S(2)}) collective-permute-start(bf16[2,15,1536]{2,1,0:T(8,128)(2,1)S(1)} %get-tuple-element.78), channel_id=1, source_target_pairs={{0,1},{1,2},{2,3},{3,4},{4,5},{5,6},{6,7},{7,8},{8,9},{9,10},{10,1... | collective-permute-start | bytes 276488 | tf_op jit(solution)/shard_map/ppermute | solution.py:21
  63.7 3.3 %fusion = (f32[2048]{0:T(1024)S(1)}, f32[2048,2048]{0,1:T(8,128)S(1)}) fusion(pred[2048]{0:T(1024)(128)(4,1)S(1)} %iota_compare_fusion.2, bf16[2048,96]{1,0:T(8,128)(2,1)S(1)} %bitcast.48, bf16[2048,96]{1,0:T(8,128)(2,1)S(1)} %bitcast.50), kind=kOutput, calls=%fused_computation.4 | convolution fusion | flops 817887232 | bytes 17573888 | tf_op jit(solution)/shard_map/dot_general | solution.py:77
  67.0 4.9 %fusion.1 = f32[2048]{0:T(1024)S(1)} fusion(f32[2048,2048]{0,1:T(8,128)S(1)} %get-tuple-element.83, f32[2048]{0:T(1024)S(1)} %get-tuple-element.82, pred[2048]{0:T(1024)(128)(4,1)S(1)} %iota_compare_fusion.2), kind=kLoop, calls=%fused_computation.5 | loop fusion | flops 16775168 | bytes 16795648 | tf_op jit(solution)/shard_map/reduce_sum | solution.py:31
  71.9 3.9 %fusion.25 = bf16[2048,96]{0,1:T(8,128)(2,1)S(1)} fusion(bf16[2048,96]{1,0:T(8,128)(2,1)S(1)} %bitcast.51, f32[2048,2048]{0,1:T(8,128)S(1)} %get-tuple-element.83, f32[2048]{0:T(1024)S(1)} %get-tuple-element.82, pred[2048]{0:T(1024)(128)(4,1)S(1)} %iota_compare_fusion.2, f32[2048]{0:T(1024)S(1)} %fusion.1), kind=kOutput, calls=%fused_computation.79 | convolution fusion | flops 822476800 | bytes 17582080 | tf_op jit(solution)/shard_map/dot_general | solution.py:79
  76.8 7.0 %all-to-all-start.1 = ((bf16[32,64,96]{2,1,0:T(8,128)(2,1)}), bf16[32,64,96]{2,1,0:T(8,128)(2,1)S(1)}, u32[]{:S(2)}, u32[]{:S(2)}) async-start(bf16[32,64,96]{2,1,0:T(8,128)(2,1)} %bitcast.7), calls=%async_computation.1 | async-start | bytes 1048576 | tf_op jit(solution)/shard_map/all_to_all | solution.py:98
  84.2 3.1 %fusion.93 = bf16[2,64,1536]{2,1,0:T(8,128)(2,1)S(1)} fusion(f32[2,94,1536]{2,1,0:T(8,128)S(1)} %maximum_convert_fusion, f32[1536]{0:T(1024)S(1)} %get-tuple-element.40, f32[1536]{0:T(1024)S(1)} %get-tuple-element.41, f32[1536]{0:T(1024)S(1)} %get-tuple-element.42, f32[1536]{0:T(1024)S(1)} %get-tuple-element.43, f32[1536]{0:T(1024)S(1)} %get-tuple-element.44, ...), kind=kLoop, calls=%fused_computation.181 | loop fusion | flops 12386304 | bytes 24963584 | tf_op jit(solution)/shard_map/convert_element_type | solution.py:182
  87.4 12.8 %all-to-all-done.1 = bf16[32,64,96]{2,1,0:T(8,128)(2,1)S(1)} async-done(((bf16[32,64,96]{2,1,0:T(8,128)(2,1)}), bf16[32,64,96]{2,1,0:T(8,128)(2,1)S(1)}, u32[]{:S(2)}, u32[]{:S(2)}) %all-to-all-start.1) | async-done | bytes 393248 | tf_op jit(solution)/shard_map/all_to_all | solution.py:98
  101.7 3.1 %fusion.19 = bf16[2,64,1536]{2,1,0:T(8,128)(2,1)S(1)} fusion(bf16[2,64,1536]{2,1,0:T(8,128)(2,1)S(1)} %dot_general.19, bf16[1536,1536]{1,0:T(8,128)(2,1)} %param.15, bf16[2,64,1536]{2,1,0:T(8,128)(2,1)S(1)} %copy-done.1, f32[2,64]{1,0:T(2,128)S(1)} %compare_convert_fusion), kind=kOutput, calls=%fused_computation.49 | convolution fusion | flops 604766208 | bytes 5898752 | tf_op jit(solution)/shard_map/dot_general | solution.py:158
  106.2 4.7 %collective-permute-start = (bf16[2,15,1536]{2,1,0:T(8,128)(2,1)S(1)}, bf16[2,15,1536]{2,1,0:T(8,128)(2,1)S(1)}, u32[]{:S(2)}, u32[]{:S(2)}) collective-permute-start(bf16[2,15,1536]{2,1,0:T(8,128)(2,1)S(1)} %get-tuple-element.80), channel_id=1, source_target_pairs={{0,1},{1,2},{2,3},{3,4},{4,5},{5,6},{6,7},{7,8},{8,9},{9,10},{10,1... | collective-permute-start | bytes 276488 | tf_op jit(solution)/shard_map/ppermute | solution.py:21
  120.3 5.1 %fusion.90 = f32[1536,1536]{1,0:T(8,128)} fusion(bf16[2,256,1536]{2,1,0:T(8,128)(2,1)S(1)} %pad_maximum_fusion), kind=kOutput, calls=%fused_computation.176 | convolution fusion | flops 1207959552 | bytes 11010048 | tf_op jit(solution)/shard_map/dot_general | solution.py:52
  125.4 10.6 %reshape_reshape.7 = f32[18432,128]{1,0:T(8,128)} reshape(f32[1536,1536]{1,0:T(8,128)} %fusion.90) | data formatting | bytes 18874368 | tf_op jit(solution)/shard_map/reshape;reshape | solution.py:37
  136.1 26.4 %gather_fusion = f32[11796,128]{1,0:T(8,128)} fusion(f32[18432,128]{1,0:T(8,128)} %reshape_reshape.7, s32[12288]{0:T(1024)S(1)} %copy-done.3), kind=kCustom, calls=%fused_computation | custom fusion | bytes 12126288 | tf_op jit(solution)/shard_map/jit(_take)/gather | solution.py:38
  162.5 10.5 %select_reduce_fusion = f32[11796]{0:T(1024)S(1)} fusion(f32[11796,128]{1,0:T(8,128)} %gather_fusion, s32[11796]{0:T(1024)S(1)} %copy-done.2, pred[11796]{0:T(1024)(128)(4,1)S(1)} %copy-done.64), kind=kLoop, calls=%fused_computation.40 | loop fusion | flops 6027756 | bytes 6145716 | tf_op jit(solution)/shard_map/reduce_sum | solution.py:41
  176.5 3.6 %collective-permute-done.6 = f32[24068]{0:T(1024)S(1)} collective-permute-done((f32[24068]{0:T(1024)S(1)}, f32[24068]{0:T(1024)S(1)}, u32[]{:S(2)}, u32[]{:S(2)}) %collective-permute-start.6) | collective-permute-done | bytes 96304 | tf_op jit(solution)/shard_map/ppermute | solution.py:71
  180.8 5.8 %collective-permute-done.7 = f32[24068]{0:T(1024)S(1)} collective-permute-done((f32[24068]{0:T(1024)S(1)}, f32[24068]{0:T(1024)S(1)}, u32[]{:S(2)}, u32[]{:S(2)}) %collective-permute-start.7) | collective-permute-done | bytes 96304 | tf_op jit(solution)/shard_map/ppermute | solution.py:71
  191.7 4.5 %collective-permute-start.9 = (f32[24068]{0:T(1024)S(1)}, f32[24068]{0:T(1024)S(1)}, u32[]{:S(2)}, u32[]{:S(2)}) collective-permute-start(f32[24068]{0:T(1024)S(1)} %add.337), channel_id=1, source_target_pairs={{0,2},{1,3},{2,0},{3,1},{4,6},{5,7},{6,4},{7,5},{8,10},{9,11},{10,... | collective-permute-start | bytes 288824 | tf_op jit(solution)/shard_map/ppermute | solution.py:71
  196.1 3.6 %collective-permute-done.9 = f32[24068]{0:T(1024)S(1)} collective-permute-done((f32[24068]{0:T(1024)S(1)}, f32[24068]{0:T(1024)S(1)}, u32[]{:S(2)}, u32[]{:S(2)}) %collective-permute-start.9) | collective-permute-done | bytes 96304 | tf_op jit(solution)/shard_map/ppermute | solution.py:71
  199.8 4.9 %collective-permute-start.10 = (f32[24068]{0:T(1024)S(1)}, f32[24068]{0:T(1024)S(1)}, u32[]{:S(2)}, u32[]{:S(2)}) collective-permute-start(f32[24068]{0:T(1024)S(1)} %add.338), channel_id=1, source_target_pairs={{0,4},{1,5},{2,6},{3,7},{4,0},{5,1},{6,2},{7,3},{8,12},{9,13},{10,... | collective-permute-start | bytes 288824 | tf_op jit(solution)/shard_map/ppermute | solution.py:71
  204.7 3.8 %collective-permute-done.10 = f32[24068]{0:T(1024)S(1)} collective-permute-done((f32[24068]{0:T(1024)S(1)}, f32[24068]{0:T(1024)S(1)}, u32[]{:S(2)}, u32[]{:S(2)}) %collective-permute-start.10) | collective-permute-done | bytes 96304 | tf_op jit(solution)/shard_map/ppermute | solution.py:71
  208.5 4.0 %collective-permute-start.11 = (f32[24068]{0:T(1024)S(1)}, f32[24068]{0:T(1024)S(1)}, u32[]{:S(2)}, u32[]{:S(2)}) collective-permute-start(f32[24068]{0:T(1024)S(1)} %add.339), channel_id=1, source_target_pairs={{0,8},{1,9},{2,10},{3,11},{4,12},{5,13},{6,14},{7,15},{8,0},{9,1},... | collective-permute-start | bytes 288824 | tf_op jit(solution)/shard_map/ppermute | solution.py:71
  212.5 4.7 %fusion.16 = bf16[2,64,1536]{2,1,0:T(8,128)(2,1)} fusion(bf16[2,64,1536]{2,1,0:T(8,128)(2,1)S(1)} %fusion.93, bf16[1536,1536]{1,0:T(8,128)(2,1)} %param.15), kind=kOutput, calls=%fused_computation.48 | convolution fusion | flops 604176384 | bytes 5505024 | tf_op jit(solution)/shard_map/dot_general | solution.py:184
  219.6 4.5 %fusion.58 = bf16[2,64,1536]{2,1,0:T(8,128)(2,1)} fusion(bf16[2,64,1536]{2,1,0:T(8,128)(2,1)S(1)} %fusion.19, bf16[2,15,1536]{2,1,0:T(8,128)(2,1)S(1)} %collective-permute-done.1, bf16[2,15,1536]{2,1,0:T(8,128)(2,1)S(1)} %collective-permute-done, f32[1536]{0:T(1024)S(1)} %get-tuple-element.40, f32[1536]{0:T(1024)S(1)} %copy-done.7, f32[1536]{0:T(1024)S(1)} %copy-done.9, ...), kind=kLoop, calls=%fused_computation.143 | loop fusion | flops 35979264 | bytes 1161216 | tf_op jit(solution)/shard_map/convert_element_type | solution.py:175
  (231 shorter events, 38.6 us)
Async XLA Ops:
  7.0 50.7 %all-to-all-start = ((bf16[32,3,64,96]{3,2,1,0:T(8,128)(2,1)}), bf16[32,3,64,96]{3,2,1,0:T(8,128)(2,1)S(1)}, u32[]{:S(2)}, u32[]{:S(2)}) async-start(bf16[32,3,64,96]{3,2,1,0:T(8,128)(2,1)} %bitcast.45), calls=%async_computation | async-start | bytes 3145728 | tf_op jit(solution)/shard_map/all_to_all | solution.py:91
  20.4 63.5 %copy-start.40 = (f32[1536]{0:T(1024)}, f32[1536]{0:T(1024)S(1)}, u32[]{:S(2)}) copy-start(f32[1536]{0:T(1024)S(1)} %get-tuple-element.58) | copy-start | bytes 18436
  20.4 63.5 %copy-start.42 = (f32[1536]{0:T(1024)}, f32[1536]{0:T(1024)S(1)}, u32[]{:S(2)}) copy-start(f32[1536]{0:T(1024)S(1)} %get-tuple-element.59) | copy-start | bytes 18436
  20.4 63.5 %copy-start.44 = (f32[1536]{0:T(1024)}, f32[1536]{0:T(1024)S(1)}, u32[]{:S(2)}) copy-start(f32[1536]{0:T(1024)S(1)} %get-tuple-element.60) | copy-start | bytes 18436
  20.4 63.5 %copy-start.46 = (f32[1536]{0:T(1024)}, f32[1536]{0:T(1024)S(1)}, u32[]{:S(2)}) copy-start(f32[1536]{0:T(1024)S(1)} %get-tuple-element.61) | copy-start | bytes 18436
  20.4 63.5 %copy-start.48 = (f32[1536]{0:T(1024)}, f32[1536]{0:T(1024)S(1)}, u32[]{:S(2)}) copy-start(f32[1536]{0:T(1024)S(1)} %get-tuple-element.62) | copy-start | bytes 18436
  20.5 63.5 %copy-start.50 = (f32[1536]{0:T(1024)}, f32[1536]{0:T(1024)S(1)}, u32[]{:S(2)}) copy-start(f32[1536]{0:T(1024)S(1)} %get-tuple-element.63) | copy-start | bytes 18436
  20.5 63.5 %copy-start.52 = (f32[1536]{0:T(1024)}, f32[1536]{0:T(1024)S(1)}, u32[]{:S(2)}) copy-start(f32[1536]{0:T(1024)S(1)} %get-tuple-element.64) | copy-start | bytes 18436
  20.5 63.5 %copy-start.54 = (f32[1536]{0:T(1024)}, f32[1536]{0:T(1024)S(1)}, u32[]{:S(2)}) copy-start(f32[1536]{0:T(1024)S(1)} %get-tuple-element.65) | copy-start | bytes 18436
  20.5 63.5 %copy-start.56 = (f32[1536]{0:T(1024)}, f32[1536]{0:T(1024)S(1)}, u32[]{:S(2)}) copy-start(f32[1536]{0:T(1024)S(1)} %get-tuple-element.66) | copy-start | bytes 18436
  57.8 25.9 %collective-permute-start.3 = (bf16[2,15,1536]{2,1,0:T(8,128)(2,1)S(1)}, bf16[2,15,1536]{2,1,0:T(8,128)(2,1)S(1)}, u32[]{:S(2)}, u32[]{:S(2)}) collective-permute-start(bf16[2,15,1536]{2,1,0:T(8,128)(2,1)S(1)} %get-tuple-element.79), channel_id=1, source_target_pairs={{1,0},{2,1},{3,2},{4,3},{5,4},{6,5},{7,6},{8,7},{9,8},{10,9},{11,1... | collective-permute-start | bytes 276488 | tf_op jit(solution)/shard_map/ppermute | solution.py:22
  59.1 24.6 %collective-permute-start.2 = (bf16[2,15,1536]{2,1,0:T(8,128)(2,1)S(1)}, bf16[2,15,1536]{2,1,0:T(8,128)(2,1)S(1)}, u32[]{:S(2)}, u32[]{:S(2)}) collective-permute-start(bf16[2,15,1536]{2,1,0:T(8,128)(2,1)S(1)} %get-tuple-element.78), channel_id=1, source_target_pairs={{0,1},{1,2},{2,3},{3,4},{4,5},{5,6},{6,7},{7,8},{8,9},{9,10},{10,1... | collective-permute-start | bytes 276488 | tf_op jit(solution)/shard_map/ppermute | solution.py:21
  76.8 23.4 %all-to-all-start.1 = ((bf16[32,64,96]{2,1,0:T(8,128)(2,1)}), bf16[32,64,96]{2,1,0:T(8,128)(2,1)S(1)}, u32[]{:S(2)}, u32[]{:S(2)}) async-start(bf16[32,64,96]{2,1,0:T(8,128)(2,1)} %bitcast.7), calls=%async_computation.1 | async-start | bytes 1048576 | tf_op jit(solution)/shard_map/all_to_all | solution.py:98
  104.9 10.4 %collective-permute-start.1 = (bf16[2,15,1536]{2,1,0:T(8,128)(2,1)S(1)}, bf16[2,15,1536]{2,1,0:T(8,128)(2,1)S(1)}, u32[]{:S(2)}, u32[]{:S(2)}) collective-permute-start(bf16[2,15,1536]{2,1,0:T(8,128)(2,1)S(1)} %get-tuple-element.81), channel_id=1, source_target_pairs={{1,0},{2,1},{3,2},{4,3},{5,4},{6,5},{7,6},{8,7},{9,8},{10,9},{11,1... | collective-permute-start | bytes 276488 | tf_op jit(solution)/shard_map/ppermute | solution.py:22
  106.2 6.9 %collective-permute-start = (bf16[2,15,1536]{2,1,0:T(8,128)(2,1)S(1)}, bf16[2,15,1536]{2,1,0:T(8,128)(2,1)S(1)}, u32[]{:S(2)}, u32[]{:S(2)}) collective-permute-start(bf16[2,15,1536]{2,1,0:T(8,128)(2,1)S(1)} %get-tuple-element.80), channel_id=1, source_target_pairs={{0,1},{1,2},{2,3},{3,4},{4,5},{5,6},{6,7},{7,8},{8,9},{9,10},{10,1... | collective-permute-start | bytes 276488 | tf_op jit(solution)/shard_map/ppermute | solution.py:21
  110.9 9.3 %collective-permute-start.4 = (bf16[2,128,1536]{2,1,0:T(8,128)(2,1)S(1)}, bf16[2,128,1536]{2,1,0:T(8,128)(2,1)S(1)}, u32[]{:S(2)}, u32[]{:S(2)}) collective-permute-start(bf16[2,128,1536]{2,1,0:T(8,128)(2,1)S(1)} %pad_maximum_fusion.1), channel_id=1, source_target_pairs={{0,32},{32,0},{64,96},{96,64},{128,160},{160,128},{192,224},{224,1... | collective-permute-start | bytes 2359304 | tf_op jit(solution)/shard_map/ppermute | solution.py:50
  173.8 1.3 collective-permute-start.5
  175.2 4.9 %collective-permute-start.6 = (f32[24068]{0:T(1024)S(1)}, f32[24068]{0:T(1024)S(1)}, u32[]{:S(2)}, u32[]{:S(2)}) collective-permute-start(f32[24068]{0:T(1024)S(1)} %fusion.164), channel_id=1, source_target_pairs={{0,64},{32,96},{64,0},{96,32},{128,192},{160,224},{192,128},{224,1... | collective-permute-start | bytes 288824 | tf_op jit(solution)/shard_map/ppermute | solution.py:71
  180.3 6.2 %collective-permute-start.7 = (f32[24068]{0:T(1024)S(1)}, f32[24068]{0:T(1024)S(1)}, u32[]{:S(2)}, u32[]{:S(2)}) collective-permute-start(f32[24068]{0:T(1024)S(1)} %add.335), channel_id=1, source_target_pairs={{0,128},{32,160},{64,192},{96,224},{128,0},{160,32},{192,64},{224,... | collective-permute-start | bytes 288824 | tf_op jit(solution)/shard_map/ppermute | solution.py:71
  186.6 5.1 %collective-permute-start.8 = (f32[24068]{0:T(1024)S(1)}, f32[24068]{0:T(1024)S(1)}, u32[]{:S(2)}, u32[]{:S(2)}) collective-permute-start(f32[24068]{0:T(1024)S(1)} %add.336), channel_id=1, source_target_pairs={{0,1},{1,0},{2,3},{3,2},{4,5},{5,4},{6,7},{7,6},{8,9},{9,8},{10,11... | collective-permute-start | bytes 288824 | tf_op jit(solution)/shard_map/ppermute | solution.py:71
  191.7 8.1 %collective-permute-start.9 = (f32[24068]{0:T(1024)S(1)}, f32[24068]{0:T(1024)S(1)}, u32[]{:S(2)}, u32[]{:S(2)}) collective-permute-start(f32[24068]{0:T(1024)S(1)} %add.337), channel_id=1, source_target_pairs={{0,2},{1,3},{2,0},{3,1},{4,6},{5,7},{6,4},{7,5},{8,10},{9,11},{10,... | collective-permute-start | bytes 288824 | tf_op jit(solution)/shard_map/ppermute | solution.py:71
  199.8 8.7 %collective-permute-start.10 = (f32[24068]{0:T(1024)S(1)}, f32[24068]{0:T(1024)S(1)}, u32[]{:S(2)}, u32[]{:S(2)}) collective-permute-start(f32[24068]{0:T(1024)S(1)} %add.338), channel_id=1, source_target_pairs={{0,4},{1,5},{2,6},{3,7},{4,0},{5,1},{6,2},{7,3},{8,12},{9,13},{10,... | collective-permute-start | bytes 288824 | tf_op jit(solution)/shard_map/ppermute | solution.py:71
  208.5 8.7 %collective-permute-start.11 = (f32[24068]{0:T(1024)S(1)}, f32[24068]{0:T(1024)S(1)}, u32[]{:S(2)}, u32[]{:S(2)}) collective-permute-start(f32[24068]{0:T(1024)S(1)} %add.339), channel_id=1, source_target_pairs={{0,8},{1,9},{2,10},{3,11},{4,12},{5,13},{6,14},{7,15},{8,0},{9,1},... | collective-permute-start | bytes 288824 | tf_op jit(solution)/shard_map/ppermute | solution.py:71
  217.3 6.9 %collective-permute-start.12 = (f32[24068]{0:T(1024)S(1)}, f32[24068]{0:T(1024)S(1)}, u32[]{:S(2)}, u32[]{:S(2)}) collective-permute-start(f32[24068]{0:T(1024)S(1)} %add.340), channel_id=1, source_target_pairs={{0,16},{1,17},{2,18},{3,19},{4,20},{5,21},{6,22},{7,23},{8,24},{9,... | collective-permute-start | bytes 288824 | tf_op jit(solution)/shard_map/ppermute | solution.py:71
  (58 other events, 2596.1 us)
where the time goes:
time: 226 us; the launch traced here: 225 us
  waiting for transfers between devices  69.5 us (31%)
  starting transfers between devices  49.9 us (22%)
  local copies, waits for them, and re-layouts  49.4 us (22%)
  other arithmetic  34.4 us (15%)
  matrix products  20.1 us (9%)
    all_to_all x1, waiting for transfers between devices, head_attention(): gathered = lax.all_to_all(stacked, 'seq', 0, 0, tiled=True)  33.9 us
    gather x2, local copies, waits for them, and re-layouts, pick_entries(): chosen = jnp.take(blocks, picks // lane, axis=0)  27.6 us
    ppermute x8, waiting for transfers between devices, butterfly_sum(): value = value + lax.ppermute(value, axis, pairs)  20.7 us
    ppermute x8, starting transfers between devices, butterfly_sum(): value = value + lax.ppermute(value, axis, pairs)  19.7 us
    all_to_all x1, waiting for transfers between devices, head_attention(): back = lax.all_to_all(out_rows, 'seq', 0, 0, tiled=True)  12.8 us
    reduce_sum x2, other arithmetic, pick_entries(): return jnp.sum(jnp.where(hit, chosen, jnp.float32(0.0)), axis=1)  11.5 us
    all_to_all x1, starting transfers between devices, head_attention(): gathered = lax.all_to_all(stacked, 'seq', 0, 0, tiled=True)  11.3 us
    another operation x2, local copies, waits for them, and re-layouts, pick_entries(): blocks = flat.reshape(flat.shape[0] // lane, lane)  10.6 us
  transfers between devices with their start and end apart: 15, of which 9 were waited for; matrix products, arithmetic and copies ran while one was open for 17% of the time, Pallas kernels for 0%

commit v1 on v0

--- a/solution.py
+++ b/solution.py
@@ -40,6 +40,13 @@
     hit = lane_ids[None, :] == (picks % lane)[:, None]
     return jnp.sum(jnp.where(hit, chosen, jnp.float32(0.0)), axis=1)
 
+def block_entries(blocks, block_of, lane_of):
+    chosen = jnp.take(blocks, block_of, axis=0)
+    lane_ids = jnp.arange(blocks.shape[1], dtype=jnp.int32)
+    hit = lane_ids[None, :] == lane_of[:, None]
+    return jnp.sum(jnp.where(hit, chosen, jnp.float32(0.0)), axis=1)
+
+
 def group_picks(context_flat, grad_flat, picks, axis, levels):
     count = lax.axis_size(axis)
     levels = min(levels, count.bit_length() - 1)
@@ -49,15 +56,17 @@
         step = 1 << level
         other = lax.ppermute(pair, axis, [(i, i ^ step) for i in range(count)])
         pair = jnp.concatenate([pair, other], axis=1)
-    table = lax.dot_general(
-        pair[0], pair[1], (((0,), (0,)), ((), ())), preferred_element_type=jnp.float32
-    )
+    depth, table_rows = pair.shape[1], pair.shape[2]
+    lane = math.gcd(table_rows, 128)
+    grad_blocks = pair[1].reshape(depth, table_rows // lane, lane)
+    table = jnp.einsum("ncl,nr->crl", grad_blocks, pair[0], preferred_element_type=jnp.float32)
     total = picks.shape[0]
     rows = -(-total // group)
     padded_picks = jnp.pad(picks, (0, rows * group - total))
     first = (lax.axis_index(axis) % group) * rows
     mine = lax.dynamic_slice(padded_picks, (first,), (rows,))
-    values = pick_entries(table, mine)
+    block_of = (mine % table_rows) // lane * table_rows + mine // table_rows
+    values = block_entries(table.reshape(-1, lane), block_of, mine % lane)
     spread = lax.dynamic_update_slice(jnp.zeros((rows * group,), jnp.float32), values, (first,))
     return spread[:total]
 

time: 226 us -> 216 us (0.956)
  local copies, waits for them, and re-layouts: 49.4 us -> 39.8 us
    gather x0 -> x1, local copies, waits for them, and re-layouts: none -> 26.4 us  [block_entries(): chosen = jnp.take(blocks, block_of, axis=0)]
    gather x2 -> x1, local copies, waits for them, and re-layouts: 27.6 us -> 1.32 us  [pick_entries(): chosen = jnp.take(blocks, picks // lane, axis=0)]
    another operation x2 -> x1, local copies, waits for them, and re-layouts: 10.6 us -> 0.02 us  [pick_entries(): blocks = flat.reshape(flat.shape[0] // lane, lane)]
    reduce_sum x0 -> x1, other arithmetic: none -> 10.5 us  [block_entries(): return jnp.sum(jnp.where(hit, chosen, jnp.float32(0.0)), axis=1)]
    reduce_sum x2 -> x1, other arithmetic: 11.5 us -> 0.98 us  [pick_entries(): return jnp.sum(jnp.where(hit, chosen, jnp.float32(0.0)), axis=1)]
  transfers between devices with their start and end apart: 15 -> 15, of which waited for: 9 -> 9; matrix products, arithmetic and copies ran while one was open for 17% -> 18% of each run, Pallas kernels for 0% -> 0%
where the time goes in v1:
time: 216 us; the launch traced here: 215 us
  waiting for transfers between devices  69.6 us (32%)
  starting transfers between devices  49.6 us (23%)
  local copies, waits for them, and re-layouts  39.8 us (18%)
  other arithmetic  35 us (16%)
  matrix products  19.5 us (9%)
    all_to_all x1, waiting for transfers between devices, head_attention(): gathered = lax.all_to_all(stacked, 'seq', 0, 0, tiled=True)  34.2 us
    gather x1, local copies, waits for them, and re-layouts, block_entries(): chosen = jnp.take(blocks, block_of, axis=0)  26.4 us
    ppermute x8, waiting for transfers between devices, butterfly_sum(): value = value + lax.ppermute(value, axis, pairs)  20.9 us
    ppermute x8, starting transfers between devices, butterfly_sum(): value = value + lax.ppermute(value, axis, pairs)  19.5 us
    all_to_all x1, waiting for transfers between devices, head_attention(): back = lax.all_to_all(out_rows, 'seq', 0, 0, tiled=True)  12.8 us
    all_to_all x1, starting transfers between devices, head_attention(): gathered = lax.all_to_all(stacked, 'seq', 0, 0, tiled=True)  11.3 us
    reduce_sum x1, other arithmetic, block_entries(): return jnp.sum(jnp.where(hit, chosen, jnp.float32(0.0)), axis=1)  10.5 us
    ppermute x2, starting transfers between devices, padded(): before = lax.ppermute(last, axis, up)  9.24 us
  transfers between devices with their start and end apart: 15, of which 9 were waited for; matrix products, arithmetic and copies ran while one was open for 18% of the time, Pallas kernels for 0%

profile of v1, /device:TPU:16, one launch (start us, length us, event | category | flops | bytes accessed | tf_op | source)
XLA Modules:
  0.0 215.2 jit_solution(7858826402996385731)
XLA Ops:
  7.0 11.3 %all-to-all-start = ((bf16[32,3,64,96]{3,2,1,0:T(8,128)(2,1)}), bf16[32,3,64,96]{3,2,1,0:T(8,128)(2,1)S(1)}, u32[]{:S(2)}, u32[]{:S(2)}) async-start(bf16[32,3,64,96]{3,2,1,0:T(8,128)(2,1)} %bitcast.2), calls=%async_computation | async-start | bytes 3145728 | tf_op jit(solution)/shard_map/all_to_all | solution.py:100
  23.5 34.2 %all-to-all-done = bf16[32,3,64,96]{3,2,1,0:T(8,128)(2,1)S(1)} async-done(((bf16[32,3,64,96]{3,2,1,0:T(8,128)(2,1)}), bf16[32,3,64,96]{3,2,1,0:T(8,128)(2,1)S(1)}, u32[]{:S(2)}, u32[]{:S(2)}) %all-to-all-start) | async-done | bytes 1179680 | tf_op jit(solution)/shard_map/all_to_all | solution.py:100
  59.1 4.6 %collective-permute-start.2 = (bf16[2,15,1536]{2,1,0:T(8,128)(2,1)S(1)}, bf16[2,15,1536]{2,1,0:T(8,128)(2,1)S(1)}, u32[]{:S(2)}, u32[]{:S(2)}) collective-permute-start(bf16[2,15,1536]{2,1,0:T(8,128)(2,1)S(1)} %get-tuple-element.77), channel_id=1, source_target_pairs={{0,1},{1,2},{2,3},{3,4},{4,5},{5,6},{6,7},{7,8},{8,9},{9,10},{10,1... | collective-permute-start | bytes 276488 | tf_op jit(solution)/shard_map/ppermute | solution.py:21
  63.7 3.4 %fusion = (f32[2048]{0:T(1024)S(1)}, f32[2048,2048]{0,1:T(8,128)S(1)}) fusion(pred[2048]{0:T(1024)(128)(4,1)S(1)} %iota_compare_fusion.2, bf16[2048,96]{1,0:T(8,128)(2,1)S(1)} %bitcast.51, bf16[2048,96]{1,0:T(8,128)(2,1)S(1)} %bitcast.53), kind=kOutput, calls=%fused_computation.4 | convolution fusion | flops 817887232 | bytes 17573888 | tf_op jit(solution)/shard_map/dot_general | solution.py:86
  67.0 4.9 %fusion.1 = f32[2048]{0:T(1024)S(1)} fusion(f32[2048,2048]{0,1:T(8,128)S(1)} %get-tuple-element.82, f32[2048]{0:T(1024)S(1)} %get-tuple-element.81, pred[2048]{0:T(1024)(128)(4,1)S(1)} %iota_compare_fusion.2), kind=kLoop, calls=%fused_computation.5 | loop fusion | flops 16775168 | bytes 16795648 | tf_op jit(solution)/shard_map/reduce_sum | solution.py:31
  72.0 3.9 %fusion.25 = bf16[2048,96]{0,1:T(8,128)(2,1)S(1)} fusion(bf16[2048,96]{1,0:T(8,128)(2,1)S(1)} %bitcast.54, f32[2048,2048]{0,1:T(8,128)S(1)} %get-tuple-element.82, f32[2048]{0:T(1024)S(1)} %get-tuple-element.81, pred[2048]{0:T(1024)(128)(4,1)S(1)} %iota_compare_fusion.2, f32[2048]{0:T(1024)S(1)} %fusion.1), kind=kOutput, calls=%fused_computation.79 | convolution fusion | flops 822476800 | bytes 17582080 | tf_op jit(solution)/shard_map/dot_general | solution.py:88
  76.9 6.9 %all-to-all-start.1 = ((bf16[32,64,96]{2,1,0:T(8,128)(2,1)}), bf16[32,64,96]{2,1,0:T(8,128)(2,1)S(1)}, u32[]{:S(2)}, u32[]{:S(2)}) async-start(bf16[32,64,96]{2,1,0:T(8,128)(2,1)} %bitcast.7), calls=%async_computation.1 | async-start | bytes 1048576 | tf_op jit(solution)/shard_map/all_to_all | solution.py:107
  84.1 3.1 %fusion.93 = bf16[2,64,1536]{2,1,0:T(8,128)(2,1)S(1)} fusion(f32[2,94,1536]{2,1,0:T(8,128)S(1)} %maximum_convert_fusion, f32[1536]{0:T(1024)S(1)} %get-tuple-element.40, f32[1536]{0:T(1024)S(1)} %get-tuple-element.41, f32[1536]{0:T(1024)S(1)} %get-tuple-element.42, f32[1536]{0:T(1024)S(1)} %get-tuple-element.43, f32[1536]{0:T(1024)S(1)} %get-tuple-element.44, ...), kind=kLoop, calls=%fused_computation.180 | loop fusion | flops 12386304 | bytes 24963584 | tf_op jit(solution)/shard_map/convert_element_type | solution.py:191
  87.5 12.8 %all-to-all-done.1 = bf16[32,64,96]{2,1,0:T(8,128)(2,1)S(1)} async-done(((bf16[32,64,96]{2,1,0:T(8,128)(2,1)}), bf16[32,64,96]{2,1,0:T(8,128)(2,1)S(1)}, u32[]{:S(2)}, u32[]{:S(2)}) %all-to-all-start.1) | async-done | bytes 393248 | tf_op jit(solution)/shard_map/all_to_all | solution.py:107
  101.8 3.1 %fusion.19 = bf16[2,64,1536]{2,1,0:T(8,128)(2,1)S(1)} fusion(bf16[2,64,1536]{2,1,0:T(8,128)(2,1)S(1)} %dot_general.19, bf16[1536,1536]{1,0:T(8,128)(2,1)} %param.15, bf16[2,64,1536]{2,1,0:T(8,128)(2,1)S(1)} %copy-done.1, f32[2,64]{1,0:T(2,128)} %copy-done.23), kind=kOutput, calls=%fused_computation.49 | convolution fusion | flops 604766208 | bytes 5898752 | tf_op jit(solution)/shard_map/dot_general | solution.py:167
  106.2 4.7 %collective-permute-start = (bf16[2,15,1536]{2,1,0:T(8,128)(2,1)S(1)}, bf16[2,15,1536]{2,1,0:T(8,128)(2,1)S(1)}, u32[]{:S(2)}, u32[]{:S(2)}) collective-permute-start(bf16[2,15,1536]{2,1,0:T(8,128)(2,1)S(1)} %get-tuple-element.79), channel_id=1, source_target_pairs={{0,1},{1,2},{2,3},{3,4},{4,5},{5,6},{6,7},{7,8},{8,9},{9,10},{10,1... | collective-permute-start | bytes 276488 | tf_op jit(solution)/shard_map/ppermute | solution.py:21
  121.8 4.5 %fusion.90 = f32[1536,12,128]{2,0,1:T(8,128)} fusion(bf16[256,12,128]{0,2,1:T(8,128)(2,1)S(1)} %bitcast.50, bf16[2,256,1536]{1,2,0:T(8,128)(2,1)S(1)} %pad_maximum_fusion), kind=kOutput, calls=%fused_computation.176 | convolution fusion | flops 1207959552 | bytes 11010048 | tf_op jit(solution)/shard_map/ncl,nr->crl/dot_general | solution.py:62
  126.3 26.4 %gather_fusion = f32[11796,128]{1,0:T(8,128)} fusion(f32[18432,128]{1,0:T(8,128)} %bitcast.45, s32[12288]{0:T(1024)S(1)} %pad_clamp_fusion), kind=kCustom, calls=%fused_computation | custom fusion | bytes 12126288 | tf_op jit(solution)/shard_map/jit(_take)/gather | solution.py:44
  152.7 10.5 %select_reduce_fusion = f32[11796]{0:T(1024)S(1)} fusion(f32[11796,128]{1,0:T(8,128)} %gather_fusion, s32[11796]{0:T(1024)S(1)} %add_select_fusion.3, pred[11796]{0:T(1024)(128)(4,1)S(1)} %copy-done.22), kind=kLoop, calls=%fused_computation.40 | loop fusion | flops 6027756 | bytes 6145716 | tf_op jit(solution)/shard_map/reduce_sum | solution.py:47
  166.7 3.6 %collective-permute-done.6 = f32[24068]{0:T(1024)S(1)} collective-permute-done((f32[24068]{0:T(1024)S(1)}, f32[24068]{0:T(1024)S(1)}, u32[]{:S(2)}, u32[]{:S(2)}) %collective-permute-start.6) | collective-permute-done | bytes 96304 | tf_op jit(solution)/shard_map/ppermute | solution.py:80
  170.8 5.8 %collective-permute-done.7 = f32[24068]{0:T(1024)S(1)} collective-permute-done((f32[24068]{0:T(1024)S(1)}, f32[24068]{0:T(1024)S(1)}, u32[]{:S(2)}, u32[]{:S(2)}) %collective-permute-start.7) | collective-permute-done | bytes 96304 | tf_op jit(solution)/shard_map/ppermute | solution.py:80
  179.1 2.6 %collective-permute-done.8 = f32[24068]{0:T(1024)S(1)} collective-permute-done((f32[24068]{0:T(1024)S(1)}, f32[24068]{0:T(1024)S(1)}, u32[]{:S(2)}, u32[]{:S(2)}) %collective-permute-start.8) | collective-permute-done | bytes 96304 | tf_op jit(solution)/shard_map/ppermute | solution.py:80
  181.7 4.4 %collective-permute-start.9 = (f32[24068]{0:T(1024)S(1)}, f32[24068]{0:T(1024)S(1)}, u32[]{:S(2)}, u32[]{:S(2)}) collective-permute-start(f32[24068]{0:T(1024)S(1)} %add.347), channel_id=1, source_target_pairs={{0,2},{1,3},{2,0},{3,1},{4,6},{5,7},{6,4},{7,5},{8,10},{9,11},{10,... | collective-permute-start | bytes 288824 | tf_op jit(solution)/shard_map/ppermute | solution.py:80
  186.1 3.6 %collective-permute-done.9 = f32[24068]{0:T(1024)S(1)} collective-permute-done((f32[24068]{0:T(1024)S(1)}, f32[24068]{0:T(1024)S(1)}, u32[]{:S(2)}, u32[]{:S(2)}) %collective-permute-start.9) | collective-permute-done | bytes 96304 | tf_op jit(solution)/shard_map/ppermute | solution.py:80
  189.7 5.0 %collective-permute-start.10 = (f32[24068]{0:T(1024)S(1)}, f32[24068]{0:T(1024)S(1)}, u32[]{:S(2)}, u32[]{:S(2)}) collective-permute-start(f32[24068]{0:T(1024)S(1)} %add.348), channel_id=1, source_target_pairs={{0,4},{1,5},{2,6},{3,7},{4,0},{5,1},{6,2},{7,3},{8,12},{9,13},{10,... | collective-permute-start | bytes 288824 | tf_op jit(solution)/shard_map/ppermute | solution.py:80
  194.7 4.0 %collective-permute-done.10 = f32[24068]{0:T(1024)S(1)} collective-permute-done((f32[24068]{0:T(1024)S(1)}, f32[24068]{0:T(1024)S(1)}, u32[]{:S(2)}, u32[]{:S(2)}) %collective-permute-start.10) | collective-permute-done | bytes 96304 | tf_op jit(solution)/shard_map/ppermute | solution.py:80
  198.7 3.9 %collective-permute-start.11 = (f32[24068]{0:T(1024)S(1)}, f32[24068]{0:T(1024)S(1)}, u32[]{:S(2)}, u32[]{:S(2)}) collective-permute-start(f32[24068]{0:T(1024)S(1)} %add.349), channel_id=1, source_target_pairs={{0,8},{1,9},{2,10},{3,11},{4,12},{5,13},{6,14},{7,15},{8,0},{9,1},... | collective-permute-start | bytes 288824 | tf_op jit(solution)/shard_map/ppermute | solution.py:80
  202.5 4.7 %fusion.16 = bf16[2,64,1536]{2,1,0:T(8,128)(2,1)} fusion(bf16[2,64,1536]{2,1,0:T(8,128)(2,1)S(1)} %fusion.93, bf16[1536,1536]{1,0:T(8,128)(2,1)} %param.15), kind=kOutput, calls=%fused_computation.48 | convolution fusion | flops 604176384 | bytes 5505024 | tf_op jit(solution)/shard_map/dot_general | solution.py:193
  209.4 4.5 %fusion.58 = bf16[2,64,1536]{2,1,0:T(8,128)(2,1)} fusion(bf16[2,64,1536]{2,1,0:T(8,128)(2,1)S(1)} %fusion.19, bf16[2,15,1536]{2,1,0:T(8,128)(2,1)S(1)} %collective-permute-done.1, bf16[2,15,1536]{2,1,0:T(8,128)(2,1)S(1)} %collective-permute-done, f32[1536]{0:T(1024)S(1)} %get-tuple-element.40, f32[1536]{0:T(1024)S(1)} %get-tuple-element.41, ...), kind=kLoop, calls=%fused_computation.143 | loop fusion | flops 35979264 | bytes 1161216 | tf_op jit(solution)/shard_map/convert_element_type | solution.py:184
  (151 shorter events, 37.4 us)
Async XLA Ops:
  5.4 52.4 %copy-start = (bf16[2,64,1536]{2,1,0:T(8,128)(2,1)S(1)}, bf16[2,64,1536]{2,1,0:T(8,128)(2,1)}, u32[]{:S(2)}) copy-start(bf16[2,64,1536]{2,1,0:T(8,128)(2,1)} %param.17) | copy-start | bytes 1179652
  7.0 50.7 %all-to-all-start = ((bf16[32,3,64,96]{3,2,1,0:T(8,128)(2,1)}), bf16[32,3,64,96]{3,2,1,0:T(8,128)(2,1)S(1)}, u32[]{:S(2)}, u32[]{:S(2)}) async-start(bf16[32,3,64,96]{3,2,1,0:T(8,128)(2,1)} %bitcast.2), calls=%async_computation | async-start | bytes 3145728 | tf_op jit(solution)/shard_map/all_to_all | solution.py:100
  22.0 62.0 %copy-start.23 = (f32[2,64]{1,0:T(2,128)}, f32[2,64]{1,0:T(2,128)S(1)}, u32[]{:S(2)}) copy-start(f32[2,64]{1,0:T(2,128)S(1)} %compare_convert_fusion) | copy-start | bytes 1540
  57.8 26.0 %collective-permute-start.3 = (bf16[2,15,1536]{2,1,0:T(8,128)(2,1)S(1)}, bf16[2,15,1536]{2,1,0:T(8,128)(2,1)S(1)}, u32[]{:S(2)}, u32[]{:S(2)}) collective-permute-start(bf16[2,15,1536]{2,1,0:T(8,128)(2,1)S(1)} %get-tuple-element.78), channel_id=1, source_target_pairs={{1,0},{2,1},{3,2},{4,3},{5,4},{6,5},{7,6},{8,7},{9,8},{10,9},{11,1... | collective-permute-start | bytes 276488 | tf_op jit(solution)/shard_map/ppermute | solution.py:22
  59.1 24.7 %collective-permute-start.2 = (bf16[2,15,1536]{2,1,0:T(8,128)(2,1)S(1)}, bf16[2,15,1536]{2,1,0:T(8,128)(2,1)S(1)}, u32[]{:S(2)}, u32[]{:S(2)}) collective-permute-start(bf16[2,15,1536]{2,1,0:T(8,128)(2,1)S(1)} %get-tuple-element.77), channel_id=1, source_target_pairs={{0,1},{1,2},{2,3},{3,4},{4,5},{5,6},{6,7},{7,8},{8,9},{9,10},{10,1... | collective-permute-start | bytes 276488 | tf_op jit(solution)/shard_map/ppermute | solution.py:21
  76.9 23.4 %all-to-all-start.1 = ((bf16[32,64,96]{2,1,0:T(8,128)(2,1)}), bf16[32,64,96]{2,1,0:T(8,128)(2,1)S(1)}, u32[]{:S(2)}, u32[]{:S(2)}) async-start(bf16[32,64,96]{2,1,0:T(8,128)(2,1)} %bitcast.7), calls=%async_computation.1 | async-start | bytes 1048576 | tf_op jit(solution)/shard_map/all_to_all | solution.py:107
  104.9 10.4 %collective-permute-start.1 = (bf16[2,15,1536]{2,1,0:T(8,128)(2,1)S(1)}, bf16[2,15,1536]{2,1,0:T(8,128)(2,1)S(1)}, u32[]{:S(2)}, u32[]{:S(2)}) collective-permute-start(bf16[2,15,1536]{2,1,0:T(8,128)(2,1)S(1)} %get-tuple-element.80), channel_id=1, source_target_pairs={{1,0},{2,1},{3,2},{4,3},{5,4},{6,5},{7,6},{8,7},{9,8},{10,9},{11,1... | collective-permute-start | bytes 276488 | tf_op jit(solution)/shard_map/ppermute | solution.py:22
  106.2 6.9 %collective-permute-start = (bf16[2,15,1536]{2,1,0:T(8,128)(2,1)S(1)}, bf16[2,15,1536]{2,1,0:T(8,128)(2,1)S(1)}, u32[]{:S(2)}, u32[]{:S(2)}) collective-permute-start(bf16[2,15,1536]{2,1,0:T(8,128)(2,1)S(1)} %get-tuple-element.79), channel_id=1, source_target_pairs={{0,1},{1,2},{2,3},{3,4},{4,5},{5,6},{6,7},{7,8},{8,9},{9,10},{10,1... | collective-permute-start | bytes 276488 | tf_op jit(solution)/shard_map/ppermute | solution.py:21
  111.2 9.2 %collective-permute-start.4 = (bf16[2,128,1536]{1,2,0:T(8,128)(2,1)S(1)}, bf16[2,128,1536]{1,2,0:T(8,128)(2,1)}, u32[]{:S(2)}, u32[]{:S(2)}) collective-permute-start(bf16[2,128,1536]{1,2,0:T(8,128)(2,1)S(1)} %pad_maximum_fusion.1), channel_id=1, source_target_pairs={{0,32},{32,0},{64,96},{96,64},{128,160},{160,128},{192,224},{224,1... | collective-permute-start | bytes 2359304 | tf_op jit(solution)/shard_map/ppermute | solution.py:57
  164.0 1.3 collective-permute-start.5
  165.4 4.9 %collective-permute-start.6 = (f32[24068]{0:T(1024)S(1)}, f32[24068]{0:T(1024)S(1)}, u32[]{:S(2)}, u32[]{:S(2)}) collective-permute-start(f32[24068]{0:T(1024)S(1)} %fusion.169), channel_id=1, source_target_pairs={{0,64},{32,96},{64,0},{96,32},{128,192},{160,224},{192,128},{224,1... | collective-permute-start | bytes 288824 | tf_op jit(solution)/shard_map/ppermute | solution.py:80
  170.3 39.0 %copy-start.5 = (f32[1536]{0:T(1024)S(1)}, f32[1536]{0:T(1024)}, u32[]{:S(2)}) copy-start(f32[1536]{0:T(1024)} %get-tuple-element.61) | copy-start | bytes 18436
  170.3 39.0 %copy-start.7 = (f32[1536]{0:T(1024)S(1)}, f32[1536]{0:T(1024)}, u32[]{:S(2)}) copy-start(f32[1536]{0:T(1024)} %get-tuple-element.62) | copy-start | bytes 18436
  170.3 39.0 %copy-start.9 = (f32[1536]{0:T(1024)S(1)}, f32[1536]{0:T(1024)}, u32[]{:S(2)}) copy-start(f32[1536]{0:T(1024)} %get-tuple-element.63) | copy-start | bytes 18436
  170.3 39.0 %copy-start.11 = (f32[1536]{0:T(1024)S(1)}, f32[1536]{0:T(1024)}, u32[]{:S(2)}) copy-start(f32[1536]{0:T(1024)} %get-tuple-element.64) | copy-start | bytes 18436
  170.3 39.0 %copy-start.13 = (f32[1536]{0:T(1024)S(1)}, f32[1536]{0:T(1024)}, u32[]{:S(2)}) copy-start(f32[1536]{0:T(1024)} %get-tuple-element.65) | copy-start | bytes 18436
  170.3 39.0 %copy-start.15 = (f32[1536]{0:T(1024)S(1)}, f32[1536]{0:T(1024)}, u32[]{:S(2)}) copy-start(f32[1536]{0:T(1024)} %get-tuple-element.66) | copy-start | bytes 18436
  170.3 39.0 %copy-start.17 = (f32[1536]{0:T(1024)S(1)}, f32[1536]{0:T(1024)}, u32[]{:S(2)}) copy-start(f32[1536]{0:T(1024)} %get-tuple-element.67) | copy-start | bytes 18436
  170.4 6.2 %collective-permute-start.7 = (f32[24068]{0:T(1024)S(1)}, f32[24068]{0:T(1024)S(1)}, u32[]{:S(2)}, u32[]{:S(2)}) collective-permute-start(f32[24068]{0:T(1024)S(1)} %add.345), channel_id=1, source_target_pairs={{0,128},{32,160},{64,192},{96,224},{128,0},{160,32},{192,64},{224,... | collective-permute-start | bytes 288824 | tf_op jit(solution)/shard_map/ppermute | solution.py:80
  176.6 5.1 %collective-permute-start.8 = (f32[24068]{0:T(1024)S(1)}, f32[24068]{0:T(1024)S(1)}, u32[]{:S(2)}, u32[]{:S(2)}) collective-permute-start(f32[24068]{0:T(1024)S(1)} %add.346), channel_id=1, source_target_pairs={{0,1},{1,0},{2,3},{3,2},{4,5},{5,4},{6,7},{7,6},{8,9},{9,8},{10,11... | collective-permute-start | bytes 288824 | tf_op jit(solution)/shard_map/ppermute | solution.py:80
  181.7 8.0 %collective-permute-start.9 = (f32[24068]{0:T(1024)S(1)}, f32[24068]{0:T(1024)S(1)}, u32[]{:S(2)}, u32[]{:S(2)}) collective-permute-start(f32[24068]{0:T(1024)S(1)} %add.347), channel_id=1, source_target_pairs={{0,2},{1,3},{2,0},{3,1},{4,6},{5,7},{6,4},{7,5},{8,10},{9,11},{10,... | collective-permute-start | bytes 288824 | tf_op jit(solution)/shard_map/ppermute | solution.py:80
  189.7 8.9 %collective-permute-start.10 = (f32[24068]{0:T(1024)S(1)}, f32[24068]{0:T(1024)S(1)}, u32[]{:S(2)}, u32[]{:S(2)}) collective-permute-start(f32[24068]{0:T(1024)S(1)} %add.348), channel_id=1, source_target_pairs={{0,4},{1,5},{2,6},{3,7},{4,0},{5,1},{6,2},{7,3},{8,12},{9,13},{10,... | collective-permute-start | bytes 288824 | tf_op jit(solution)/shard_map/ppermute | solution.py:80
  198.7 8.6 %collective-permute-start.11 = (f32[24068]{0:T(1024)S(1)}, f32[24068]{0:T(1024)S(1)}, u32[]{:S(2)}, u32[]{:S(2)}) collective-permute-start(f32[24068]{0:T(1024)S(1)} %add.349), channel_id=1, source_target_pairs={{0,8},{1,9},{2,10},{3,11},{4,12},{5,13},{6,14},{7,15},{8,0},{9,1},... | collective-permute-start | bytes 288824 | tf_op jit(solution)/shard_map/ppermute | solution.py:80
  207.3 6.6 %collective-permute-start.12 = (f32[24068]{0:T(1024)S(1)}, f32[24068]{0:T(1024)S(1)}, u32[]{:S(2)}, u32[]{:S(2)}) collective-permute-start(f32[24068]{0:T(1024)S(1)} %add.350), channel_id=1, source_target_pairs={{0,16},{1,17},{2,18},{3,19},{4,20},{5,21},{6,22},{7,23},{8,24},{9,... | collective-permute-start | bytes 288824 | tf_op jit(solution)/shard_map/ppermute | solution.py:80
  (17 other events, 290.0 us)

commit v2 on v1

--- a/solution.py
+++ b/solution.py
@@ -89,6 +89,14 @@
     return (out_rows / denom[:, None]).astype(jnp.bfloat16)
 
 
+def lane_dense_all_to_all(value):
+    chunk = math.prod(value.shape[1:])
+    if chunk % 128:
+        return lax.all_to_all(value, "seq", 0, 0, tiled=True)
+    dense = value.reshape(value.shape[0], chunk // 128, 128)
+    return lax.all_to_all(dense, "seq", 0, 0, tiled=True).reshape(value.shape)
+
+
 def head_attention(queries, key_rows, value_rows, utt_lengths, seq_index, score_scale, later):
     local_utts, frames_dev, width = queries.shape
     head_size = width // HEADS
@@ -97,14 +105,14 @@
     stacked = jnp.stack([queries, key_rows, value_rows])
     stacked = stacked.reshape(3, local_utts, frames_dev, HEADS, head_size)
     stacked = stacked.transpose(3, 1, 0, 2, 4).reshape(seq_count, 3, frames_dev, head_size)
-    gathered = lax.all_to_all(stacked, "seq", 0, 0, tiled=True)
+    gathered = lane_dense_all_to_all(stacked)
     gathered, later = lax.optimization_barrier((gathered, later))
     gathered = gathered.transpose(1, 0, 2, 3).reshape(3, full_frames, head_size)
     length = utt_lengths[seq_index % local_utts]
     key_ok = jnp.arange(full_frames, dtype=jnp.int32) < length
     out_rows = attend(gathered[0], gathered[1], gathered[2], key_ok, score_scale)
     out_rows = out_rows.reshape(seq_count, frames_dev, head_size)
-    back = lax.all_to_all(out_rows, "seq", 0, 0, tiled=True)
+    back = lane_dense_all_to_all(out_rows)
     back = back.reshape(HEADS, local_utts, frames_dev, head_size).transpose(1, 2, 0, 3)
     return back.reshape(local_utts, frames_dev, width), later
 

time: 216 us -> 210 us (0.972)
  waiting for transfers between devices: 69.6 us -> 57.4 us
  local copies, waits for them, and re-layouts: 39.8 us -> 45.9 us
    all_to_all x2, waiting for transfers between devices: 47 us -> 35 us  [lane_dense_all_to_all(): return lax.all_to_all(dense, 'seq', 0, 0, tiled=True).reshape(value.shape)]
    another operation x0 -> x3, local copies, waits for them, and re-layouts: none -> 4.8 us  [the longest x2 4.44 us: lane_dense_all_to_all(): dense = value.reshape(value.shape[0], chunk // 128, 128)]
    reshape x1, local copies, waits for them, and re-layouts: 0.34 us -> 2.75 us  [lane_dense_all_to_all(): return lax.all_to_all(dense, 'seq', 0, 0, tiled=True).reshape(value.shape)]
    another operation x3 -> x6, local copies, waits for them, and re-layouts: 4.31 us -> 4.72 us  [head_attention(): stacked = jnp.stack([queries, key_rows, value_rows])]
where the time goes in v2:
time: 210 us
  waiting for transfers between devices  57.4 us (27%)
  starting transfers between devices  49.6 us (24%)
  local copies, waits for them, and re-layouts  45.9 us (22%)
  other arithmetic  34.9 us (17%)
  matrix products  19.6 us (9%)
  between operations  2.3 us (1%)
    all_to_all x2, waiting for transfers between devices, lane_dense_all_to_all(): return lax.all_to_all(dense, 'seq', 0, 0, tiled=True).reshape(value.shape)  35 us
    gather x1, local copies, waits for them, and re-layouts, block_entries(): chosen = jnp.take(blocks, block_of, axis=0)  26.4 us
    ppermute x8, waiting for transfers between devices, butterfly_sum(): value = value + lax.ppermute(value, axis, pairs)  21 us
    ppermute x8, starting transfers between devices, butterfly_sum(): value = value + lax.ppermute(value, axis, pairs)  19.2 us
    all_to_all x2, starting transfers between devices, lane_dense_all_to_all(): return lax.all_to_all(dense, 'seq', 0, 0, tiled=True).reshape(value.shape)  17.9 us
    reduce_sum x1, other arithmetic, block_entries(): return jnp.sum(jnp.where(hit, chosen, jnp.float32(0.0)), axis=1)  10.5 us
    ppermute x2, starting transfers between devices, padded(): before = lax.ppermute(last, axis, up)  9.52 us
    reduce_sum x1, other arithmetic, softmax_rows(): return (probs.astype(jnp.bfloat16), jnp.sum(probs, axis=-1))  4.87 us
  transfers between devices with their start and end apart: 15, of which 9 were waited for; matrix products, arithmetic and copies ran while one was open for 18% of the time, Pallas kernels for 0%

profile of v2, /device:TPU:16, one launch (start us, length us, event | category | flops | bytes accessed | tf_op | source)
XLA Modules:
  0.0 209.7 jit_solution(14076969844879296448)
XLA Ops:
  5.8 3.0 %reshape_reshape.13 = bf16[32,144,128]{2,1,0:T(8,128)(2,1)} reshape(bf16[16,2,3,64,96]{4,3,2,1,0:T(8,128)(2,1)S(1)} %maximum_bitcast_fusion) | data formatting | bytes 2359296 | tf_op jit(solution)/shard_map/reshape;reshape | solution.py:96
  8.8 11.6 %all-to-all-start = ((bf16[32,144,128]{2,1,0:T(8,128)(2,1)}), bf16[32,144,128]{2,1,0:T(8,128)(2,1)}, u32[]{:S(2)}, u32[]{:S(2)}) async-start(bf16[32,144,128]{2,1,0:T(8,128)(2,1)} %reshape_reshape.13), calls=%async_computation | async-start | bytes 2359296 | tf_op jit(solution)/shard_map/all_to_all | solution.py:97
  25.8 25.8 %all-to-all-done = bf16[32,144,128]{2,1,0:T(8,128)(2,1)} async-done(((bf16[32,144,128]{2,1,0:T(8,128)(2,1)}), bf16[32,144,128]{2,1,0:T(8,128)(2,1)}, u32[]{:S(2)}, u32[]{:S(2)}) %all-to-all-start) | async-done | bytes 1179680 | tf_op jit(solution)/shard_map/all_to_all | solution.py:97
  55.9 4.7 %collective-permute-start.2 = (bf16[2,15,1536]{2,1,0:T(8,128)(2,1)S(1)}, bf16[2,15,1536]{2,1,0:T(8,128)(2,1)S(1)}, u32[]{:S(2)}, u32[]{:S(2)}) collective-permute-start(bf16[2,15,1536]{2,1,0:T(8,128)(2,1)S(1)} %get-tuple-element.77), channel_id=1, source_target_pairs={{0,1},{1,2},{2,3},{3,4},{4,5},{5,6},{6,7},{7,8},{8,9},{9,10},{10,1... | collective-permute-start | bytes 276488 | tf_op jit(solution)/shard_map/ppermute | solution.py:21
  60.7 3.3 %fusion = (f32[2048]{0:T(1024)S(1)}, f32[2048,2048]{0,1:T(8,128)S(1)}) fusion(pred[2048]{0:T(1024)(128)(4,1)S(1)} %iota_compare_fusion.2, bf16[2048,96]{1,0:T(8,128)(2,1)S(1)} %bitcast.48, bf16[2048,96]{1,0:T(8,128)(2,1)S(1)} %bitcast.49), kind=kOutput, calls=%fused_computation.4 | convolution fusion | flops 817887232 | bytes 17573888 | tf_op jit(solution)/shard_map/dot_general | solution.py:86
  64.0 4.9 %fusion.1 = f32[2048]{0:T(1024)S(1)} fusion(f32[2048,2048]{0,1:T(8,128)S(1)} %get-tuple-element.82, f32[2048]{0:T(1024)S(1)} %get-tuple-element.81, pred[2048]{0:T(1024)(128)(4,1)S(1)} %iota_compare_fusion.2), kind=kLoop, calls=%fused_computation.5 | loop fusion | flops 16775168 | bytes 16795648 | tf_op jit(solution)/shard_map/reduce_sum | solution.py:31
  68.9 3.9 %fusion.25 = bf16[2048,96]{0,1:T(8,128)(2,1)S(1)} fusion(bf16[2048,96]{1,0:T(8,128)(2,1)S(1)} %bitcast.50, f32[2048,2048]{0,1:T(8,128)S(1)} %get-tuple-element.82, f32[2048]{0:T(1024)S(1)} %get-tuple-element.81, pred[2048]{0:T(1024)(128)(4,1)S(1)} %iota_compare_fusion.2, f32[2048]{0:T(1024)S(1)} %fusion.1), kind=kOutput, calls=%fused_computation.79 | convolution fusion | flops 822476800 | bytes 17582080 | tf_op jit(solution)/shard_map/dot_general | solution.py:88
  74.5 6.4 %all-to-all-start.1 = ((bf16[32,48,128]{2,1,0:T(8,128)(2,1)}), bf16[32,48,128]{2,1,0:T(8,128)(2,1)S(1)}, u32[]{:S(2)}, u32[]{:S(2)}) async-start(bf16[32,48,128]{2,1,0:T(8,128)(2,1)} %reshape_reshape.14), calls=%async_computation.1 | async-start | bytes 786432 | tf_op jit(solution)/shard_map/all_to_all | solution.py:97
  81.3 3.1 %fusion.93 = bf16[2,64,1536]{2,1,0:T(8,128)(2,1)S(1)} fusion(f32[2,94,1536]{2,1,0:T(8,128)S(1)} %maximum_convert_fusion, f32[1536]{0:T(1024)S(1)} %get-tuple-element.40, f32[1536]{0:T(1024)S(1)} %get-tuple-element.41, f32[1536]{0:T(1024)S(1)} %get-tuple-element.42, f32[1536]{0:T(1024)S(1)} %get-tuple-element.43, f32[1536]{0:T(1024)S(1)} %get-tuple-element.44, ...), kind=kLoop, calls=%fused_computation.180 | loop fusion | flops 12386304 | bytes 24963584 | tf_op jit(solution)/shard_map/convert_element_type | solution.py:199
  84.7 9.1 %all-to-all-done.1 = bf16[32,48,128]{2,1,0:T(8,128)(2,1)S(1)} async-done(((bf16[32,48,128]{2,1,0:T(8,128)(2,1)}), bf16[32,48,128]{2,1,0:T(8,128)(2,1)S(1)}, u32[]{:S(2)}, u32[]{:S(2)}) %all-to-all-start.1) | async-done | bytes 393248 | tf_op jit(solution)/shard_map/all_to_all | solution.py:97
  96.6 3.2 %fusion.19 = bf16[2,64,1536]{2,1,0:T(8,128)(2,1)S(1)} fusion(bf16[2,64,1536]{2,1,0:T(8,128)(2,1)S(1)} %dot_general.19, bf16[1536,1536]{1,0:T(8,128)(2,1)} %param.15, bf16[2,64,1536]{2,1,0:T(8,128)(2,1)} %param.13, f32[2,64]{1,0:T(2,128)S(1)} %copy-done.61), kind=kOutput, calls=%fused_computation.49 | convolution fusion | flops 604766208 | bytes 5898752 | tf_op jit(solution)/shard_map/dot_general | solution.py:175
  101.2 4.8 %collective-permute-start = (bf16[2,15,1536]{2,1,0:T(8,128)(2,1)S(1)}, bf16[2,15,1536]{2,1,0:T(8,128)(2,1)S(1)}, u32[]{:S(2)}, u32[]{:S(2)}) collective-permute-start(bf16[2,15,1536]{2,1,0:T(8,128)(2,1)S(1)} %get-tuple-element.79), channel_id=1, source_target_pairs={{0,1},{1,2},{2,3},{3,4},{4,5},{5,6},{6,7},{7,8},{8,9},{9,10},{10,1... | collective-permute-start | bytes 276488 | tf_op jit(solution)/shard_map/ppermute | solution.py:21
  116.1 4.5 %fusion.90 = f32[1536,12,128]{2,0,1:T(8,128)} fusion(bf16[256,12,128]{0,2,1:T(8,128)(2,1)S(1)} %bitcast.47, bf16[2,256,1536]{1,2,0:T(8,128)(2,1)S(1)} %pad_maximum_fusion), kind=kOutput, calls=%fused_computation.176 | convolution fusion | flops 1207959552 | bytes 11010048 | tf_op jit(solution)/shard_map/ncl,nr->crl/dot_general | solution.py:62
  120.5 26.4 %gather_fusion = f32[11796,128]{1,0:T(8,128)} fusion(f32[18432,128]{1,0:T(8,128)} %bitcast.42, s32[12288]{0:T(1024)S(1)} %copy-done.1), kind=kCustom, calls=%fused_computation | custom fusion | bytes 12126288 | tf_op jit(solution)/shard_map/jit(_take)/gather | solution.py:44
  146.9 10.5 %select_reduce_fusion = f32[11796]{0:T(1024)S(1)} fusion(f32[11796,128]{1,0:T(8,128)} %gather_fusion, s32[11796]{0:T(1024)S(1)} %add_select_fusion.3, pred[11796]{0:T(1024)(128)(4,1)S(1)} %copy-done.58), kind=kLoop, calls=%fused_computation.40 | loop fusion | flops 6027756 | bytes 6145716 | tf_op jit(solution)/shard_map/reduce_sum | solution.py:47
  160.9 3.6 %collective-permute-done.6 = f32[24068]{0:T(1024)S(1)} collective-permute-done((f32[24068]{0:T(1024)S(1)}, f32[24068]{0:T(1024)S(1)}, u32[]{:S(2)}, u32[]{:S(2)}) %collective-permute-start.6) | collective-permute-done | bytes 96304 | tf_op jit(solution)/shard_map/ppermute | solution.py:80
  165.2 5.7 %collective-permute-done.7 = f32[24068]{0:T(1024)S(1)} collective-permute-done((f32[24068]{0:T(1024)S(1)}, f32[24068]{0:T(1024)S(1)}, u32[]{:S(2)}, u32[]{:S(2)}) %collective-permute-start.7) | collective-permute-done | bytes 96304 | tf_op jit(solution)/shard_map/ppermute | solution.py:80
  176.1 4.4 %collective-permute-start.9 = (f32[24068]{0:T(1024)S(1)}, f32[24068]{0:T(1024)S(1)}, u32[]{:S(2)}, u32[]{:S(2)}) collective-permute-start(f32[24068]{0:T(1024)S(1)} %add.347), channel_id=1, source_target_pairs={{0,2},{1,3},{2,0},{3,1},{4,6},{5,7},{6,4},{7,5},{8,10},{9,11},{10,... | collective-permute-start | bytes 288824 | tf_op jit(solution)/shard_map/ppermute | solution.py:80
  180.5 3.6 %collective-permute-done.9 = f32[24068]{0:T(1024)S(1)} collective-permute-done((f32[24068]{0:T(1024)S(1)}, f32[24068]{0:T(1024)S(1)}, u32[]{:S(2)}, u32[]{:S(2)}) %collective-permute-start.9) | collective-permute-done | bytes 96304 | tf_op jit(solution)/shard_map/ppermute | solution.py:80
  184.2 4.8 %collective-permute-start.10 = (f32[24068]{0:T(1024)S(1)}, f32[24068]{0:T(1024)S(1)}, u32[]{:S(2)}, u32[]{:S(2)}) collective-permute-start(f32[24068]{0:T(1024)S(1)} %add.348), channel_id=1, source_target_pairs={{0,4},{1,5},{2,6},{3,7},{4,0},{5,1},{6,2},{7,3},{8,12},{9,13},{10,... | collective-permute-start | bytes 288824 | tf_op jit(solution)/shard_map/ppermute | solution.py:80
  189.0 4.2 %collective-permute-done.10 = f32[24068]{0:T(1024)S(1)} collective-permute-done((f32[24068]{0:T(1024)S(1)}, f32[24068]{0:T(1024)S(1)}, u32[]{:S(2)}, u32[]{:S(2)}) %collective-permute-start.10) | collective-permute-done | bytes 96304 | tf_op jit(solution)/shard_map/ppermute | solution.py:80
  193.1 3.0 %collective-permute-start.11 = (f32[24068]{0:T(1024)S(1)}, f32[24068]{0:T(1024)S(1)}, u32[]{:S(2)}, u32[]{:S(2)}) collective-permute-start(f32[24068]{0:T(1024)S(1)} %add.349), channel_id=1, source_target_pairs={{0,8},{1,9},{2,10},{3,11},{4,12},{5,13},{6,14},{7,15},{8,0},{9,1},... | collective-permute-start | bytes 288824 | tf_op jit(solution)/shard_map/ppermute | solution.py:80
  196.1 4.7 %fusion.16 = bf16[2,64,1536]{2,1,0:T(8,128)(2,1)} fusion(bf16[2,64,1536]{2,1,0:T(8,128)(2,1)S(1)} %fusion.93, bf16[1536,1536]{1,0:T(8,128)(2,1)} %param.15), kind=kOutput, calls=%fused_computation.48 | convolution fusion | flops 604176384 | bytes 5505024 | tf_op jit(solution)/shard_map/dot_general | solution.py:201
  203.9 4.5 %fusion.58 = bf16[2,64,1536]{2,1,0:T(8,128)(2,1)} fusion(bf16[2,64,1536]{2,1,0:T(8,128)(2,1)S(1)} %fusion.19, bf16[2,15,1536]{2,1,0:T(8,128)(2,1)S(1)} %collective-permute-done.1, bf16[2,15,1536]{2,1,0:T(8,128)(2,1)S(1)} %collective-permute-done, f32[1536]{0:T(1024)S(1)} %get-tuple-element.40, f32[1536]{0:T(1024)S(1)} %get-tuple-element.41, ...), kind=kLoop, calls=%fused_computation.143 | loop fusion | flops 35979264 | bytes 1161216 | tf_op jit(solution)/shard_map/convert_element_type | solution.py:192
  (237 shorter events, 43.7 us)
Async XLA Ops:
  8.8 42.9 %all-to-all-start = ((bf16[32,144,128]{2,1,0:T(8,128)(2,1)}), bf16[32,144,128]{2,1,0:T(8,128)(2,1)}, u32[]{:S(2)}, u32[]{:S(2)}) async-start(bf16[32,144,128]{2,1,0:T(8,128)(2,1)} %reshape_reshape.13), calls=%async_computation | async-start | bytes 2359296 | tf_op jit(solution)/shard_map/all_to_all | solution.py:97
  23.1 58.0 %copy-start.34 = (f32[1536]{0:T(1024)}, f32[1536]{0:T(1024)S(1)}, u32[]{:S(2)}) copy-start(f32[1536]{0:T(1024)S(1)} %get-tuple-element.58) | copy-start | bytes 18436
  23.1 58.0 %copy-start.36 = (f32[1536]{0:T(1024)}, f32[1536]{0:T(1024)S(1)}, u32[]{:S(2)}) copy-start(f32[1536]{0:T(1024)S(1)} %get-tuple-element.59) | copy-start | bytes 18436
  23.1 58.0 %copy-start.38 = (f32[1536]{0:T(1024)}, f32[1536]{0:T(1024)S(1)}, u32[]{:S(2)}) copy-start(f32[1536]{0:T(1024)S(1)} %get-tuple-element.60) | copy-start | bytes 18436
  23.1 58.0 %copy-start.40 = (f32[1536]{0:T(1024)}, f32[1536]{0:T(1024)S(1)}, u32[]{:S(2)}) copy-start(f32[1536]{0:T(1024)S(1)} %get-tuple-element.61) | copy-start | bytes 18436
  23.1 58.0 %copy-start.42 = (f32[1536]{0:T(1024)}, f32[1536]{0:T(1024)S(1)}, u32[]{:S(2)}) copy-start(f32[1536]{0:T(1024)S(1)} %get-tuple-element.62) | copy-start | bytes 18436
  23.1 58.0 %copy-start.44 = (f32[1536]{0:T(1024)}, f32[1536]{0:T(1024)S(1)}, u32[]{:S(2)}) copy-start(f32[1536]{0:T(1024)S(1)} %get-tuple-element.63) | copy-start | bytes 18436
  23.1 58.0 %copy-start.46 = (f32[1536]{0:T(1024)}, f32[1536]{0:T(1024)S(1)}, u32[]{:S(2)}) copy-start(f32[1536]{0:T(1024)S(1)} %get-tuple-element.64) | copy-start | bytes 18436
  23.2 58.0 %copy-start.48 = (f32[1536]{0:T(1024)}, f32[1536]{0:T(1024)S(1)}, u32[]{:S(2)}) copy-start(f32[1536]{0:T(1024)S(1)} %get-tuple-element.65) | copy-start | bytes 18436
  23.2 58.0 %copy-start.50 = (f32[1536]{0:T(1024)}, f32[1536]{0:T(1024)S(1)}, u32[]{:S(2)}) copy-start(f32[1536]{0:T(1024)S(1)} %get-tuple-element.66) | copy-start | bytes 18436
  54.6 26.3 %collective-permute-start.3 = (bf16[2,15,1536]{2,1,0:T(8,128)(2,1)S(1)}, bf16[2,15,1536]{2,1,0:T(8,128)(2,1)S(1)}, u32[]{:S(2)}, u32[]{:S(2)}) collective-permute-start(bf16[2,15,1536]{2,1,0:T(8,128)(2,1)S(1)} %get-tuple-element.78), channel_id=1, source_target_pairs={{1,0},{2,1},{3,2},{4,3},{5,4},{6,5},{7,6},{8,7},{9,8},{10,9},{11,1... | collective-permute-start | bytes 276488 | tf_op jit(solution)/shard_map/ppermute | solution.py:22
  55.9 25.0 %collective-permute-start.2 = (bf16[2,15,1536]{2,1,0:T(8,128)(2,1)S(1)}, bf16[2,15,1536]{2,1,0:T(8,128)(2,1)S(1)}, u32[]{:S(2)}, u32[]{:S(2)}) collective-permute-start(bf16[2,15,1536]{2,1,0:T(8,128)(2,1)S(1)} %get-tuple-element.77), channel_id=1, source_target_pairs={{0,1},{1,2},{2,3},{3,4},{4,5},{5,6},{6,7},{7,8},{8,9},{9,10},{10,1... | collective-permute-start | bytes 276488 | tf_op jit(solution)/shard_map/ppermute | solution.py:21
  74.5 19.4 %all-to-all-start.1 = ((bf16[32,48,128]{2,1,0:T(8,128)(2,1)}), bf16[32,48,128]{2,1,0:T(8,128)(2,1)S(1)}, u32[]{:S(2)}, u32[]{:S(2)}) async-start(bf16[32,48,128]{2,1,0:T(8,128)(2,1)} %reshape_reshape.14), calls=%async_computation.1 | async-start | bytes 786432 | tf_op jit(solution)/shard_map/all_to_all | solution.py:97
  99.9 10.5 %collective-permute-start.1 = (bf16[2,15,1536]{2,1,0:T(8,128)(2,1)S(1)}, bf16[2,15,1536]{2,1,0:T(8,128)(2,1)S(1)}, u32[]{:S(2)}, u32[]{:S(2)}) collective-permute-start(bf16[2,15,1536]{2,1,0:T(8,128)(2,1)S(1)} %get-tuple-element.80), channel_id=1, source_target_pairs={{1,0},{2,1},{3,2},{4,3},{5,4},{6,5},{7,6},{8,7},{9,8},{10,9},{11,1... | collective-permute-start | bytes 276488 | tf_op jit(solution)/shard_map/ppermute | solution.py:22
  101.2 7.0 %collective-permute-start = (bf16[2,15,1536]{2,1,0:T(8,128)(2,1)S(1)}, bf16[2,15,1536]{2,1,0:T(8,128)(2,1)S(1)}, u32[]{:S(2)}, u32[]{:S(2)}) collective-permute-start(bf16[2,15,1536]{2,1,0:T(8,128)(2,1)S(1)} %get-tuple-element.79), channel_id=1, source_target_pairs={{0,1},{1,2},{2,3},{3,4},{4,5},{5,6},{6,7},{7,8},{8,9},{9,10},{10,1... | collective-permute-start | bytes 276488 | tf_op jit(solution)/shard_map/ppermute | solution.py:21
  106.4 8.2 %collective-permute-start.4 = (bf16[2,128,1536]{1,2,0:T(8,128)(2,1)S(1)}, bf16[2,128,1536]{1,2,0:T(8,128)(2,1)}, u32[]{:S(2)}, u32[]{:S(2)}) collective-permute-start(bf16[2,128,1536]{1,2,0:T(8,128)(2,1)S(1)} %pad_maximum_fusion.1), channel_id=1, source_target_pairs={{0,32},{32,0},{64,96},{96,64},{128,160},{160,128},{192,224},{224,1... | collective-permute-start | bytes 2359304 | tf_op jit(solution)/shard_map/ppermute | solution.py:57
  158.2 1.3 collective-permute-start.5
  159.6 4.9 %collective-permute-start.6 = (f32[24068]{0:T(1024)S(1)}, f32[24068]{0:T(1024)S(1)}, u32[]{:S(2)}, u32[]{:S(2)}) collective-permute-start(f32[24068]{0:T(1024)S(1)} %fusion.169), channel_id=1, source_target_pairs={{0,64},{32,96},{64,0},{96,32},{128,192},{160,224},{192,128},{224,1... | collective-permute-start | bytes 288824 | tf_op jit(solution)/shard_map/ppermute | solution.py:80
  164.8 6.2 %collective-permute-start.7 = (f32[24068]{0:T(1024)S(1)}, f32[24068]{0:T(1024)S(1)}, u32[]{:S(2)}, u32[]{:S(2)}) collective-permute-start(f32[24068]{0:T(1024)S(1)} %add.345), channel_id=1, source_target_pairs={{0,128},{32,160},{64,192},{96,224},{128,0},{160,32},{192,64},{224,... | collective-permute-start | bytes 288824 | tf_op jit(solution)/shard_map/ppermute | solution.py:80
  171.0 5.1 %collective-permute-start.8 = (f32[24068]{0:T(1024)S(1)}, f32[24068]{0:T(1024)S(1)}, u32[]{:S(2)}, u32[]{:S(2)}) collective-permute-start(f32[24068]{0:T(1024)S(1)} %add.346), channel_id=1, source_target_pairs={{0,1},{1,0},{2,3},{3,2},{4,5},{5,4},{6,7},{7,6},{8,9},{9,8},{10,11... | collective-permute-start | bytes 288824 | tf_op jit(solution)/shard_map/ppermute | solution.py:80
  176.1 8.0 %collective-permute-start.9 = (f32[24068]{0:T(1024)S(1)}, f32[24068]{0:T(1024)S(1)}, u32[]{:S(2)}, u32[]{:S(2)}) collective-permute-start(f32[24068]{0:T(1024)S(1)} %add.347), channel_id=1, source_target_pairs={{0,2},{1,3},{2,0},{3,1},{4,6},{5,7},{6,4},{7,5},{8,10},{9,11},{10,... | collective-permute-start | bytes 288824 | tf_op jit(solution)/shard_map/ppermute | solution.py:80
  184.2 9.0 %collective-permute-start.10 = (f32[24068]{0:T(1024)S(1)}, f32[24068]{0:T(1024)S(1)}, u32[]{:S(2)}, u32[]{:S(2)}) collective-permute-start(f32[24068]{0:T(1024)S(1)} %add.348), channel_id=1, source_target_pairs={{0,4},{1,5},{2,6},{3,7},{4,0},{5,1},{6,2},{7,3},{8,12},{9,13},{10,... | collective-permute-start | bytes 288824 | tf_op jit(solution)/shard_map/ppermute | solution.py:80
  193.1 7.7 %collective-permute-start.11 = (f32[24068]{0:T(1024)S(1)}, f32[24068]{0:T(1024)S(1)}, u32[]{:S(2)}, u32[]{:S(2)}) collective-permute-start(f32[24068]{0:T(1024)S(1)} %add.349), channel_id=1, source_target_pairs={{0,8},{1,9},{2,10},{3,11},{4,12},{5,13},{6,14},{7,15},{8,0},{9,1},... | collective-permute-start | bytes 288824 | tf_op jit(solution)/shard_map/ppermute | solution.py:80
  200.8 7.5 %collective-permute-start.12 = (f32[24068]{0:T(1024)S(1)}, f32[24068]{0:T(1024)S(1)}, u32[]{:S(2)}, u32[]{:S(2)}) collective-permute-start(f32[24068]{0:T(1024)S(1)} %add.350), channel_id=1, source_target_pairs={{0,16},{1,17},{2,18},{3,19},{4,20},{5,21},{6,22},{7,23},{8,24},{9,... | collective-permute-start | bytes 288824 | tf_op jit(solution)/shard_map/ppermute | solution.py:80
  (57 other events, 2335.2 us)

commit v3 on v2

--- a/solution.py
+++ b/solution.py
@@ -67,14 +67,14 @@
     mine = lax.dynamic_slice(padded_picks, (first,), (rows,))
     block_of = (mine % table_rows) // lane * table_rows + mine // table_rows
     values = block_entries(table.reshape(-1, lane), block_of, mine % lane)
-    spread = lax.dynamic_update_slice(jnp.zeros((rows * group,), jnp.float32), values, (first,))
-    return spread[:total]
-
-
-def butterfly_sum(value, axes):
+    return values, lax.axis_index(axis) % group
+
+
+def butterfly_sum(value, axes, first_step=None):
+    first_step = first_step or {}
     for axis in axes:
         count = lax.axis_size(axis)
-        step = 1
+        step = first_step.get(axis, 1)
         while step < count:
             pairs = [(i, i ^ step) for i in range(count)]
             value = value + lax.ppermute(value, axis, pairs)
@@ -202,10 +202,16 @@
         grad_flat, out_weight, (((1,), (1,)), ((), ())), preferred_element_type=jnp.float32
     )
     context_grad = context_grad.reshape(local_utts, frames_dev, width).astype(jnp.bfloat16)
-    weight_vals = group_picks(context_flat, grad_flat, pick_weight, "dp", 1)
+    weight_half, member = group_picks(context_flat, grad_flat, pick_weight, "dp", 1)
     kernel_vals = pick_entries(kernel_grad, pick_kernel)
-    joined = butterfly_sum(jnp.concatenate([weight_vals, kernel_vals]), ("dp", "seq"))
-    weight_sum, kernel_sum = joined[: weight_vals.shape[0]], joined[weight_vals.shape[0] :]
+    half_count = weight_half.shape[0]
+    joined = butterfly_sum(jnp.concatenate([weight_half, kernel_vals]), ("dp", "seq"), {"dp": 2})
+    dp_count = lax.axis_size("dp")
+    other = lax.ppermute(joined, "dp", [(i, i ^ 1) for i in range(dp_count)])
+    low, high = jnp.where(member == 0, joined, other), jnp.where(member == 0, other, joined)
+    total = pick_weight.shape[0]
+    weight_sum = jnp.concatenate([low[:half_count], high[:half_count]])[:total]
+    kernel_sum = low[half_count:] + high[half_count:]
     total_slots = local_utts * lax.axis_size("dp") * full_frames
     norm_factor = 1.0 / math.sqrt(total_slots)
     return (conv_out, context_grad, weight_sum * norm_factor, kernel_sum * norm_factor)

time: 210 us -> 209 us (level); the launches traced: 210 us -> 206 us
  waiting for transfers between devices: 57.4 us -> 53.5 us
    ppermute x8 -> x7, waiting for transfers between devices: 21 us -> 17.1 us  [butterfly_sum(): value = value + lax.ppermute(value, axis, pairs)]
    ppermute x8 -> x7, starting transfers between devices: 19.2 us -> 20.4 us  [butterfly_sum(): value = value + lax.ppermute(value, axis, pairs)]
  transfers between devices with their start and end apart: 15 -> 15, of which waited for: 9 -> 9; matrix products, arithmetic and copies ran while one was open for 18% -> 19% of each run, Pallas kernels for 0% -> 0%
where the time goes in v3:
time: 209 us; the launch traced here: 206 us
  waiting for transfers between devices  53.5 us (26%)
  starting transfers between devices  50.9 us (24%)
  local copies, waits for them, and re-layouts  45.2 us (22%)
  other arithmetic  34.9 us (17%)
  matrix products  19.6 us (9%)
  between operations  2.3 us (1%)
    all_to_all x2, waiting for transfers between devices, lane_dense_all_to_all(): return lax.all_to_all(dense, 'seq', 0, 0, tiled=True).reshape(value.shape)  35 us
    gather x1, local copies, waits for them, and re-layouts, block_entries(): chosen = jnp.take(blocks, block_of, axis=0)  26.4 us
    ppermute x7, starting transfers between devices, butterfly_sum(): value = value + lax.ppermute(value, axis, pairs)  20.4 us
    all_to_all x2, starting transfers between devices, lane_dense_all_to_all(): return lax.all_to_all(dense, 'seq', 0, 0, tiled=True).reshape(value.shape)  18 us
    ppermute x7, waiting for transfers between devices, butterfly_sum(): value = value + lax.ppermute(value, axis, pairs)  17.1 us
    reduce_sum x1, other arithmetic, block_entries(): return jnp.sum(jnp.where(hit, chosen, jnp.float32(0.0)), axis=1)  10.5 us
    ppermute x2, starting transfers between devices, padded(): before = lax.ppermute(last, axis, up)  9.53 us
    reduce_sum x1, other arithmetic, softmax_rows(): return (probs.astype(jnp.bfloat16), jnp.sum(probs, axis=-1))  4.87 us
  transfers between devices with their start and end apart: 15, of which 9 were waited for; matrix products, arithmetic and copies ran while one was open for 19% of the time, Pallas kernels for 0%

profile of v3, /device:TPU:16, one launch (start us, length us, event | category | flops | bytes accessed | tf_op | source)
XLA Modules:
  0.0 206.5 jit_solution(16920792292600987413)
XLA Ops:
  5.8 3.0 %reshape_reshape.13 = bf16[32,144,128]{2,1,0:T(8,128)(2,1)} reshape(bf16[16,2,3,64,96]{4,3,2,1,0:T(8,128)(2,1)S(1)} %maximum_bitcast_fusion) | data formatting | bytes 2359296 | tf_op jit(solution)/shard_map/reshape;reshape | solution.py:96
  8.8 11.6 %all-to-all-start = ((bf16[32,144,128]{2,1,0:T(8,128)(2,1)}), bf16[32,144,128]{2,1,0:T(8,128)(2,1)}, u32[]{:S(2)}, u32[]{:S(2)}) async-start(bf16[32,144,128]{2,1,0:T(8,128)(2,1)} %reshape_reshape.13), calls=%async_computation | async-start | bytes 2359296 | tf_op jit(solution)/shard_map/all_to_all | solution.py:97
  25.8 25.8 %all-to-all-done = bf16[32,144,128]{2,1,0:T(8,128)(2,1)} async-done(((bf16[32,144,128]{2,1,0:T(8,128)(2,1)}), bf16[32,144,128]{2,1,0:T(8,128)(2,1)}, u32[]{:S(2)}, u32[]{:S(2)}) %all-to-all-start) | async-done | bytes 1179680 | tf_op jit(solution)/shard_map/all_to_all | solution.py:97
  51.7 2.7 %reshape.117 = bf16[32,3,64,96]{3,2,1,0:T(8,128)(2,1)S(1)} reshape(bf16[32,144,128]{2,1,0:T(8,128)(2,1)} %all-to-all-done) | data formatting | bytes 2359296 | tf_op jit(solution)/shard_map/reshape | solution.py:97
  55.9 4.7 %collective-permute-start.2 = (bf16[2,15,1536]{2,1,0:T(8,128)(2,1)S(1)}, bf16[2,15,1536]{2,1,0:T(8,128)(2,1)S(1)}, u32[]{:S(2)}, u32[]{:S(2)}) collective-permute-start(bf16[2,15,1536]{2,1,0:T(8,128)(2,1)S(1)} %get-tuple-element.77), channel_id=1, source_target_pairs={{0,1},{1,2},{2,3},{3,4},{4,5},{5,6},{6,7},{7,8},{8,9},{9,10},{10,1... | collective-permute-start | bytes 276488 | tf_op jit(solution)/shard_map/ppermute | solution.py:21
  60.7 3.3 %fusion = (f32[2048]{0:T(1024)S(1)}, f32[2048,2048]{0,1:T(8,128)S(1)}) fusion(pred[2048]{0:T(1024)(128)(4,1)S(1)} %iota_compare_fusion.2, bf16[2048,96]{1,0:T(8,128)(2,1)S(1)} %bitcast.50, bf16[2048,96]{1,0:T(8,128)(2,1)S(1)} %bitcast.51), kind=kOutput, calls=%fused_computation.4 | convolution fusion | flops 817887232 | bytes 17573888 | tf_op jit(solution)/shard_map/dot_general | solution.py:86
  64.0 4.9 %fusion.1 = f32[2048]{0:T(1024)S(1)} fusion(f32[2048,2048]{0,1:T(8,128)S(1)} %get-tuple-element.84, f32[2048]{0:T(1024)S(1)} %get-tuple-element.83, pred[2048]{0:T(1024)(128)(4,1)S(1)} %iota_compare_fusion.2), kind=kLoop, calls=%fused_computation.5 | loop fusion | flops 16775168 | bytes 16795648 | tf_op jit(solution)/shard_map/reduce_sum | solution.py:31
  68.9 3.9 %fusion.25 = bf16[2048,96]{0,1:T(8,128)(2,1)S(1)} fusion(bf16[2048,96]{1,0:T(8,128)(2,1)S(1)} %bitcast.52, f32[2048,2048]{0,1:T(8,128)S(1)} %get-tuple-element.84, f32[2048]{0:T(1024)S(1)} %get-tuple-element.83, pred[2048]{0:T(1024)(128)(4,1)S(1)} %iota_compare_fusion.2, f32[2048]{0:T(1024)S(1)} %fusion.1), kind=kOutput, calls=%fused_computation.79 | convolution fusion | flops 822476800 | bytes 17582080 | tf_op jit(solution)/shard_map/dot_general | solution.py:88
  74.5 6.4 %all-to-all-start.1 = ((bf16[32,48,128]{2,1,0:T(8,128)(2,1)}), bf16[32,48,128]{2,1,0:T(8,128)(2,1)S(1)}, u32[]{:S(2)}, u32[]{:S(2)}) async-start(bf16[32,48,128]{2,1,0:T(8,128)(2,1)} %reshape_reshape.14), calls=%async_computation.1 | async-start | bytes 786432 | tf_op jit(solution)/shard_map/all_to_all | solution.py:97
  81.3 3.1 %fusion.93 = bf16[2,64,1536]{2,1,0:T(8,128)(2,1)S(1)} fusion(f32[2,94,1536]{2,1,0:T(8,128)S(1)} %maximum_convert_fusion, f32[1536]{0:T(1024)S(1)} %get-tuple-element.40, f32[1536]{0:T(1024)S(1)} %get-tuple-element.41, f32[1536]{0:T(1024)S(1)} %get-tuple-element.42, f32[1536]{0:T(1024)S(1)} %get-tuple-element.43, f32[1536]{0:T(1024)S(1)} %get-tuple-element.44, ...), kind=kLoop, calls=%fused_computation.180 | loop fusion | flops 12386304 | bytes 24963584 | tf_op jit(solution)/shard_map/convert_element_type | solution.py:199
  84.7 9.1 %all-to-all-done.1 = bf16[32,48,128]{2,1,0:T(8,128)(2,1)S(1)} async-done(((bf16[32,48,128]{2,1,0:T(8,128)(2,1)}), bf16[32,48,128]{2,1,0:T(8,128)(2,1)S(1)}, u32[]{:S(2)}, u32[]{:S(2)}) %all-to-all-start.1) | async-done | bytes 393248 | tf_op jit(solution)/shard_map/all_to_all | solution.py:97
  96.6 3.2 %fusion.19 = bf16[2,64,1536]{2,1,0:T(8,128)(2,1)S(1)} fusion(bf16[2,64,1536]{2,1,0:T(8,128)(2,1)S(1)} %dot_general.19, bf16[1536,1536]{1,0:T(8,128)(2,1)} %param.15, bf16[2,64,1536]{2,1,0:T(8,128)(2,1)} %param.13, f32[2,64]{1,0:T(2,128)S(1)} %copy-done.61), kind=kOutput, calls=%fused_computation.49 | convolution fusion | flops 604766208 | bytes 5898752 | tf_op jit(solution)/shard_map/dot_general | solution.py:175
  101.2 4.8 %collective-permute-start = (bf16[2,15,1536]{2,1,0:T(8,128)(2,1)S(1)}, bf16[2,15,1536]{2,1,0:T(8,128)(2,1)S(1)}, u32[]{:S(2)}, u32[]{:S(2)}) collective-permute-start(bf16[2,15,1536]{2,1,0:T(8,128)(2,1)S(1)} %get-tuple-element.79), channel_id=1, source_target_pairs={{0,1},{1,2},{2,3},{3,4},{4,5},{5,6},{6,7},{7,8},{8,9},{9,10},{10,1... | collective-permute-start | bytes 276488 | tf_op jit(solution)/shard_map/ppermute | solution.py:21
  116.1 4.5 %fusion.90 = f32[1536,12,128]{2,0,1:T(8,128)} fusion(bf16[256,12,128]{0,2,1:T(8,128)(2,1)S(1)} %bitcast.49, bf16[2,256,1536]{1,2,0:T(8,128)(2,1)S(1)} %pad_maximum_fusion), kind=kOutput, calls=%fused_computation.176 | convolution fusion | flops 1207959552 | bytes 11010048 | tf_op jit(solution)/shard_map/ncl,nr->crl/dot_general | solution.py:62
  120.5 26.4 %gather_fusion = f32[11796,128]{1,0:T(8,128)} fusion(f32[18432,128]{1,0:T(8,128)} %bitcast.44, s32[12288]{0:T(1024)S(1)} %copy-done.1), kind=kCustom, calls=%fused_computation | custom fusion | bytes 12126288 | tf_op jit(solution)/shard_map/jit(_take)/gather | solution.py:44
  146.9 10.5 %select_reduce_fusion = f32[11796]{0:T(1024)S(1)} fusion(f32[11796,128]{1,0:T(8,128)} %gather_fusion, s32[11796]{0:T(1024)S(1)} %add_select_fusion.3, pred[11796]{0:T(1024)(128)(4,1)S(1)} %copy-done.58), kind=kLoop, calls=%fused_computation.40 | loop fusion | flops 6027756 | bytes 6145716 | tf_op jit(solution)/shard_map/reduce_sum | solution.py:47
  159.1 2.8 %collective-permute-done.5 = f32[12272]{0:T(1024)S(1)} collective-permute-done((f32[12272]{0:T(1024)S(1)}, f32[12272]{0:T(1024)S(1)}, u32[]{:S(2)}, u32[]{:S(2)}) %collective-permute-start.5) | collective-permute-done | bytes 49120 | tf_op jit(solution)/shard_map/ppermute | solution.py:80
  162.4 5.2 %collective-permute-done.6 = f32[12272]{0:T(1024)S(1)} collective-permute-done((f32[12272]{0:T(1024)S(1)}, f32[12272]{0:T(1024)S(1)}, u32[]{:S(2)}, u32[]{:S(2)}) %collective-permute-start.6) | collective-permute-done | bytes 49120 | tf_op jit(solution)/shard_map/ppermute | solution.py:80
  172.4 3.7 %collective-permute-start.8 = (f32[12272]{0:T(1024)S(1)}, f32[12272]{0:T(1024)S(1)}, u32[]{:S(2)}, u32[]{:S(2)}) collective-permute-start(f32[12272]{0:T(1024)S(1)} %add.346), channel_id=1, source_target_pairs={{0,2},{1,3},{2,0},{3,1},{4,6},{5,7},{6,4},{7,5},{8,10},{9,11},{10,... | collective-permute-start | bytes 147272 | tf_op jit(solution)/shard_map/ppermute | solution.py:80
  178.2 5.4 %collective-permute-start.9 = (f32[12272]{0:T(1024)S(1)}, f32[12272]{0:T(1024)S(1)}, u32[]{:S(2)}, u32[]{:S(2)}) collective-permute-start(f32[12272]{0:T(1024)S(1)} %add.347), channel_id=1, source_target_pairs={{0,4},{1,5},{2,6},{3,7},{4,0},{5,1},{6,2},{7,3},{8,12},{9,13},{10,... | collective-permute-start | bytes 147272 | tf_op jit(solution)/shard_map/ppermute | solution.py:80
  186.3 3.9 %collective-permute-start.10 = (f32[12272]{0:T(1024)S(1)}, f32[12272]{0:T(1024)S(1)}, u32[]{:S(2)}, u32[]{:S(2)}) collective-permute-start(f32[12272]{0:T(1024)S(1)} %add.348), channel_id=1, source_target_pairs={{0,8},{1,9},{2,10},{3,11},{4,12},{5,13},{6,14},{7,15},{8,0},{9,1},... | collective-permute-start | bytes 147272 | tf_op jit(solution)/shard_map/ppermute | solution.py:80
  192.3 3.2 %collective-permute-start.11 = (f32[12272]{0:T(1024)S(1)}, f32[12272]{0:T(1024)S(1)}, u32[]{:S(2)}, u32[]{:S(2)}) collective-permute-start(f32[12272]{0:T(1024)S(1)} %add.349), channel_id=1, source_target_pairs={{0,16},{1,17},{2,18},{3,19},{4,20},{5,21},{6,22},{7,23},{8,24},{9,... | collective-permute-start | bytes 147272 | tf_op jit(solution)/shard_map/ppermute | solution.py:80
  195.5 4.7 %fusion.16 = bf16[2,64,1536]{2,1,0:T(8,128)(2,1)} fusion(bf16[2,64,1536]{2,1,0:T(8,128)(2,1)S(1)} %fusion.93, bf16[1536,1536]{1,0:T(8,128)(2,1)} %param.15), kind=kOutput, calls=%fused_computation.48 | convolution fusion | flops 604176384 | bytes 5505024 | tf_op jit(solution)/shard_map/dot_general | solution.py:201
  200.6 4.5 %fusion.58 = bf16[2,64,1536]{2,1,0:T(8,128)(2,1)} fusion(bf16[2,64,1536]{2,1,0:T(8,128)(2,1)S(1)} %fusion.19, bf16[2,15,1536]{2,1,0:T(8,128)(2,1)S(1)} %collective-permute-done.1, bf16[2,15,1536]{2,1,0:T(8,128)(2,1)S(1)} %collective-permute-done, f32[1536]{0:T(1024)S(1)} %get-tuple-element.40, f32[1536]{0:T(1024)S(1)} %get-tuple-element.41, ...), kind=kLoop, calls=%fused_computation.143 | loop fusion | flops 35979264 | bytes 1161216 | tf_op jit(solution)/shard_map/convert_element_type | solution.py:192
  (235 shorter events, 42.7 us)
Async XLA Ops:
  8.8 42.9 %all-to-all-start = ((bf16[32,144,128]{2,1,0:T(8,128)(2,1)}), bf16[32,144,128]{2,1,0:T(8,128)(2,1)}, u32[]{:S(2)}, u32[]{:S(2)}) async-start(bf16[32,144,128]{2,1,0:T(8,128)(2,1)} %reshape_reshape.13), calls=%async_computation | async-start | bytes 2359296 | tf_op jit(solution)/shard_map/all_to_all | solution.py:97
  23.1 58.0 %copy-start.34 = (f32[1536]{0:T(1024)}, f32[1536]{0:T(1024)S(1)}, u32[]{:S(2)}) copy-start(f32[1536]{0:T(1024)S(1)} %get-tuple-element.58) | copy-start | bytes 18436
  23.1 58.0 %copy-start.36 = (f32[1536]{0:T(1024)}, f32[1536]{0:T(1024)S(1)}, u32[]{:S(2)}) copy-start(f32[1536]{0:T(1024)S(1)} %get-tuple-element.59) | copy-start | bytes 18436
  23.1 58.0 %copy-start.38 = (f32[1536]{0:T(1024)}, f32[1536]{0:T(1024)S(1)}, u32[]{:S(2)}) copy-start(f32[1536]{0:T(1024)S(1)} %get-tuple-element.60) | copy-start | bytes 18436
  23.1 58.0 %copy-start.40 = (f32[1536]{0:T(1024)}, f32[1536]{0:T(1024)S(1)}, u32[]{:S(2)}) copy-start(f32[1536]{0:T(1024)S(1)} %get-tuple-element.61) | copy-start | bytes 18436
  23.1 58.0 %copy-start.42 = (f32[1536]{0:T(1024)}, f32[1536]{0:T(1024)S(1)}, u32[]{:S(2)}) copy-start(f32[1536]{0:T(1024)S(1)} %get-tuple-element.62) | copy-start | bytes 18436
  23.1 58.0 %copy-start.44 = (f32[1536]{0:T(1024)}, f32[1536]{0:T(1024)S(1)}, u32[]{:S(2)}) copy-start(f32[1536]{0:T(1024)S(1)} %get-tuple-element.63) | copy-start | bytes 18436
  23.1 58.0 %copy-start.46 = (f32[1536]{0:T(1024)}, f32[1536]{0:T(1024)S(1)}, u32[]{:S(2)}) copy-start(f32[1536]{0:T(1024)S(1)} %get-tuple-element.64) | copy-start | bytes 18436
  23.2 58.0 %copy-start.48 = (f32[1536]{0:T(1024)}, f32[1536]{0:T(1024)S(1)}, u32[]{:S(2)}) copy-start(f32[1536]{0:T(1024)S(1)} %get-tuple-element.65) | copy-start | bytes 18436
  23.2 58.0 %copy-start.50 = (f32[1536]{0:T(1024)}, f32[1536]{0:T(1024)S(1)}, u32[]{:S(2)}) copy-start(f32[1536]{0:T(1024)S(1)} %get-tuple-element.66) | copy-start | bytes 18436
  54.6 26.3 %collective-permute-start.3 = (bf16[2,15,1536]{2,1,0:T(8,128)(2,1)S(1)}, bf16[2,15,1536]{2,1,0:T(8,128)(2,1)S(1)}, u32[]{:S(2)}, u32[]{:S(2)}) collective-permute-start(bf16[2,15,1536]{2,1,0:T(8,128)(2,1)S(1)} %get-tuple-element.78), channel_id=1, source_target_pairs={{1,0},{2,1},{3,2},{4,3},{5,4},{6,5},{7,6},{8,7},{9,8},{10,9},{11,1... | collective-permute-start | bytes 276488 | tf_op jit(solution)/shard_map/ppermute | solution.py:22
  55.9 25.0 %collective-permute-start.2 = (bf16[2,15,1536]{2,1,0:T(8,128)(2,1)S(1)}, bf16[2,15,1536]{2,1,0:T(8,128)(2,1)S(1)}, u32[]{:S(2)}, u32[]{:S(2)}) collective-permute-start(bf16[2,15,1536]{2,1,0:T(8,128)(2,1)S(1)} %get-tuple-element.77), channel_id=1, source_target_pairs={{0,1},{1,2},{2,3},{3,4},{4,5},{5,6},{6,7},{7,8},{8,9},{9,10},{10,1... | collective-permute-start | bytes 276488 | tf_op jit(solution)/shard_map/ppermute | solution.py:21
  74.5 19.4 %all-to-all-start.1 = ((bf16[32,48,128]{2,1,0:T(8,128)(2,1)}), bf16[32,48,128]{2,1,0:T(8,128)(2,1)S(1)}, u32[]{:S(2)}, u32[]{:S(2)}) async-start(bf16[32,48,128]{2,1,0:T(8,128)(2,1)} %reshape_reshape.14), calls=%async_computation.1 | async-start | bytes 786432 | tf_op jit(solution)/shard_map/all_to_all | solution.py:97
  99.9 10.5 %collective-permute-start.1 = (bf16[2,15,1536]{2,1,0:T(8,128)(2,1)S(1)}, bf16[2,15,1536]{2,1,0:T(8,128)(2,1)S(1)}, u32[]{:S(2)}, u32[]{:S(2)}) collective-permute-start(bf16[2,15,1536]{2,1,0:T(8,128)(2,1)S(1)} %get-tuple-element.80), channel_id=1, source_target_pairs={{1,0},{2,1},{3,2},{4,3},{5,4},{6,5},{7,6},{8,7},{9,8},{10,9},{11,1... | collective-permute-start | bytes 276488 | tf_op jit(solution)/shard_map/ppermute | solution.py:22
  101.2 7.0 %collective-permute-start = (bf16[2,15,1536]{2,1,0:T(8,128)(2,1)S(1)}, bf16[2,15,1536]{2,1,0:T(8,128)(2,1)S(1)}, u32[]{:S(2)}, u32[]{:S(2)}) collective-permute-start(bf16[2,15,1536]{2,1,0:T(8,128)(2,1)S(1)} %get-tuple-element.79), channel_id=1, source_target_pairs={{0,1},{1,2},{2,3},{3,4},{4,5},{5,6},{6,7},{7,8},{8,9},{9,10},{10,1... | collective-permute-start | bytes 276488 | tf_op jit(solution)/shard_map/ppermute | solution.py:21
  106.4 8.2 %collective-permute-start.4 = (bf16[2,128,1536]{1,2,0:T(8,128)(2,1)S(1)}, bf16[2,128,1536]{1,2,0:T(8,128)(2,1)}, u32[]{:S(2)}, u32[]{:S(2)}) collective-permute-start(bf16[2,128,1536]{1,2,0:T(8,128)(2,1)S(1)} %pad_maximum_fusion.1), channel_id=1, source_target_pairs={{0,32},{32,0},{64,96},{96,64},{128,160},{160,128},{192,224},{224,1... | collective-permute-start | bytes 2359304 | tf_op jit(solution)/shard_map/ppermute | solution.py:57
  157.8 4.1 %collective-permute-start.5 = (f32[12272]{0:T(1024)S(1)}, f32[12272]{0:T(1024)S(1)}, u32[]{:S(2)}, u32[]{:S(2)}) collective-permute-start(f32[12272]{0:T(1024)S(1)} %pad_maximum_fusion.4), channel_id=1, source_target_pairs={{0,64},{32,96},{64,0},{96,32},{128,192},{160,224},{192,128},{224,1... | collective-permute-start | bytes 147272 | tf_op jit(solution)/shard_map/ppermute | solution.py:80
  162.0 5.6 %collective-permute-start.6 = (f32[12272]{0:T(1024)S(1)}, f32[12272]{0:T(1024)S(1)}, u32[]{:S(2)}, u32[]{:S(2)}) collective-permute-start(f32[12272]{0:T(1024)S(1)} %fusion.170), channel_id=1, source_target_pairs={{0,128},{32,160},{64,192},{96,224},{128,0},{160,32},{192,64},{224,... | collective-permute-start | bytes 147272 | tf_op jit(solution)/shard_map/ppermute | solution.py:80
  167.6 4.7 %collective-permute-start.7 = (f32[12272]{0:T(1024)S(1)}, f32[12272]{0:T(1024)S(1)}, u32[]{:S(2)}, u32[]{:S(2)}) collective-permute-start(f32[12272]{0:T(1024)S(1)} %add.345), channel_id=1, source_target_pairs={{0,1},{1,0},{2,3},{3,2},{4,5},{5,4},{6,7},{7,6},{8,9},{9,8},{10,11... | collective-permute-start | bytes 147272 | tf_op jit(solution)/shard_map/ppermute | solution.py:80
  172.4 5.8 %collective-permute-start.8 = (f32[12272]{0:T(1024)S(1)}, f32[12272]{0:T(1024)S(1)}, u32[]{:S(2)}, u32[]{:S(2)}) collective-permute-start(f32[12272]{0:T(1024)S(1)} %add.346), channel_id=1, source_target_pairs={{0,2},{1,3},{2,0},{3,1},{4,6},{5,7},{6,4},{7,5},{8,10},{9,11},{10,... | collective-permute-start | bytes 147272 | tf_op jit(solution)/shard_map/ppermute | solution.py:80
  178.2 8.1 %collective-permute-start.9 = (f32[12272]{0:T(1024)S(1)}, f32[12272]{0:T(1024)S(1)}, u32[]{:S(2)}, u32[]{:S(2)}) collective-permute-start(f32[12272]{0:T(1024)S(1)} %add.347), channel_id=1, source_target_pairs={{0,4},{1,5},{2,6},{3,7},{4,0},{5,1},{6,2},{7,3},{8,12},{9,13},{10,... | collective-permute-start | bytes 147272 | tf_op jit(solution)/shard_map/ppermute | solution.py:80
  186.3 6.0 %collective-permute-start.10 = (f32[12272]{0:T(1024)S(1)}, f32[12272]{0:T(1024)S(1)}, u32[]{:S(2)}, u32[]{:S(2)}) collective-permute-start(f32[12272]{0:T(1024)S(1)} %add.348), channel_id=1, source_target_pairs={{0,8},{1,9},{2,10},{3,11},{4,12},{5,13},{6,14},{7,15},{8,0},{9,1},... | collective-permute-start | bytes 147272 | tf_op jit(solution)/shard_map/ppermute | solution.py:80
  192.3 7.9 %collective-permute-start.11 = (f32[12272]{0:T(1024)S(1)}, f32[12272]{0:T(1024)S(1)}, u32[]{:S(2)}, u32[]{:S(2)}) collective-permute-start(f32[12272]{0:T(1024)S(1)} %add.349), channel_id=1, source_target_pairs={{0,16},{1,17},{2,18},{3,19},{4,20},{5,21},{6,22},{7,23},{8,24},{9,... | collective-permute-start | bytes 147272 | tf_op jit(solution)/shard_map/ppermute | solution.py:80
  200.2 4.9 %collective-permute-start.12 = (f32[12272]{0:T(1024)S(1)}, f32[12272]{0:T(1024)S(1)}, u32[]{:S(2)}, u32[]{:S(2)}) collective-permute-start(f32[12272]{0:T(1024)S(1)} %add.350), channel_id=1, source_target_pairs={{0,32},{32,0},{64,96},{96,64},{128,160},{160,128},{192,224},{224,1... | collective-permute-start | bytes 147272 | tf_op jit(solution)/shard_map/ppermute | solution.py:210
  (57 other events, 2437.1 us)

commit v4 on v3

--- a/solution.py
+++ b/solution.py
@@ -181,7 +181,8 @@
     tap_count = conv_kernel.shape[0]
     half_taps = (tap_count - 1) // 2
     kernel_f = conv_kernel.astype(jnp.float32)
-    hidden_pad = padded(hidden, (("seq", 1),), half_taps)
+    both_pad = padded(jnp.stack([hidden, conv_cotangent]), (("seq", 2),), half_taps)
+    hidden_pad = both_pad[0]
     cot_f = conv_cotangent.astype(jnp.float32)
     conv_sum = jnp.zeros((local_utts, frames_dev, width), jnp.float32)
     kernel_rows = []
@@ -191,7 +192,7 @@
         kernel_rows.append(jnp.sum(window * cot_f, axis=(0, 1)))
     conv_out = conv_sum.astype(jnp.bfloat16)
     kernel_grad = jnp.stack(kernel_rows)
-    cot_pad = padded(conv_cotangent, (("seq", 1),), half_taps).astype(jnp.float32)
+    cot_pad = both_pad[1].astype(jnp.float32)
     back_sum = jnp.zeros((local_utts, frames_dev, width), jnp.float32)
     for offset in range(tap_count):
         begin = 2 * half_taps - offset

time: 209 us -> 201 us (0.962)
  starting transfers between devices: 50.9 us -> 29.4 us
  waiting for transfers between devices: 53.5 us -> 70.4 us
  matrix products: 19.6 us -> 17.2 us
    ppermute x7, starting transfers between devices: 20.4 us -> 7.01 us  [butterfly_sum(): value = value + lax.ppermute(value, axis, pairs)]
    ppermute x7, waiting for transfers between devices: 17.1 us -> 26.6 us  [butterfly_sum(): value = value + lax.ppermute(value, axis, pairs)]
    all_to_all x2, waiting for transfers between devices: 35 us -> 40.9 us  [lane_dense_all_to_all(): return lax.all_to_all(dense, 'seq', 0, 0, tiled=True).reshape(value.shape)]
    ppermute x2 -> x1, starting transfers between devices: 9.53 us -> 4.26 us  [padded(): before = lax.ppermute(last, axis, up)]
    ppermute x2 -> x1, waiting for transfers between devices: 0.01 us -> 2.85 us  [padded(): after = lax.ppermute(leading, axis, down)]
    dot_general x1, matrix products: 4.71 us -> 2.4 us  [on_device(): lax.dot_general(grad_flat, out_weight, (((1,), (1,)), ((), ())), preferre...]
  transfers between devices with their start and end apart: 15 -> 13, of which waited for: 9 -> 10; matrix products, arithmetic and copies ran while one was open for 19% -> 10% of each run, Pallas kernels for 0% -> 0%
where the time goes in v4:
time: 201 us; the launch traced here: 199 us
  waiting for transfers between devices  70.4 us (35%)
  local copies, waits for them, and re-layouts  44.6 us (22%)
  other arithmetic  35.5 us (18%)
  starting transfers between devices  29.4 us (15%)
  matrix products  17.2 us (9%)
    all_to_all x2, waiting for transfers between devices, lane_dense_all_to_all(): return lax.all_to_all(dense, 'seq', 0, 0, tiled=True).reshape(value.shape)  40.9 us
    ppermute x7, waiting for transfers between devices, butterfly_sum(): value = value + lax.ppermute(value, axis, pairs)  26.6 us
    gather x1, local copies, waits for them, and re-layouts, block_entries(): chosen = jnp.take(blocks, block_of, axis=0)  26.4 us
    all_to_all x2, starting transfers between devices, lane_dense_all_to_all(): return lax.all_to_all(dense, 'seq', 0, 0, tiled=True).reshape(value.shape)  16.7 us
    reduce_sum x1, other arithmetic, block_entries(): return jnp.sum(jnp.where(hit, chosen, jnp.float32(0.0)), axis=1)  10.5 us
    ppermute x7, starting transfers between devices, butterfly_sum(): value = value + lax.ppermute(value, axis, pairs)  7.01 us
    reduce_sum x1, other arithmetic, softmax_rows(): return (probs.astype(jnp.bfloat16), jnp.sum(probs, axis=-1))  4.87 us
    another operation x6, local copies, waits for them, and re-layouts, head_attention(): stacked = jnp.stack([queries, key_rows, value_rows])  4.72 us
  transfers between devices with their start and end apart: 13, of which 10 were waited for; matrix products, arithmetic and copies ran while one was open for 10% of the time, Pallas kernels for 0%

profile of v4, /device:TPU:16, one launch (start us, length us, event | category | flops | bytes accessed | tf_op | source)
XLA Modules:
  0.0 198.9 jit_solution(14990081774400145035)
XLA Ops:
  5.8 3.0 %reshape_reshape.13 = bf16[32,144,128]{2,1,0:T(8,128)(2,1)} reshape(bf16[16,2,3,64,96]{4,3,2,1,0:T(8,128)(2,1)S(1)} %maximum_bitcast_fusion) | data formatting | bytes 2359296 | tf_op jit(solution)/shard_map/reshape;reshape | solution.py:96
  8.7 11.3 %all-to-all-start = ((bf16[32,144,128]{2,1,0:T(8,128)(2,1)}), bf16[32,144,128]{2,1,0:T(8,128)(2,1)S(1)}, u32[]{:S(2)}, u32[]{:S(2)}) async-start(bf16[32,144,128]{2,1,0:T(8,128)(2,1)} %reshape_reshape.13), calls=%async_computation | async-start | bytes 2359296 | tf_op jit(solution)/shard_map/all_to_all | solution.py:97
  22.6 28.8 %all-to-all-done = bf16[32,144,128]{2,1,0:T(8,128)(2,1)S(1)} async-done(((bf16[32,144,128]{2,1,0:T(8,128)(2,1)}), bf16[32,144,128]{2,1,0:T(8,128)(2,1)S(1)}, u32[]{:S(2)}, u32[]{:S(2)}) %all-to-all-start) | async-done | bytes 1179680 | tf_op jit(solution)/shard_map/all_to_all | solution.py:97
  52.6 3.3 %fusion = (f32[2048]{0:T(1024)S(1)}, f32[2048,2048]{0,1:T(8,128)S(1)}) fusion(pred[2048]{0:T(1024)(128)(4,1)S(1)} %iota_compare_fusion.2, bf16[2048,96]{1,0:T(8,128)(2,1)S(1)} %bitcast.66, bf16[2048,96]{1,0:T(8,128)(2,1)S(1)} %bitcast.67), kind=kOutput, calls=%fused_computation.4 | convolution fusion | flops 817887232 | bytes 17573888 | tf_op jit(solution)/shard_map/dot_general | solution.py:86
  55.9 4.9 %fusion.1 = f32[2048]{0:T(1024)S(1)} fusion(f32[2048,2048]{0,1:T(8,128)S(1)} %get-tuple-element.84, f32[2048]{0:T(1024)S(1)} %get-tuple-element.83, pred[2048]{0:T(1024)(128)(4,1)S(1)} %iota_compare_fusion.2), kind=kLoop, calls=%fused_computation.5 | loop fusion | flops 16775168 | bytes 16795648 | tf_op jit(solution)/shard_map/reduce_sum | solution.py:31
  60.8 3.9 %fusion.28 = bf16[2048,96]{0,1:T(8,128)(2,1)S(1)} fusion(bf16[2048,96]{1,0:T(8,128)(2,1)S(1)} %bitcast.68, f32[2048,2048]{0,1:T(8,128)S(1)} %get-tuple-element.84, f32[2048]{0:T(1024)S(1)} %get-tuple-element.83, pred[2048]{0:T(1024)(128)(4,1)S(1)} %iota_compare_fusion.2, f32[2048]{0:T(1024)S(1)} %fusion.1), kind=kOutput, calls=%fused_computation.52 | convolution fusion | flops 822476800 | bytes 17582080 | tf_op jit(solution)/shard_map/dot_general | solution.py:88
  66.4 5.4 %all-to-all-start.1 = ((bf16[32,48,128]{2,1,0:T(8,128)(2,1)}), bf16[32,48,128]{2,1,0:T(8,128)(2,1)S(1)}, u32[]{:S(2)}, u32[]{:S(2)}) async-start(bf16[32,48,128]{2,1,0:T(8,128)(2,1)} %reshape_reshape.14), calls=%async_computation.1 | async-start | bytes 786432 | tf_op jit(solution)/shard_map/all_to_all | solution.py:97
  73.4 12.1 %all-to-all-done.1 = bf16[32,48,128]{2,1,0:T(8,128)(2,1)S(1)} async-done(((bf16[32,48,128]{2,1,0:T(8,128)(2,1)}), bf16[32,48,128]{2,1,0:T(8,128)(2,1)S(1)}, u32[]{:S(2)}, u32[]{:S(2)}) %all-to-all-start.1) | async-done | bytes 393248 | tf_op jit(solution)/shard_map/all_to_all | solution.py:97
  86.8 3.1 %fusion.22 = bf16[1,2,64,1536]{3,2,1,0:T(8,128)(2,1)S(1)} fusion(bf16[2,64,1536]{2,1,0:T(8,128)(2,1)S(1)} %dot_general.19, bf16[1536,1536]{1,0:T(8,128)(2,1)} %param.15, bf16[2,64,1536]{2,1,0:T(8,128)(2,1)S(1)} %copy-done.1, f32[2,64]{1,0:T(2,128)S(1)} %compare_convert_fusion), kind=kOutput, calls=%fused_computation.50 | convolution fusion | flops 604766208 | bytes 5898752 | tf_op jit(solution)/shard_map/dot_general | solution.py:175
  90.7 4.3 %collective-permute-start = (bf16[2,2,15,1536]{3,2,1,0:T(8,128)(2,1)}, bf16[2,2,15,1536]{3,2,1,0:T(8,128)(2,1)S(1)}, u32[]{:S(2)}, u32[]{:S(2)}) collective-permute-start(bf16[2,2,15,1536]{3,2,1,0:T(8,128)(2,1)} %get-tuple-element.79), channel_id=1, source_target_pairs={{0,1},{1,2},{2,3},{3,4},{4,5},{5,6},{6,7},{7,8},{8,9},{9,10},{10,1... | collective-permute-start | bytes 552968 | tf_op jit(solution)/shard_map/ppermute | solution.py:21
  99.7 2.8 %collective-permute-done.1 = bf16[2,2,15,1536]{3,2,1,0:T(8,128)(2,1)S(1)} collective-permute-done((bf16[2,2,15,1536]{3,2,1,0:T(8,128)(2,1)S(1)}, bf16[2,2,15,1536]{3,2,1,0:T(8,128)(2,1)S(1)}, u32[]{:S(2)}, u32[]{:S(2)}) %collective-permute-start.1) | collective-permute-done | bytes 184352 | tf_op jit(solution)/shard_map/ppermute | solution.py:22
  103.0 4.0 %fusion.96 = bf16[2,64,1536]{2,1,0:T(8,128)(2,1)S(1)} fusion(f32[2,94,1536]{2,1,0:T(8,128)S(1)} %get-tuple-element.77, f32[1536]{0:T(1024)S(1)} %get-tuple-element.40, f32[1536]{0:T(1024)S(1)} %get-tuple-element.41, f32[1536]{0:T(1024)S(1)} %get-tuple-element.42, f32[1536]{0:T(1024)S(1)} %get-tuple-element.43, f32[1536]{0:T(1024)S(1)} %get-tuple-element.44, ...), kind=kLoop, calls=%fused_computation.154 | loop fusion | flops 12386304 | bytes 24963584 | tf_op jit(solution)/shard_map/convert_element_type | solution.py:200
  107.5 2.1 %fusion.92 = (f32[1536]{0:T(1024)S(1)}, f32[1536]{0:T(1024)S(1)}, f32[1536]{0:T(1024)S(1)}, f32[1536]{0:T(1024)S(1)}, f32[1536]{0:T(1024)S(1)}, /*index=5*/f32[1...) fusion(bf16[2,64,1536]{2,1,0:T(8,128)(2,1)S(1)} %copy-done, ...), kind=kLoop, calls=%fused_computation.148 | loop fusion | flops 10785792 | bytes 7581696 | tf_op jit(solution)/shard_map/reduce_sum | solution.py:192
  115.4 4.5 %fusion.93 = f32[1536,12,128]{2,0,1:T(8,128)} fusion(bf16[256,12,128]{0,2,1:T(8,128)(2,1)S(1)} %bitcast.65, bf16[2,256,1536]{1,2,0:T(8,128)(2,1)S(1)} %pad_maximum_fusion), kind=kOutput, calls=%fused_computation.150 | convolution fusion | flops 1207959552 | bytes 11010048 | tf_op jit(solution)/shard_map/ncl,nr->crl/dot_general | solution.py:62
  119.9 26.4 %gather_fusion = f32[11796,128]{1,0:T(8,128)} fusion(f32[18432,128]{1,0:T(8,128)} %bitcast.56, s32[12288]{0:T(1024)S(1)} %pad_clamp_fusion), kind=kCustom, calls=%fused_computation | custom fusion | bytes 12126288 | tf_op jit(solution)/shard_map/jit(_take)/gather | solution.py:44
  146.5 10.5 %select_reduce_fusion = f32[11796]{0:T(1024)S(1)} fusion(f32[11796,128]{1,0:T(8,128)} %gather_fusion, s32[11796]{0:T(1024)S(1)} %add_select_fusion.3, pred[11796]{0:T(1024)(128)(4,1)S(1)} %copy-done.38), kind=kLoop, calls=%fused_computation.40 | loop fusion | flops 6027756 | bytes 6145716 | tf_op jit(solution)/shard_map/reduce_sum | solution.py:47
  158.4 2.9 %collective-permute-done.3 = f32[12272]{0:T(1024)S(1)} collective-permute-done((f32[12272]{0:T(1024)S(1)}, f32[12272]{0:T(1024)S(1)}, u32[]{:S(2)}, u32[]{:S(2)}) %collective-permute-start.3) | collective-permute-done | bytes 49120 | tf_op jit(solution)/shard_map/ppermute | solution.py:80
  161.7 5.3 %collective-permute-done.4 = f32[12272]{0:T(1024)S(1)} collective-permute-done((f32[12272]{0:T(1024)S(1)}, f32[12272]{0:T(1024)S(1)}, u32[]{:S(2)}, u32[]{:S(2)}) %collective-permute-start.4) | collective-permute-done | bytes 49120 | tf_op jit(solution)/shard_map/ppermute | solution.py:80
  167.6 3.5 %collective-permute-done.5 = f32[12272]{0:T(1024)S(1)} collective-permute-done((f32[12272]{0:T(1024)S(1)}, f32[12272]{0:T(1024)S(1)}, u32[]{:S(2)}, u32[]{:S(2)}) %collective-permute-start.5) | collective-permute-done | bytes 49120 | tf_op jit(solution)/shard_map/ppermute | solution.py:80
  172.2 4.6 %collective-permute-done.6 = f32[12272]{0:T(1024)S(1)} collective-permute-done((f32[12272]{0:T(1024)S(1)}, f32[12272]{0:T(1024)S(1)}, u32[]{:S(2)}, u32[]{:S(2)}) %collective-permute-start.6) | collective-permute-done | bytes 49120 | tf_op jit(solution)/shard_map/ppermute | solution.py:80
  178.2 6.6 %collective-permute-done.7 = f32[12272]{0:T(1024)S(1)} collective-permute-done((f32[12272]{0:T(1024)S(1)}, f32[12272]{0:T(1024)S(1)}, u32[]{:S(2)}, u32[]{:S(2)}) %collective-permute-start.7) | collective-permute-done | bytes 49120 | tf_op jit(solution)/shard_map/ppermute | solution.py:80
  185.4 3.6 %collective-permute-done.8 = f32[12272]{0:T(1024)S(1)} collective-permute-done((f32[12272]{0:T(1024)S(1)}, f32[12272]{0:T(1024)S(1)}, u32[]{:S(2)}, u32[]{:S(2)}) %collective-permute-start.8) | collective-permute-done | bytes 49120 | tf_op jit(solution)/shard_map/ppermute | solution.py:80
  190.9 3.9 %fusion.61 = bf16[2,64,1536]{2,1,0:T(8,128)(2,1)} fusion(f32[1536]{0:T(1024)S(1)} %get-tuple-element.40, f32[1536]{0:T(1024)S(1)} %get-tuple-element.41, f32[1536]{0:T(1024)S(1)} %get-tuple-element.42, f32[1536]{0:T(1024)S(1)} %get-tuple-element.43, f32[1536]{0:T(1024)S(1)} %get-tuple-element.44, f32[1536]{0:T(1024)S(1)} %get-tuple-element.45, ...), kind=kLoop, calls=%fused_computation.117 | loop fusion | flops 18284544 | bytes 12773376 | tf_op jit(solution)/shard_map/convert_element_type | solution.py:193
  195.1 2.4 %fusion.16 = bf16[2,64,1536]{2,1,0:T(8,128)(2,1)} fusion(bf16[2,64,1536]{2,1,0:T(8,128)(2,1)S(1)} %fusion.96, bf16[1536,1536]{1,0:T(8,128)(2,1)S(1)} %bitcast.58), kind=kOutput, calls=%fused_computation.48 | convolution fusion | flops 604176384 | bytes 5505024 | tf_op jit(solution)/shard_map/dot_general | solution.py:202
  (188 shorter events, 34.0 us)
Async XLA Ops:
  8.7 42.7 %all-to-all-start = ((bf16[32,144,128]{2,1,0:T(8,128)(2,1)}), bf16[32,144,128]{2,1,0:T(8,128)(2,1)S(1)}, u32[]{:S(2)}, u32[]{:S(2)}) async-start(bf16[32,144,128]{2,1,0:T(8,128)(2,1)} %reshape_reshape.13), calls=%async_computation | async-start | bytes 2359296 | tf_op jit(solution)/shard_map/all_to_all | solution.py:97
  21.5 65.3 %copy-start.39 = (f32[2,64]{1,0:T(2,128)}, f32[2,64]{1,0:T(2,128)S(1)}, u32[]{:S(2)}) copy-start(f32[2,64]{1,0:T(2,128)S(1)} %compare_convert_fusion) | copy-start | bytes 1540
  66.4 19.1 %all-to-all-start.1 = ((bf16[32,48,128]{2,1,0:T(8,128)(2,1)}), bf16[32,48,128]{2,1,0:T(8,128)(2,1)S(1)}, u32[]{:S(2)}, u32[]{:S(2)}) async-start(bf16[32,48,128]{2,1,0:T(8,128)(2,1)} %reshape_reshape.14), calls=%async_computation.1 | async-start | bytes 786432 | tf_op jit(solution)/shard_map/all_to_all | solution.py:97
  90.7 9.0 %collective-permute-start = (bf16[2,2,15,1536]{3,2,1,0:T(8,128)(2,1)}, bf16[2,2,15,1536]{3,2,1,0:T(8,128)(2,1)S(1)}, u32[]{:S(2)}, u32[]{:S(2)}) collective-permute-start(bf16[2,2,15,1536]{3,2,1,0:T(8,128)(2,1)} %get-tuple-element.79), channel_id=1, source_target_pairs={{0,1},{1,2},{2,3},{3,4},{4,5},{5,6},{6,7},{7,8},{8,9},{9,10},{10,1... | collective-permute-start | bytes 552968 | tf_op jit(solution)/shard_map/ppermute | solution.py:21
  95.0 7.6 %collective-permute-start.1 = (bf16[2,2,15,1536]{3,2,1,0:T(8,128)(2,1)S(1)}, bf16[2,2,15,1536]{3,2,1,0:T(8,128)(2,1)S(1)}, u32[]{:S(2)}, u32[]{:S(2)}) collective-permute-start(bf16[2,2,15,1536]{3,2,1,0:T(8,128)(2,1)S(1)} %get-tuple-element.80), channel_id=1, source_target_pairs={{1,0},{2,1},{3,2},{4,3},{5,4},{6,5},{7,6},{8,7},{9,8},{10,9},{11,1... | collective-permute-start | bytes 552968 | tf_op jit(solution)/shard_map/ppermute | solution.py:22
  107.4 6.6 %collective-permute-start.2 = (bf16[2,128,1536]{1,2,0:T(8,128)(2,1)S(1)}, bf16[2,128,1536]{1,2,0:T(8,128)(2,1)}, u32[]{:S(2)}, u32[]{:S(2)}) collective-permute-start(bf16[2,128,1536]{1,2,0:T(8,128)(2,1)S(1)} %pad_maximum_fusion.2), channel_id=1, source_target_pairs={{0,32},{32,0},{64,96},{96,64},{128,160},{160,128},{192,224},{224,1... | collective-permute-start | bytes 2359304 | tf_op jit(solution)/shard_map/ppermute | solution.py:57
  146.3 44.4 %copy-start.5 = (f32[1536]{0:T(1024)S(1)}, f32[1536]{0:T(1024)}, u32[]{:S(2)}) copy-start(f32[1536]{0:T(1024)} %copy-done.4) | copy-start | bytes 18436
  146.3 44.4 %copy-start.7 = (f32[1536]{0:T(1024)S(1)}, f32[1536]{0:T(1024)}, u32[]{:S(2)}) copy-start(f32[1536]{0:T(1024)} %copy-done.6) | copy-start | bytes 18436
  146.3 44.4 %copy-start.9 = (f32[1536]{0:T(1024)S(1)}, f32[1536]{0:T(1024)}, u32[]{:S(2)}) copy-start(f32[1536]{0:T(1024)} %copy-done.8) | copy-start | bytes 18436
  146.3 44.4 %copy-start.11 = (f32[1536]{0:T(1024)S(1)}, f32[1536]{0:T(1024)}, u32[]{:S(2)}) copy-start(f32[1536]{0:T(1024)} %copy-done.10) | copy-start | bytes 18436
  146.3 44.4 %copy-start.13 = (f32[1536]{0:T(1024)S(1)}, f32[1536]{0:T(1024)}, u32[]{:S(2)}) copy-start(f32[1536]{0:T(1024)} %copy-done.12) | copy-start | bytes 18436
  146.3 44.4 %copy-start.15 = (f32[1536]{0:T(1024)S(1)}, f32[1536]{0:T(1024)}, u32[]{:S(2)}) copy-start(f32[1536]{0:T(1024)} %copy-done.14) | copy-start | bytes 18436
  146.3 44.4 %copy-start.17 = (f32[1536]{0:T(1024)S(1)}, f32[1536]{0:T(1024)}, u32[]{:S(2)}) copy-start(f32[1536]{0:T(1024)} %get-tuple-element.53) | copy-start | bytes 18436
  146.3 44.4 %copy-start.19 = (f32[1536]{0:T(1024)S(1)}, f32[1536]{0:T(1024)}, u32[]{:S(2)}) copy-start(f32[1536]{0:T(1024)} %get-tuple-element.54) | copy-start | bytes 18436
  146.3 44.4 %copy-start.21 = (f32[1536]{0:T(1024)S(1)}, f32[1536]{0:T(1024)}, u32[]{:S(2)}) copy-start(f32[1536]{0:T(1024)} %get-tuple-element.55) | copy-start | bytes 18436
  146.4 44.4 %copy-start.23 = (f32[1536]{0:T(1024)S(1)}, f32[1536]{0:T(1024)}, u32[]{:S(2)}) copy-start(f32[1536]{0:T(1024)} %get-tuple-element.56) | copy-start | bytes 18436
  157.1 4.2 %collective-permute-start.3 = (f32[12272]{0:T(1024)S(1)}, f32[12272]{0:T(1024)S(1)}, u32[]{:S(2)}, u32[]{:S(2)}) collective-permute-start(f32[12272]{0:T(1024)S(1)} %pad_maximum_fusion.5), channel_id=1, source_target_pairs={{0,64},{32,96},{64,0},{96,32},{128,192},{160,224},{192,128},{224,1... | collective-permute-start | bytes 147272 | tf_op jit(solution)/shard_map/ppermute | solution.py:80
  161.4 5.6 %collective-permute-start.4 = (f32[12272]{0:T(1024)S(1)}, f32[12272]{0:T(1024)S(1)}, u32[]{:S(2)}, u32[]{:S(2)}) collective-permute-start(f32[12272]{0:T(1024)S(1)} %fusion.144), channel_id=1, source_target_pairs={{0,128},{32,160},{64,192},{96,224},{128,0},{160,32},{192,64},{224,... | collective-permute-start | bytes 147272 | tf_op jit(solution)/shard_map/ppermute | solution.py:80
  167.0 4.2 %collective-permute-start.5 = (f32[12272]{0:T(1024)S(1)}, f32[12272]{0:T(1024)S(1)}, u32[]{:S(2)}, u32[]{:S(2)}) collective-permute-start(f32[12272]{0:T(1024)S(1)} %add.345), channel_id=1, source_target_pairs={{0,1},{1,0},{2,3},{3,2},{4,5},{5,4},{6,7},{7,6},{8,9},{9,8},{10,11... | collective-permute-start | bytes 147272 | tf_op jit(solution)/shard_map/ppermute | solution.py:80
  171.2 5.6 %collective-permute-start.6 = (f32[12272]{0:T(1024)S(1)}, f32[12272]{0:T(1024)S(1)}, u32[]{:S(2)}, u32[]{:S(2)}) collective-permute-start(f32[12272]{0:T(1024)S(1)} %add.346), channel_id=1, source_target_pairs={{0,2},{1,3},{2,0},{3,1},{4,6},{5,7},{6,4},{7,5},{8,10},{9,11},{10,... | collective-permute-start | bytes 147272 | tf_op jit(solution)/shard_map/ppermute | solution.py:80
  176.8 8.1 %collective-permute-start.7 = (f32[12272]{0:T(1024)S(1)}, f32[12272]{0:T(1024)S(1)}, u32[]{:S(2)}, u32[]{:S(2)}) collective-permute-start(f32[12272]{0:T(1024)S(1)} %add.347), channel_id=1, source_target_pairs={{0,4},{1,5},{2,6},{3,7},{4,0},{5,1},{6,2},{7,3},{8,12},{9,13},{10,... | collective-permute-start | bytes 147272 | tf_op jit(solution)/shard_map/ppermute | solution.py:80
  184.9 4.2 %collective-permute-start.8 = (f32[12272]{0:T(1024)S(1)}, f32[12272]{0:T(1024)S(1)}, u32[]{:S(2)}, u32[]{:S(2)}) collective-permute-start(f32[12272]{0:T(1024)S(1)} %add.348), channel_id=1, source_target_pairs={{0,8},{1,9},{2,10},{3,11},{4,12},{5,13},{6,14},{7,15},{8,0},{9,1},... | collective-permute-start | bytes 147272 | tf_op jit(solution)/shard_map/ppermute | solution.py:80
  189.1 5.9 %collective-permute-start.9 = (f32[12272]{0:T(1024)S(1)}, f32[12272]{0:T(1024)S(1)}, u32[]{:S(2)}, u32[]{:S(2)}) collective-permute-start(f32[12272]{0:T(1024)S(1)} %add.349), channel_id=1, source_target_pairs={{0,16},{1,17},{2,18},{3,19},{4,20},{5,21},{6,22},{7,23},{8,24},{9,... | collective-permute-start | bytes 147272 | tf_op jit(solution)/shard_map/ppermute | solution.py:80
  195.0 2.5 %collective-permute-start.10 = (f32[12272]{0:T(1024)S(1)}, f32[12272]{0:T(1024)S(1)}, u32[]{:S(2)}, u32[]{:S(2)}) collective-permute-start(f32[12272]{0:T(1024)S(1)} %add.350), channel_id=1, source_target_pairs={{0,32},{32,0},{64,96},{96,64},{128,160},{160,128},{192,224},{224,1... | collective-permute-start | bytes 147272 | tf_op jit(solution)/shard_map/ppermute | solution.py:211
  (34 other events, 799.6 us)

commit v5 on v4

--- a/solution.py
+++ b/solution.py
@@ -44,7 +44,9 @@
     chosen = jnp.take(blocks, block_of, axis=0)
     lane_ids = jnp.arange(blocks.shape[1], dtype=jnp.int32)
     hit = lane_ids[None, :] == lane_of[:, None]
-    return jnp.sum(jnp.where(hit, chosen, jnp.float32(0.0)), axis=1)
+    masked = jnp.where(hit, chosen, jnp.float32(0.0))
+    ones = jnp.ones((blocks.shape[1], blocks.shape[1]), jnp.float32)
+    return jnp.dot(masked, ones, precision=lax.Precision.HIGHEST)[:, 0]
 
 
 def group_picks(context_flat, grad_flat, picks, axis, levels):

time: 201 us -> 204 us (1.015)
  matrix products: 17.2 us -> 30.5 us
  other arithmetic: 35.5 us -> 25.5 us
    dot_general x0 -> x1, matrix products: none -> 13.4 us  [block_entries(): return jnp.dot(masked, ones, precision=lax.Precision.HIGHEST)[:, 0]]
    reduce_sum x1 -> x0, other arithmetic: 10.5 us -> none  [block_entries(): return jnp.sum(jnp.where(hit, chosen, jnp.float32(0.0)), axis=1)]
where the time goes in v5:
time: 204 us; the launch traced here: 202 us
  waiting for transfers between devices  70.3 us (34%)
  local copies, waits for them, and re-layouts  44 us (22%)
  matrix products  30.5 us (15%)
  starting transfers between devices  29.6 us (15%)
  other arithmetic  25.5 us (12%)
    all_to_all x2, waiting for transfers between devices, lane_dense_all_to_all(): return lax.all_to_all(dense, 'seq', 0, 0, tiled=True).reshape(value.shape)  40.3 us
    ppermute x7, waiting for transfers between devices, butterfly_sum(): value = value + lax.ppermute(value, axis, pairs)  26.5 us
    gather x1, local copies, waits for them, and re-layouts, block_entries(): chosen = jnp.take(blocks, block_of, axis=0)  26.4 us
    all_to_all x2, starting transfers between devices, lane_dense_all_to_all(): return lax.all_to_all(dense, 'seq', 0, 0, tiled=True).reshape(value.shape)  16.7 us
    dot_general x1, matrix products, block_entries(): return jnp.dot(masked, ones, precision=lax.Precision.HIGHEST)[:, 0]  13.4 us
    ppermute x7, starting transfers between devices, butterfly_sum(): value = value + lax.ppermute(value, axis, pairs)  7.16 us
    reduce_sum x1, other arithmetic, softmax_rows(): return (probs.astype(jnp.bfloat16), jnp.sum(probs, axis=-1))  4.87 us
    another operation x6, local copies, waits for them, and re-layouts, head_attention(): stacked = jnp.stack([queries, key_rows, value_rows])  4.72 us
  transfers between devices with their start and end apart: 13, of which 10 were waited for; matrix products, arithmetic and copies ran while one was open for 10% of the time, Pallas kernels for 0%

profile of v5, /device:TPU:16, one launch (start us, length us, event | category | flops | bytes accessed | tf_op | source)
XLA Modules:
  0.0 201.6 jit_solution(36063236173209899)
XLA Ops:
  5.8 3.0 %reshape_reshape.13 = bf16[32,144,128]{2,1,0:T(8,128)(2,1)} reshape(bf16[16,2,3,64,96]{4,3,2,1,0:T(8,128)(2,1)S(1)} %maximum_bitcast_fusion) | data formatting | bytes 2359296 | tf_op jit(solution)/shard_map/reshape;reshape | solution.py:98
  8.7 11.3 %all-to-all-start = ((bf16[32,144,128]{2,1,0:T(8,128)(2,1)}), bf16[32,144,128]{2,1,0:T(8,128)(2,1)S(1)}, u32[]{:S(2)}, u32[]{:S(2)}) async-start(bf16[32,144,128]{2,1,0:T(8,128)(2,1)} %reshape_reshape.13), calls=%async_computation | async-start | bytes 2359296 | tf_op jit(solution)/shard_map/all_to_all | solution.py:99
  22.6 28.8 %all-to-all-done = bf16[32,144,128]{2,1,0:T(8,128)(2,1)S(1)} async-done(((bf16[32,144,128]{2,1,0:T(8,128)(2,1)}), bf16[32,144,128]{2,1,0:T(8,128)(2,1)S(1)}, u32[]{:S(2)}, u32[]{:S(2)}) %all-to-all-start) | async-done | bytes 1179680 | tf_op jit(solution)/shard_map/all_to_all | solution.py:99
  52.6 3.3 %fusion = (f32[2048]{0:T(1024)S(1)}, f32[2048,2048]{0,1:T(8,128)S(1)}) fusion(pred[2048]{0:T(1024)(128)(4,1)S(1)} %iota_compare_fusion.3, bf16[2048,96]{1,0:T(8,128)(2,1)S(1)} %bitcast.66, bf16[2048,96]{1,0:T(8,128)(2,1)S(1)} %bitcast.67), kind=kOutput, calls=%fused_computation.4 | convolution fusion | flops 817887232 | bytes 17573888 | tf_op jit(solution)/shard_map/dot_general | solution.py:88
  55.9 4.9 %fusion.1 = f32[2048]{0:T(1024)S(1)} fusion(f32[2048,2048]{0,1:T(8,128)S(1)} %get-tuple-element.84, f32[2048]{0:T(1024)S(1)} %get-tuple-element.83, pred[2048]{0:T(1024)(128)(4,1)S(1)} %iota_compare_fusion.3), kind=kLoop, calls=%fused_computation.5 | loop fusion | flops 16775168 | bytes 16795648 | tf_op jit(solution)/shard_map/reduce_sum | solution.py:31
  60.8 3.9 %fusion.35 = bf16[2048,96]{0,1:T(8,128)(2,1)S(1)} fusion(bf16[2048,96]{1,0:T(8,128)(2,1)S(1)} %bitcast.68, f32[2048,2048]{0,1:T(8,128)S(1)} %get-tuple-element.84, f32[2048]{0:T(1024)S(1)} %get-tuple-element.83, pred[2048]{0:T(1024)(128)(4,1)S(1)} %iota_compare_fusion.3, f32[2048]{0:T(1024)S(1)} %fusion.1), kind=kOutput, calls=%fused_computation.58 | convolution fusion | flops 822476800 | bytes 17582080 | tf_op jit(solution)/shard_map/dot_general | solution.py:90
  66.4 5.4 %all-to-all-start.1 = ((bf16[32,48,128]{2,1,0:T(8,128)(2,1)}), bf16[32,48,128]{2,1,0:T(8,128)(2,1)S(1)}, u32[]{:S(2)}, u32[]{:S(2)}) async-start(bf16[32,48,128]{2,1,0:T(8,128)(2,1)} %reshape_reshape.14), calls=%async_computation.1 | async-start | bytes 786432 | tf_op jit(solution)/shard_map/all_to_all | solution.py:99
  74.1 11.5 %all-to-all-done.1 = bf16[32,48,128]{2,1,0:T(8,128)(2,1)S(1)} async-done(((bf16[32,48,128]{2,1,0:T(8,128)(2,1)}), bf16[32,48,128]{2,1,0:T(8,128)(2,1)S(1)}, u32[]{:S(2)}, u32[]{:S(2)}) %all-to-all-start.1) | async-done | bytes 393248 | tf_op jit(solution)/shard_map/all_to_all | solution.py:99
  86.8 3.1 %fusion.29 = bf16[1,2,64,1536]{3,2,1,0:T(8,128)(2,1)S(1)} fusion(bf16[2,64,1536]{2,1,0:T(8,128)(2,1)S(1)} %dot_general.22, bf16[1536,1536]{1,0:T(8,128)(2,1)} %param.15, bf16[2,64,1536]{2,1,0:T(8,128)(2,1)S(1)} %copy-done.1, f32[2,64]{1,0:T(2,128)S(1)} %compare_convert_fusion), kind=kOutput, calls=%fused_computation.56 | convolution fusion | flops 604766208 | bytes 5898752 | tf_op jit(solution)/shard_map/dot_general | solution.py:177
  90.7 4.3 %collective-permute-start = (bf16[2,2,15,1536]{3,2,1,0:T(8,128)(2,1)}, bf16[2,2,15,1536]{3,2,1,0:T(8,128)(2,1)S(1)}, u32[]{:S(2)}, u32[]{:S(2)}) collective-permute-start(bf16[2,2,15,1536]{3,2,1,0:T(8,128)(2,1)} %get-tuple-element.79), channel_id=1, source_target_pairs={{0,1},{1,2},{2,3},{3,4},{4,5},{5,6},{6,7},{7,8},{8,9},{9,10},{10,1... | collective-permute-start | bytes 552968 | tf_op jit(solution)/shard_map/ppermute | solution.py:21
  99.1 3.5 %collective-permute-done.1 = bf16[2,2,15,1536]{3,2,1,0:T(8,128)(2,1)S(1)} collective-permute-done((bf16[2,2,15,1536]{3,2,1,0:T(8,128)(2,1)S(1)}, bf16[2,2,15,1536]{3,2,1,0:T(8,128)(2,1)S(1)}, u32[]{:S(2)}, u32[]{:S(2)}) %collective-permute-start.1) | collective-permute-done | bytes 184352 | tf_op jit(solution)/shard_map/ppermute | solution.py:22
  103.0 4.0 %fusion.106 = bf16[2,64,1536]{2,1,0:T(8,128)(2,1)S(1)} fusion(f32[2,94,1536]{2,1,0:T(8,128)S(1)} %get-tuple-element.77, f32[1536]{0:T(1024)S(1)} %get-tuple-element.40, f32[1536]{0:T(1024)S(1)} %get-tuple-element.41, f32[1536]{0:T(1024)S(1)} %get-tuple-element.42, f32[1536]{0:T(1024)S(1)} %get-tuple-element.43, f32[1536]{0:T(1024)S(1)} %get-tuple-element.44, ...), kind=kLoop, calls=%fused_computation.161 | loop fusion | flops 12386304 | bytes 24963584 | tf_op jit(solution)/shard_map/convert_element_type | solution.py:202
  107.4 2.1 %fusion.102 = (f32[1536]{0:T(1024)S(1)}, f32[1536]{0:T(1024)S(1)}, f32[1536]{0:T(1024)S(1)}, f32[1536]{0:T(1024)S(1)}, f32[1536]{0:T(1024)S(1)}, /*index=5*/f32[...) fusion(bf16[2,64,1536]{2,1,0:T(8,128)(2,1)S(1)} %copy-done, ...), kind=kLoop, calls=%fused_computation.155 | loop fusion | flops 10785792 | bytes 7581696 | tf_op jit(solution)/shard_map/reduce_sum | solution.py:194
  115.3 4.5 %fusion.103 = f32[1536,12,128]{2,0,1:T(8,128)} fusion(bf16[256,12,128]{0,2,1:T(8,128)(2,1)S(1)} %bitcast.65, bf16[2,256,1536]{1,2,0:T(8,128)(2,1)S(1)} %pad_maximum_fusion), kind=kOutput, calls=%fused_computation.157 | convolution fusion | flops 1207959552 | bytes 11010048 | tf_op jit(solution)/shard_map/ncl,nr->crl/dot_general | solution.py:64
  119.8 26.4 %gather_fusion = f32[11796,128]{1,0:T(8,128)} fusion(f32[18432,128]{1,0:T(8,128)} %bitcast.56, s32[12288]{0:T(1024)S(1)} %pad_clamp_fusion), kind=kCustom, calls=%fused_computation | custom fusion | bytes 12126288 | tf_op jit(solution)/shard_map/jit(_take)/gather | solution.py:44
  146.4 13.4 %fusion.38 = f32[11796]{0:T(1024)S(1)} fusion(f32[11796,128]{1,0:T(8,128)} %gather_fusion, s32[11796]{0:T(1024)S(1)} %copy-done.27, pred[11796]{0:T(1024)(128)(4,1)S(1)} %copy-done.28), kind=kOutput, calls=%fused_computation.62 | convolution fusion | flops 22648320 | bytes 6145716 | tf_op jit(solution)/shard_map/dot_general | solution.py:49
  161.1 2.8 %collective-permute-done.3 = f32[12272]{0:T(1024)S(1)} collective-permute-done((f32[12272]{0:T(1024)S(1)}, f32[12272]{0:T(1024)S(1)}, u32[]{:S(2)}, u32[]{:S(2)}) %collective-permute-start.3) | collective-permute-done | bytes 49120 | tf_op jit(solution)/shard_map/ppermute | solution.py:82
  164.4 5.3 %collective-permute-done.4 = f32[12272]{0:T(1024)S(1)} collective-permute-done((f32[12272]{0:T(1024)S(1)}, f32[12272]{0:T(1024)S(1)}, u32[]{:S(2)}, u32[]{:S(2)}) %collective-permute-start.4) | collective-permute-done | bytes 49120 | tf_op jit(solution)/shard_map/ppermute | solution.py:82
  170.3 3.5 %collective-permute-done.5 = f32[12272]{0:T(1024)S(1)} collective-permute-done((f32[12272]{0:T(1024)S(1)}, f32[12272]{0:T(1024)S(1)}, u32[]{:S(2)}, u32[]{:S(2)}) %collective-permute-start.5) | collective-permute-done | bytes 49120 | tf_op jit(solution)/shard_map/ppermute | solution.py:82
  174.9 4.6 %collective-permute-done.6 = f32[12272]{0:T(1024)S(1)} collective-permute-done((f32[12272]{0:T(1024)S(1)}, f32[12272]{0:T(1024)S(1)}, u32[]{:S(2)}, u32[]{:S(2)}) %collective-permute-start.6) | collective-permute-done | bytes 49120 | tf_op jit(solution)/shard_map/ppermute | solution.py:82
  180.9 6.6 %collective-permute-done.7 = f32[12272]{0:T(1024)S(1)} collective-permute-done((f32[12272]{0:T(1024)S(1)}, f32[12272]{0:T(1024)S(1)}, u32[]{:S(2)}, u32[]{:S(2)}) %collective-permute-start.7) | collective-permute-done | bytes 49120 | tf_op jit(solution)/shard_map/ppermute | solution.py:82
  188.1 3.6 %collective-permute-done.8 = f32[12272]{0:T(1024)S(1)} collective-permute-done((f32[12272]{0:T(1024)S(1)}, f32[12272]{0:T(1024)S(1)}, u32[]{:S(2)}, u32[]{:S(2)}) %collective-permute-start.8) | collective-permute-done | bytes 49120 | tf_op jit(solution)/shard_map/ppermute | solution.py:82
  193.7 3.9 %fusion.71 = bf16[2,64,1536]{2,1,0:T(8,128)(2,1)} fusion(f32[1536]{0:T(1024)S(1)} %get-tuple-element.40, f32[1536]{0:T(1024)S(1)} %get-tuple-element.41, f32[1536]{0:T(1024)S(1)} %get-tuple-element.42, f32[1536]{0:T(1024)S(1)} %get-tuple-element.43, f32[1536]{0:T(1024)S(1)} %get-tuple-element.44, f32[1536]{0:T(1024)S(1)} %get-tuple-element.45, ...), kind=kLoop, calls=%fused_computation.124 | loop fusion | flops 18284544 | bytes 12773376 | tf_op jit(solution)/shard_map/convert_element_type | solution.py:195
  197.8 2.4 %fusion.23 = bf16[2,64,1536]{2,1,0:T(8,128)(2,1)} fusion(bf16[2,64,1536]{2,1,0:T(8,128)(2,1)S(1)} %fusion.106, bf16[1536,1536]{1,0:T(8,128)(2,1)S(1)} %bitcast.58), kind=kOutput, calls=%fused_computation.54 | convolution fusion | flops 604176384 | bytes 5505024 | tf_op jit(solution)/shard_map/dot_general | solution.py:204
  (168 shorter events, 34.1 us)
Async XLA Ops:
  8.7 42.7 %all-to-all-start = ((bf16[32,144,128]{2,1,0:T(8,128)(2,1)}), bf16[32,144,128]{2,1,0:T(8,128)(2,1)S(1)}, u32[]{:S(2)}, u32[]{:S(2)}) async-start(bf16[32,144,128]{2,1,0:T(8,128)(2,1)} %reshape_reshape.13), calls=%async_computation | async-start | bytes 2359296 | tf_op jit(solution)/shard_map/all_to_all | solution.py:99
  21.5 65.3 %copy-start.29 = (f32[2,64]{1,0:T(2,128)}, f32[2,64]{1,0:T(2,128)S(1)}, u32[]{:S(2)}) copy-start(f32[2,64]{1,0:T(2,128)S(1)} %compare_convert_fusion) | copy-start | bytes 1540
  66.4 19.1 %all-to-all-start.1 = ((bf16[32,48,128]{2,1,0:T(8,128)(2,1)}), bf16[32,48,128]{2,1,0:T(8,128)(2,1)S(1)}, u32[]{:S(2)}, u32[]{:S(2)}) async-start(bf16[32,48,128]{2,1,0:T(8,128)(2,1)} %reshape_reshape.14), calls=%async_computation.1 | async-start | bytes 786432 | tf_op jit(solution)/shard_map/all_to_all | solution.py:99
  90.7 8.4 %collective-permute-start = (bf16[2,2,15,1536]{3,2,1,0:T(8,128)(2,1)}, bf16[2,2,15,1536]{3,2,1,0:T(8,128)(2,1)S(1)}, u32[]{:S(2)}, u32[]{:S(2)}) collective-permute-start(bf16[2,2,15,1536]{3,2,1,0:T(8,128)(2,1)} %get-tuple-element.79), channel_id=1, source_target_pairs={{0,1},{1,2},{2,3},{3,4},{4,5},{5,6},{6,7},{7,8},{8,9},{9,10},{10,1... | collective-permute-start | bytes 552968 | tf_op jit(solution)/shard_map/ppermute | solution.py:21
  95.0 7.6 %collective-permute-start.1 = (bf16[2,2,15,1536]{3,2,1,0:T(8,128)(2,1)S(1)}, bf16[2,2,15,1536]{3,2,1,0:T(8,128)(2,1)S(1)}, u32[]{:S(2)}, u32[]{:S(2)}) collective-permute-start(bf16[2,2,15,1536]{3,2,1,0:T(8,128)(2,1)S(1)} %get-tuple-element.80), channel_id=1, source_target_pairs={{1,0},{2,1},{3,2},{4,3},{5,4},{6,5},{7,6},{8,7},{9,8},{10,9},{11,1... | collective-permute-start | bytes 552968 | tf_op jit(solution)/shard_map/ppermute | solution.py:22
  107.3 6.6 %collective-permute-start.2 = (bf16[2,128,1536]{1,2,0:T(8,128)(2,1)S(1)}, bf16[2,128,1536]{1,2,0:T(8,128)(2,1)}, u32[]{:S(2)}, u32[]{:S(2)}) collective-permute-start(bf16[2,128,1536]{1,2,0:T(8,128)(2,1)S(1)} %pad_maximum_fusion.2), channel_id=1, source_target_pairs={{0,32},{32,0},{64,96},{96,64},{128,160},{160,128},{192,224},{224,1... | collective-permute-start | bytes 2359304 | tf_op jit(solution)/shard_map/ppermute | solution.py:59
  146.2 47.3 %copy-start.11 = (f32[1536]{0:T(1024)S(1)}, f32[1536]{0:T(1024)}, u32[]{:S(2)}) copy-start(f32[1536]{0:T(1024)} %copy-done.10) | copy-start | bytes 18436
  146.2 47.3 %copy-start.13 = (f32[1536]{0:T(1024)S(1)}, f32[1536]{0:T(1024)}, u32[]{:S(2)}) copy-start(f32[1536]{0:T(1024)} %copy-done.12) | copy-start | bytes 18436
  146.2 47.3 %copy-start.15 = (f32[1536]{0:T(1024)S(1)}, f32[1536]{0:T(1024)}, u32[]{:S(2)}) copy-start(f32[1536]{0:T(1024)} %copy-done.14) | copy-start | bytes 18436
  146.2 47.3 %copy-start.16 = (f32[1536]{0:T(1024)S(1)}, f32[1536]{0:T(1024)}, u32[]{:S(2)}) copy-start(f32[1536]{0:T(1024)} %get-tuple-element.59) | copy-start | bytes 18436
  146.3 47.3 %copy-start.17 = (f32[1536]{0:T(1024)S(1)}, f32[1536]{0:T(1024)}, u32[]{:S(2)}) copy-start(f32[1536]{0:T(1024)} %get-tuple-element.60) | copy-start | bytes 18436
  146.3 47.3 %copy-start.18 = (f32[1536]{0:T(1024)S(1)}, f32[1536]{0:T(1024)}, u32[]{:S(2)}) copy-start(f32[1536]{0:T(1024)} %get-tuple-element.61) | copy-start | bytes 18436
  146.3 47.3 %copy-start.19 = (f32[1536]{0:T(1024)S(1)}, f32[1536]{0:T(1024)}, u32[]{:S(2)}) copy-start(f32[1536]{0:T(1024)} %get-tuple-element.62) | copy-start | bytes 18436
  146.3 47.3 %copy-start.20 = (f32[1536]{0:T(1024)S(1)}, f32[1536]{0:T(1024)}, u32[]{:S(2)}) copy-start(f32[1536]{0:T(1024)} %get-tuple-element.63) | copy-start | bytes 18436
  146.3 47.3 %copy-start.21 = (f32[1536]{0:T(1024)S(1)}, f32[1536]{0:T(1024)}, u32[]{:S(2)}) copy-start(f32[1536]{0:T(1024)} %get-tuple-element.64) | copy-start | bytes 18436
  146.3 47.3 %copy-start.22 = (f32[1536]{0:T(1024)S(1)}, f32[1536]{0:T(1024)}, u32[]{:S(2)}) copy-start(f32[1536]{0:T(1024)} %get-tuple-element.65) | copy-start | bytes 18436
  159.8 4.2 %collective-permute-start.3 = (f32[12272]{0:T(1024)S(1)}, f32[12272]{0:T(1024)S(1)}, u32[]{:S(2)}, u32[]{:S(2)}) collective-permute-start(f32[12272]{0:T(1024)S(1)} %pad_maximum_fusion.5), channel_id=1, source_target_pairs={{0,64},{32,96},{64,0},{96,32},{128,192},{160,224},{192,128},{224,1... | collective-permute-start | bytes 147272 | tf_op jit(solution)/shard_map/ppermute | solution.py:82
  164.1 5.6 %collective-permute-start.4 = (f32[12272]{0:T(1024)S(1)}, f32[12272]{0:T(1024)S(1)}, u32[]{:S(2)}, u32[]{:S(2)}) collective-permute-start(f32[12272]{0:T(1024)S(1)} %fusion.158), channel_id=1, source_target_pairs={{0,128},{32,160},{64,192},{96,224},{128,0},{160,32},{192,64},{224,... | collective-permute-start | bytes 147272 | tf_op jit(solution)/shard_map/ppermute | solution.py:82
  169.7 4.2 %collective-permute-start.5 = (f32[12272]{0:T(1024)S(1)}, f32[12272]{0:T(1024)S(1)}, u32[]{:S(2)}, u32[]{:S(2)}) collective-permute-start(f32[12272]{0:T(1024)S(1)} %add.345), channel_id=1, source_target_pairs={{0,1},{1,0},{2,3},{3,2},{4,5},{5,4},{6,7},{7,6},{8,9},{9,8},{10,11... | collective-permute-start | bytes 147272 | tf_op jit(solution)/shard_map/ppermute | solution.py:82
  173.9 5.6 %collective-permute-start.6 = (f32[12272]{0:T(1024)S(1)}, f32[12272]{0:T(1024)S(1)}, u32[]{:S(2)}, u32[]{:S(2)}) collective-permute-start(f32[12272]{0:T(1024)S(1)} %add.346), channel_id=1, source_target_pairs={{0,2},{1,3},{2,0},{3,1},{4,6},{5,7},{6,4},{7,5},{8,10},{9,11},{10,... | collective-permute-start | bytes 147272 | tf_op jit(solution)/shard_map/ppermute | solution.py:82
  179.5 8.1 %collective-permute-start.7 = (f32[12272]{0:T(1024)S(1)}, f32[12272]{0:T(1024)S(1)}, u32[]{:S(2)}, u32[]{:S(2)}) collective-permute-start(f32[12272]{0:T(1024)S(1)} %add.347), channel_id=1, source_target_pairs={{0,4},{1,5},{2,6},{3,7},{4,0},{5,1},{6,2},{7,3},{8,12},{9,13},{10,... | collective-permute-start | bytes 147272 | tf_op jit(solution)/shard_map/ppermute | solution.py:82
  187.6 4.2 %collective-permute-start.8 = (f32[12272]{0:T(1024)S(1)}, f32[12272]{0:T(1024)S(1)}, u32[]{:S(2)}, u32[]{:S(2)}) collective-permute-start(f32[12272]{0:T(1024)S(1)} %add.348), channel_id=1, source_target_pairs={{0,8},{1,9},{2,10},{3,11},{4,12},{5,13},{6,14},{7,15},{8,0},{9,1},... | collective-permute-start | bytes 147272 | tf_op jit(solution)/shard_map/ppermute | solution.py:82
  191.8 5.9 %collective-permute-start.9 = (f32[12272]{0:T(1024)S(1)}, f32[12272]{0:T(1024)S(1)}, u32[]{:S(2)}, u32[]{:S(2)}) collective-permute-start(f32[12272]{0:T(1024)S(1)} %add.349), channel_id=1, source_target_pairs={{0,16},{1,17},{2,18},{3,19},{4,20},{5,21},{6,22},{7,23},{8,24},{9,... | collective-permute-start | bytes 147272 | tf_op jit(solution)/shard_map/ppermute | solution.py:82
  197.7 2.5 %collective-permute-start.10 = (f32[12272]{0:T(1024)S(1)}, f32[12272]{0:T(1024)S(1)}, u32[]{:S(2)}, u32[]{:S(2)}) collective-permute-start(f32[12272]{0:T(1024)S(1)} %add.350), channel_id=1, source_target_pairs={{0,32},{32,0},{64,96},{96,64},{128,160},{160,128},{192,224},{224,1... | collective-permute-start | bytes 147272 | tf_op jit(solution)/shard_map/ppermute | solution.py:213
  (24 other events, 577.5 us)

commit v6 on v4

--- a/solution.py
+++ b/solution.py
@@ -206,7 +206,7 @@
     weight_half, member = group_picks(context_flat, grad_flat, pick_weight, "dp", 1)
     kernel_vals = pick_entries(kernel_grad, pick_kernel)
     half_count = weight_half.shape[0]
-    joined = butterfly_sum(jnp.concatenate([weight_half, kernel_vals]), ("dp", "seq"), {"dp": 2})
+    joined = butterfly_sum(jnp.concatenate([weight_half, kernel_vals]), ("seq", "dp"), {"dp": 2})
     dp_count = lax.axis_size("dp")
     other = lax.ppermute(joined, "dp", [(i, i ^ 1) for i in range(dp_count)])
     low, high = jnp.where(member == 0, joined, other), jnp.where(member == 0, other, joined)

time: 201 us -> 203 us (level)
  no operation moved by 1% of the time
where the time goes in v6:
time: 203 us; the launch traced here: 199 us
  waiting for transfers between devices  69.9 us (34%)
  local copies, waits for them, and re-layouts  44.6 us (22%)
  other arithmetic  35.5 us (17%)
  starting transfers between devices  30.2 us (15%)
  matrix products  17.2 us (8%)
    all_to_all x2, waiting for transfers between devices, lane_dense_all_to_all(): return lax.all_to_all(dense, 'seq', 0, 0, tiled=True).reshape(value.shape)  40.9 us
    gather x1, local copies, waits for them, and re-layouts, block_entries(): chosen = jnp.take(blocks, block_of, axis=0)  26.4 us
    ppermute x7, waiting for transfers between devices, butterfly_sum(): value = value + lax.ppermute(value, axis, pairs)  26.2 us
    all_to_all x2, starting transfers between devices, lane_dense_all_to_all(): return lax.all_to_all(dense, 'seq', 0, 0, tiled=True).reshape(value.shape)  16.7 us
    reduce_sum x1, other arithmetic, block_entries(): return jnp.sum(jnp.where(hit, chosen, jnp.float32(0.0)), axis=1)  10.5 us
    ppermute x7, starting transfers between devices, butterfly_sum(): value = value + lax.ppermute(value, axis, pairs)  7.79 us
    reduce_sum x1, other arithmetic, softmax_rows(): return (probs.astype(jnp.bfloat16), jnp.sum(probs, axis=-1))  4.87 us
    another operation x6, local copies, waits for them, and re-layouts, head_attention(): stacked = jnp.stack([queries, key_rows, value_rows])  4.72 us
  transfers between devices with their start and end apart: 13, of which 10 were waited for; matrix products, arithmetic and copies ran while one was open for 10% of the time, Pallas kernels for 0%

profile of v6, /device:TPU:16, one launch (start us, length us, event | category | flops | bytes accessed | tf_op | source)
XLA Modules:
  0.0 199.2 jit_solution(12075145673083043406)
XLA Ops:
  5.8 3.0 %reshape_reshape.13 = bf16[32,144,128]{2,1,0:T(8,128)(2,1)} reshape(bf16[16,2,3,64,96]{4,3,2,1,0:T(8,128)(2,1)S(1)} %maximum_bitcast_fusion) | data formatting | bytes 2359296 | tf_op jit(solution)/shard_map/reshape;reshape | solution.py:96
  8.7 11.3 %all-to-all-start = ((bf16[32,144,128]{2,1,0:T(8,128)(2,1)}), bf16[32,144,128]{2,1,0:T(8,128)(2,1)S(1)}, u32[]{:S(2)}, u32[]{:S(2)}) async-start(bf16[32,144,128]{2,1,0:T(8,128)(2,1)} %reshape_reshape.13), calls=%async_computation | async-start | bytes 2359296 | tf_op jit(solution)/shard_map/all_to_all | solution.py:97
  22.6 28.8 %all-to-all-done = bf16[32,144,128]{2,1,0:T(8,128)(2,1)S(1)} async-done(((bf16[32,144,128]{2,1,0:T(8,128)(2,1)}), bf16[32,144,128]{2,1,0:T(8,128)(2,1)S(1)}, u32[]{:S(2)}, u32[]{:S(2)}) %all-to-all-start) | async-done | bytes 1179680 | tf_op jit(solution)/shard_map/all_to_all | solution.py:97
  52.6 3.3 %fusion = (f32[2048]{0:T(1024)S(1)}, f32[2048,2048]{0,1:T(8,128)S(1)}) fusion(pred[2048]{0:T(1024)(128)(4,1)S(1)} %iota_compare_fusion.2, bf16[2048,96]{1,0:T(8,128)(2,1)S(1)} %bitcast.66, bf16[2048,96]{1,0:T(8,128)(2,1)S(1)} %bitcast.67), kind=kOutput, calls=%fused_computation.4 | convolution fusion | flops 817887232 | bytes 17573888 | tf_op jit(solution)/shard_map/dot_general | solution.py:86
  55.9 4.9 %fusion.1 = f32[2048]{0:T(1024)S(1)} fusion(f32[2048,2048]{0,1:T(8,128)S(1)} %get-tuple-element.84, f32[2048]{0:T(1024)S(1)} %get-tuple-element.83, pred[2048]{0:T(1024)(128)(4,1)S(1)} %iota_compare_fusion.2), kind=kLoop, calls=%fused_computation.5 | loop fusion | flops 16775168 | bytes 16795648 | tf_op jit(solution)/shard_map/reduce_sum | solution.py:31
  60.8 3.9 %fusion.28 = bf16[2048,96]{0,1:T(8,128)(2,1)S(1)} fusion(bf16[2048,96]{1,0:T(8,128)(2,1)S(1)} %bitcast.68, f32[2048,2048]{0,1:T(8,128)S(1)} %get-tuple-element.84, f32[2048]{0:T(1024)S(1)} %get-tuple-element.83, pred[2048]{0:T(1024)(128)(4,1)S(1)} %iota_compare_fusion.2, f32[2048]{0:T(1024)S(1)} %fusion.1), kind=kOutput, calls=%fused_computation.52 | convolution fusion | flops 822476800 | bytes 17582080 | tf_op jit(solution)/shard_map/dot_general | solution.py:88
  66.4 5.4 %all-to-all-start.1 = ((bf16[32,48,128]{2,1,0:T(8,128)(2,1)}), bf16[32,48,128]{2,1,0:T(8,128)(2,1)S(1)}, u32[]{:S(2)}, u32[]{:S(2)}) async-start(bf16[32,48,128]{2,1,0:T(8,128)(2,1)} %reshape_reshape.14), calls=%async_computation.1 | async-start | bytes 786432 | tf_op jit(solution)/shard_map/all_to_all | solution.py:97
  73.4 12.1 %all-to-all-done.1 = bf16[32,48,128]{2,1,0:T(8,128)(2,1)S(1)} async-done(((bf16[32,48,128]{2,1,0:T(8,128)(2,1)}), bf16[32,48,128]{2,1,0:T(8,128)(2,1)S(1)}, u32[]{:S(2)}, u32[]{:S(2)}) %all-to-all-start.1) | async-done | bytes 393248 | tf_op jit(solution)/shard_map/all_to_all | solution.py:97
  86.8 3.1 %fusion.22 = bf16[1,2,64,1536]{3,2,1,0:T(8,128)(2,1)S(1)} fusion(bf16[2,64,1536]{2,1,0:T(8,128)(2,1)S(1)} %dot_general.19, bf16[1536,1536]{1,0:T(8,128)(2,1)} %param.15, bf16[2,64,1536]{2,1,0:T(8,128)(2,1)S(1)} %copy-done.1, f32[2,64]{1,0:T(2,128)S(1)} %compare_convert_fusion), kind=kOutput, calls=%fused_computation.50 | convolution fusion | flops 604766208 | bytes 5898752 | tf_op jit(solution)/shard_map/dot_general | solution.py:175
  90.7 4.3 %collective-permute-start = (bf16[2,2,15,1536]{3,2,1,0:T(8,128)(2,1)}, bf16[2,2,15,1536]{3,2,1,0:T(8,128)(2,1)S(1)}, u32[]{:S(2)}, u32[]{:S(2)}) collective-permute-start(bf16[2,2,15,1536]{3,2,1,0:T(8,128)(2,1)} %get-tuple-element.79), channel_id=1, source_target_pairs={{0,1},{1,2},{2,3},{3,4},{4,5},{5,6},{6,7},{7,8},{8,9},{9,10},{10,1... | collective-permute-start | bytes 552968 | tf_op jit(solution)/shard_map/ppermute | solution.py:21
  99.7 2.8 %collective-permute-done.1 = bf16[2,2,15,1536]{3,2,1,0:T(8,128)(2,1)S(1)} collective-permute-done((bf16[2,2,15,1536]{3,2,1,0:T(8,128)(2,1)S(1)}, bf16[2,2,15,1536]{3,2,1,0:T(8,128)(2,1)S(1)}, u32[]{:S(2)}, u32[]{:S(2)}) %collective-permute-start.1) | collective-permute-done | bytes 184352 | tf_op jit(solution)/shard_map/ppermute | solution.py:22
  103.0 4.0 %fusion.96 = bf16[2,64,1536]{2,1,0:T(8,128)(2,1)S(1)} fusion(f32[2,94,1536]{2,1,0:T(8,128)S(1)} %get-tuple-element.77, f32[1536]{0:T(1024)S(1)} %get-tuple-element.40, f32[1536]{0:T(1024)S(1)} %get-tuple-element.41, f32[1536]{0:T(1024)S(1)} %get-tuple-element.42, f32[1536]{0:T(1024)S(1)} %get-tuple-element.43, f32[1536]{0:T(1024)S(1)} %get-tuple-element.44, ...), kind=kLoop, calls=%fused_computation.154 | loop fusion | flops 12386304 | bytes 24963584 | tf_op jit(solution)/shard_map/convert_element_type | solution.py:200
  115.4 4.5 %fusion.93 = f32[1536,12,128]{2,0,1:T(8,128)} fusion(bf16[256,12,128]{0,2,1:T(8,128)(2,1)S(1)} %bitcast.65, bf16[2,256,1536]{1,2,0:T(8,128)(2,1)S(1)} %pad_maximum_fusion), kind=kOutput, calls=%fused_computation.150 | convolution fusion | flops 1207959552 | bytes 11010048 | tf_op jit(solution)/shard_map/ncl,nr->crl/dot_general | solution.py:62
  119.9 26.4 %gather_fusion = f32[11796,128]{1,0:T(8,128)} fusion(f32[18432,128]{1,0:T(8,128)} %bitcast.56, s32[12288]{0:T(1024)S(1)} %pad_clamp_fusion), kind=kCustom, calls=%fused_computation | custom fusion | bytes 12126288 | tf_op jit(solution)/shard_map/jit(_take)/gather | solution.py:44
  146.5 10.5 %select_reduce_fusion = f32[11796]{0:T(1024)S(1)} fusion(f32[11796,128]{1,0:T(8,128)} %gather_fusion, s32[11796]{0:T(1024)S(1)} %add_select_fusion.3, pred[11796]{0:T(1024)(128)(4,1)S(1)} %copy-done.38), kind=kLoop, calls=%fused_computation.40 | loop fusion | flops 6027756 | bytes 6145716 | tf_op jit(solution)/shard_map/reduce_sum | solution.py:47
  157.7 3.6 %collective-permute-done.3 = f32[12272]{0:T(1024)S(1)} collective-permute-done((f32[12272]{0:T(1024)S(1)}, f32[12272]{0:T(1024)S(1)}, u32[]{:S(2)}, u32[]{:S(2)}) %collective-permute-start.3) | collective-permute-done | bytes 49120 | tf_op jit(solution)/shard_map/ppermute | solution.py:80
  162.3 4.6 %collective-permute-done.4 = f32[12272]{0:T(1024)S(1)} collective-permute-done((f32[12272]{0:T(1024)S(1)}, f32[12272]{0:T(1024)S(1)}, u32[]{:S(2)}, u32[]{:S(2)}) %collective-permute-start.4) | collective-permute-done | bytes 49120 | tf_op jit(solution)/shard_map/ppermute | solution.py:80
  166.9 2.3 %collective-permute-start.5 = (f32[12272]{0:T(1024)S(1)}, f32[12272]{0:T(1024)S(1)}, u32[]{:S(2)}, u32[]{:S(2)}) collective-permute-start(f32[12272]{0:T(1024)S(1)} %add.345), channel_id=1, source_target_pairs={{0,4},{1,5},{2,6},{3,7},{4,0},{5,1},{6,2},{7,3},{8,12},{9,13},{10,... | collective-permute-start | bytes 147272 | tf_op jit(solution)/shard_map/ppermute | solution.py:80
  169.2 6.0 %collective-permute-done.5 = f32[12272]{0:T(1024)S(1)} collective-permute-done((f32[12272]{0:T(1024)S(1)}, f32[12272]{0:T(1024)S(1)}, u32[]{:S(2)}, u32[]{:S(2)}) %collective-permute-start.5) | collective-permute-done | bytes 49120 | tf_op jit(solution)/shard_map/ppermute | solution.py:80
  176.1 3.4 %collective-permute-done.6 = f32[12272]{0:T(1024)S(1)} collective-permute-done((f32[12272]{0:T(1024)S(1)}, f32[12272]{0:T(1024)S(1)}, u32[]{:S(2)}, u32[]{:S(2)}) %collective-permute-start.6) | collective-permute-done | bytes 49120 | tf_op jit(solution)/shard_map/ppermute | solution.py:80
  180.6 4.6 %collective-permute-done.7 = f32[12272]{0:T(1024)S(1)} collective-permute-done((f32[12272]{0:T(1024)S(1)}, f32[12272]{0:T(1024)S(1)}, u32[]{:S(2)}, u32[]{:S(2)}) %collective-permute-start.7) | collective-permute-done | bytes 49120 | tf_op jit(solution)/shard_map/ppermute | solution.py:80
  186.6 2.8 %collective-permute-done.8 = f32[12272]{0:T(1024)S(1)} collective-permute-done((f32[12272]{0:T(1024)S(1)}, f32[12272]{0:T(1024)S(1)}, u32[]{:S(2)}, u32[]{:S(2)}) %collective-permute-start.8) | collective-permute-done | bytes 49120 | tf_op jit(solution)/shard_map/ppermute | solution.py:80
  190.2 3.9 %fusion.61 = bf16[2,64,1536]{2,1,0:T(8,128)(2,1)} fusion(f32[1536]{0:T(1024)S(1)} %get-tuple-element.40, f32[1536]{0:T(1024)S(1)} %get-tuple-element.41, f32[1536]{0:T(1024)S(1)} %get-tuple-element.42, f32[1536]{0:T(1024)S(1)} %get-tuple-element.43, f32[1536]{0:T(1024)S(1)} %get-tuple-element.44, f32[1536]{0:T(1024)S(1)} %get-tuple-element.45, ...), kind=kLoop, calls=%fused_computation.117 | loop fusion | flops 18284544 | bytes 12773376 | tf_op jit(solution)/shard_map/convert_element_type | solution.py:193
  195.4 2.4 %fusion.16 = bf16[2,64,1536]{2,1,0:T(8,128)(2,1)} fusion(bf16[2,64,1536]{2,1,0:T(8,128)(2,1)S(1)} %fusion.96, bf16[1536,1536]{1,0:T(8,128)(2,1)S(1)} %bitcast.58), kind=kOutput, calls=%fused_computation.48 | convolution fusion | flops 604176384 | bytes 5505024 | tf_op jit(solution)/shard_map/dot_general | solution.py:202
  (188 shorter events, 35.6 us)
Async XLA Ops:
  8.7 42.7 %all-to-all-start = ((bf16[32,144,128]{2,1,0:T(8,128)(2,1)}), bf16[32,144,128]{2,1,0:T(8,128)(2,1)S(1)}, u32[]{:S(2)}, u32[]{:S(2)}) async-start(bf16[32,144,128]{2,1,0:T(8,128)(2,1)} %reshape_reshape.13), calls=%async_computation | async-start | bytes 2359296 | tf_op jit(solution)/shard_map/all_to_all | solution.py:97
  21.5 65.3 %copy-start.39 = (f32[2,64]{1,0:T(2,128)}, f32[2,64]{1,0:T(2,128)S(1)}, u32[]{:S(2)}) copy-start(f32[2,64]{1,0:T(2,128)S(1)} %compare_convert_fusion) | copy-start | bytes 1540
  66.4 19.1 %all-to-all-start.1 = ((bf16[32,48,128]{2,1,0:T(8,128)(2,1)}), bf16[32,48,128]{2,1,0:T(8,128)(2,1)S(1)}, u32[]{:S(2)}, u32[]{:S(2)}) async-start(bf16[32,48,128]{2,1,0:T(8,128)(2,1)} %reshape_reshape.14), calls=%async_computation.1 | async-start | bytes 786432 | tf_op jit(solution)/shard_map/all_to_all | solution.py:97
  90.7 9.0 %collective-permute-start = (bf16[2,2,15,1536]{3,2,1,0:T(8,128)(2,1)}, bf16[2,2,15,1536]{3,2,1,0:T(8,128)(2,1)S(1)}, u32[]{:S(2)}, u32[]{:S(2)}) collective-permute-start(bf16[2,2,15,1536]{3,2,1,0:T(8,128)(2,1)} %get-tuple-element.79), channel_id=1, source_target_pairs={{0,1},{1,2},{2,3},{3,4},{4,5},{5,6},{6,7},{7,8},{8,9},{9,10},{10,1... | collective-permute-start | bytes 552968 | tf_op jit(solution)/shard_map/ppermute | solution.py:21
  95.0 7.6 %collective-permute-start.1 = (bf16[2,2,15,1536]{3,2,1,0:T(8,128)(2,1)S(1)}, bf16[2,2,15,1536]{3,2,1,0:T(8,128)(2,1)S(1)}, u32[]{:S(2)}, u32[]{:S(2)}) collective-permute-start(bf16[2,2,15,1536]{3,2,1,0:T(8,128)(2,1)S(1)} %get-tuple-element.80), channel_id=1, source_target_pairs={{1,0},{2,1},{3,2},{4,3},{5,4},{6,5},{7,6},{8,7},{9,8},{10,9},{11,1... | collective-permute-start | bytes 552968 | tf_op jit(solution)/shard_map/ppermute | solution.py:22
  107.4 6.6 %collective-permute-start.2 = (bf16[2,128,1536]{1,2,0:T(8,128)(2,1)S(1)}, bf16[2,128,1536]{1,2,0:T(8,128)(2,1)}, u32[]{:S(2)}, u32[]{:S(2)}) collective-permute-start(bf16[2,128,1536]{1,2,0:T(8,128)(2,1)S(1)} %pad_maximum_fusion.2), channel_id=1, source_target_pairs={{0,32},{32,0},{64,96},{96,64},{128,160},{160,128},{192,224},{224,1... | collective-permute-start | bytes 2359304 | tf_op jit(solution)/shard_map/ppermute | solution.py:57
  146.3 43.8 %copy-start.5 = (f32[1536]{0:T(1024)S(1)}, f32[1536]{0:T(1024)}, u32[]{:S(2)}) copy-start(f32[1536]{0:T(1024)} %copy-done.4) | copy-start | bytes 18436
  146.3 43.8 %copy-start.7 = (f32[1536]{0:T(1024)S(1)}, f32[1536]{0:T(1024)}, u32[]{:S(2)}) copy-start(f32[1536]{0:T(1024)} %copy-done.6) | copy-start | bytes 18436
  146.3 43.8 %copy-start.9 = (f32[1536]{0:T(1024)S(1)}, f32[1536]{0:T(1024)}, u32[]{:S(2)}) copy-start(f32[1536]{0:T(1024)} %copy-done.8) | copy-start | bytes 18436
  146.3 43.8 %copy-start.11 = (f32[1536]{0:T(1024)S(1)}, f32[1536]{0:T(1024)}, u32[]{:S(2)}) copy-start(f32[1536]{0:T(1024)} %copy-done.10) | copy-start | bytes 18436
  146.3 43.8 %copy-start.13 = (f32[1536]{0:T(1024)S(1)}, f32[1536]{0:T(1024)}, u32[]{:S(2)}) copy-start(f32[1536]{0:T(1024)} %copy-done.12) | copy-start | bytes 18436
  146.3 43.8 %copy-start.15 = (f32[1536]{0:T(1024)S(1)}, f32[1536]{0:T(1024)}, u32[]{:S(2)}) copy-start(f32[1536]{0:T(1024)} %copy-done.14) | copy-start | bytes 18436
  146.3 43.8 %copy-start.17 = (f32[1536]{0:T(1024)S(1)}, f32[1536]{0:T(1024)}, u32[]{:S(2)}) copy-start(f32[1536]{0:T(1024)} %get-tuple-element.53) | copy-start | bytes 18436
  146.3 43.8 %copy-start.19 = (f32[1536]{0:T(1024)S(1)}, f32[1536]{0:T(1024)}, u32[]{:S(2)}) copy-start(f32[1536]{0:T(1024)} %get-tuple-element.54) | copy-start | bytes 18436
  146.3 43.8 %copy-start.21 = (f32[1536]{0:T(1024)S(1)}, f32[1536]{0:T(1024)}, u32[]{:S(2)}) copy-start(f32[1536]{0:T(1024)} %get-tuple-element.55) | copy-start | bytes 18436
  146.4 43.8 %copy-start.23 = (f32[1536]{0:T(1024)S(1)}, f32[1536]{0:T(1024)}, u32[]{:S(2)}) copy-start(f32[1536]{0:T(1024)} %get-tuple-element.56) | copy-start | bytes 18436
  157.1 4.2 %collective-permute-start.3 = (f32[12272]{0:T(1024)S(1)}, f32[12272]{0:T(1024)S(1)}, u32[]{:S(2)}, u32[]{:S(2)}) collective-permute-start(f32[12272]{0:T(1024)S(1)} %pad_maximum_fusion.5), channel_id=1, source_target_pairs={{0,1},{1,0},{2,3},{3,2},{4,5},{5,4},{6,7},{7,6},{8,9},{9,8},{10,11... | collective-permute-start | bytes 147272 | tf_op jit(solution)/shard_map/ppermute | solution.py:80
  161.4 5.5 %collective-permute-start.4 = (f32[12272]{0:T(1024)S(1)}, f32[12272]{0:T(1024)S(1)}, u32[]{:S(2)}, u32[]{:S(2)}) collective-permute-start(f32[12272]{0:T(1024)S(1)} %fusion.144), channel_id=1, source_target_pairs={{0,2},{1,3},{2,0},{3,1},{4,6},{5,7},{6,4},{7,5},{8,10},{9,11},{10,... | collective-permute-start | bytes 147272 | tf_op jit(solution)/shard_map/ppermute | solution.py:80
  166.9 8.3 %collective-permute-start.5 = (f32[12272]{0:T(1024)S(1)}, f32[12272]{0:T(1024)S(1)}, u32[]{:S(2)}, u32[]{:S(2)}) collective-permute-start(f32[12272]{0:T(1024)S(1)} %add.345), channel_id=1, source_target_pairs={{0,4},{1,5},{2,6},{3,7},{4,0},{5,1},{6,2},{7,3},{8,12},{9,13},{10,... | collective-permute-start | bytes 147272 | tf_op jit(solution)/shard_map/ppermute | solution.py:80
  175.2 4.3 %collective-permute-start.6 = (f32[12272]{0:T(1024)S(1)}, f32[12272]{0:T(1024)S(1)}, u32[]{:S(2)}, u32[]{:S(2)}) collective-permute-start(f32[12272]{0:T(1024)S(1)} %add.346), channel_id=1, source_target_pairs={{0,8},{1,9},{2,10},{3,11},{4,12},{5,13},{6,14},{7,15},{8,0},{9,1},... | collective-permute-start | bytes 147272 | tf_op jit(solution)/shard_map/ppermute | solution.py:80
  179.5 5.7 %collective-permute-start.7 = (f32[12272]{0:T(1024)S(1)}, f32[12272]{0:T(1024)S(1)}, u32[]{:S(2)}, u32[]{:S(2)}) collective-permute-start(f32[12272]{0:T(1024)S(1)} %add.347), channel_id=1, source_target_pairs={{0,16},{1,17},{2,18},{3,19},{4,20},{5,21},{6,22},{7,23},{8,24},{9,... | collective-permute-start | bytes 147272 | tf_op jit(solution)/shard_map/ppermute | solution.py:80
  185.2 4.2 %collective-permute-start.8 = (f32[12272]{0:T(1024)S(1)}, f32[12272]{0:T(1024)S(1)}, u32[]{:S(2)}, u32[]{:S(2)}) collective-permute-start(f32[12272]{0:T(1024)S(1)} %add.348), channel_id=1, source_target_pairs={{0,64},{32,96},{64,0},{96,32},{128,192},{160,224},{192,128},{224,1... | collective-permute-start | bytes 147272 | tf_op jit(solution)/shard_map/ppermute | solution.py:80
  189.4 5.9 %collective-permute-start.9 = (f32[12272]{0:T(1024)S(1)}, f32[12272]{0:T(1024)S(1)}, u32[]{:S(2)}, u32[]{:S(2)}) collective-permute-start(f32[12272]{0:T(1024)S(1)} %add.349), channel_id=1, source_target_pairs={{0,128},{32,160},{64,192},{96,224},{128,0},{160,32},{192,64},{224,... | collective-permute-start | bytes 147272 | tf_op jit(solution)/shard_map/ppermute | solution.py:80
  195.3 2.5 %collective-permute-start.10 = (f32[12272]{0:T(1024)S(1)}, f32[12272]{0:T(1024)S(1)}, u32[]{:S(2)}, u32[]{:S(2)}) collective-permute-start(f32[12272]{0:T(1024)S(1)} %add.350), channel_id=1, source_target_pairs={{0,32},{32,0},{64,96},{96,64},{128,160},{160,128},{192,224},{224,1... | collective-permute-start | bytes 147272 | tf_op jit(solution)/shard_map/ppermute | solution.py:211
  (34 other events, 790.9 us)

commit v7 on v4

--- a/solution.py
+++ b/solution.py
@@ -106,7 +106,7 @@
     stacked = stacked.reshape(3, local_utts, frames_dev, HEADS, head_size)
     stacked = stacked.transpose(3, 1, 0, 2, 4).reshape(seq_count, 3, frames_dev, head_size)
     gathered = lane_dense_all_to_all(stacked)
-    gathered, later = lax.optimization_barrier((gathered, later))
+    later = later
     gathered = gathered.transpose(1, 0, 2, 3).reshape(3, full_frames, head_size)
     length = utt_lengths[seq_index % local_utts]
     key_ok = jnp.arange(full_frames, dtype=jnp.int32) < length

time: 201 us -> 201 us (level)
  no operation moved by 1% of the time
where the time goes in v7:
time: 201 us; the launch traced here: 199 us
  waiting for transfers between devices  70.4 us (35%)
  local copies, waits for them, and re-layouts  44.6 us (22%)
  other arithmetic  35.5 us (18%)
  starting transfers between devices  29.4 us (15%)
  matrix products  17.2 us (9%)
    all_to_all x2, waiting for transfers between devices, lane_dense_all_to_all(): return lax.all_to_all(dense, 'seq', 0, 0, tiled=True).reshape(value.shape)  40.9 us
    ppermute x7, waiting for transfers between devices, butterfly_sum(): value = value + lax.ppermute(value, axis, pairs)  26.6 us
    gather x1, local copies, waits for them, and re-layouts, block_entries(): chosen = jnp.take(blocks, block_of, axis=0)  26.4 us
    all_to_all x2, starting transfers between devices, lane_dense_all_to_all(): return lax.all_to_all(dense, 'seq', 0, 0, tiled=True).reshape(value.shape)  16.7 us
    reduce_sum x1, other arithmetic, block_entries(): return jnp.sum(jnp.where(hit, chosen, jnp.float32(0.0)), axis=1)  10.5 us
    ppermute x7, starting transfers between devices, butterfly_sum(): value = value + lax.ppermute(value, axis, pairs)  7.01 us
    reduce_sum x1, other arithmetic, softmax_rows(): return (probs.astype(jnp.bfloat16), jnp.sum(probs, axis=-1))  4.87 us
    another operation x6, local copies, waits for them, and re-layouts, head_attention(): stacked = jnp.stack([queries, key_rows, value_rows])  4.72 us
  transfers between devices with their start and end apart: 13, of which 10 were waited for; matrix products, arithmetic and copies ran while one was open for 10% of the time, Pallas kernels for 0%

profile of v7, /device:TPU:16, one launch (start us, length us, event | category | flops | bytes accessed | tf_op | source)
XLA Modules:
  0.0 198.9 jit_solution(14990081774400145035)
XLA Ops:
  5.8 3.0 %reshape_reshape.13 = bf16[32,144,128]{2,1,0:T(8,128)(2,1)} reshape(bf16[16,2,3,64,96]{4,3,2,1,0:T(8,128)(2,1)S(1)} %maximum_bitcast_fusion) | data formatting | bytes 2359296 | tf_op jit(solution)/shard_map/reshape;reshape | solution.py:96
  8.7 11.3 %all-to-all-start = ((bf16[32,144,128]{2,1,0:T(8,128)(2,1)}), bf16[32,144,128]{2,1,0:T(8,128)(2,1)S(1)}, u32[]{:S(2)}, u32[]{:S(2)}) async-start(bf16[32,144,128]{2,1,0:T(8,128)(2,1)} %reshape_reshape.13), calls=%async_computation | async-start | bytes 2359296 | tf_op jit(solution)/shard_map/all_to_all | solution.py:97
  22.6 28.8 %all-to-all-done = bf16[32,144,128]{2,1,0:T(8,128)(2,1)S(1)} async-done(((bf16[32,144,128]{2,1,0:T(8,128)(2,1)}), bf16[32,144,128]{2,1,0:T(8,128)(2,1)S(1)}, u32[]{:S(2)}, u32[]{:S(2)}) %all-to-all-start) | async-done | bytes 1179680 | tf_op jit(solution)/shard_map/all_to_all | solution.py:97
  52.6 3.3 %fusion = (f32[2048]{0:T(1024)S(1)}, f32[2048,2048]{0,1:T(8,128)S(1)}) fusion(pred[2048]{0:T(1024)(128)(4,1)S(1)} %iota_compare_fusion.2, bf16[2048,96]{1,0:T(8,128)(2,1)S(1)} %bitcast.66, bf16[2048,96]{1,0:T(8,128)(2,1)S(1)} %bitcast.67), kind=kOutput, calls=%fused_computation.4 | convolution fusion | flops 817887232 | bytes 17573888 | tf_op jit(solution)/shard_map/dot_general | solution.py:86
  55.9 4.9 %fusion.1 = f32[2048]{0:T(1024)S(1)} fusion(f32[2048,2048]{0,1:T(8,128)S(1)} %get-tuple-element.80, f32[2048]{0:T(1024)S(1)} %get-tuple-element.79, pred[2048]{0:T(1024)(128)(4,1)S(1)} %iota_compare_fusion.2), kind=kLoop, calls=%fused_computation.5 | loop fusion | flops 16775168 | bytes 16795648 | tf_op jit(solution)/shard_map/reduce_sum | solution.py:31
  60.8 3.9 %fusion.28 = bf16[2048,96]{0,1:T(8,128)(2,1)S(1)} fusion(bf16[2048,96]{1,0:T(8,128)(2,1)S(1)} %bitcast.68, f32[2048,2048]{0,1:T(8,128)S(1)} %get-tuple-element.80, f32[2048]{0:T(1024)S(1)} %get-tuple-element.79, pred[2048]{0:T(1024)(128)(4,1)S(1)} %iota_compare_fusion.2, f32[2048]{0:T(1024)S(1)} %fusion.1), kind=kOutput, calls=%fused_computation.52 | convolution fusion | flops 822476800 | bytes 17582080 | tf_op jit(solution)/shard_map/dot_general | solution.py:88
  66.4 5.4 %all-to-all-start.1 = ((bf16[32,48,128]{2,1,0:T(8,128)(2,1)}), bf16[32,48,128]{2,1,0:T(8,128)(2,1)S(1)}, u32[]{:S(2)}, u32[]{:S(2)}) async-start(bf16[32,48,128]{2,1,0:T(8,128)(2,1)} %reshape_reshape.14), calls=%async_computation.1 | async-start | bytes 786432 | tf_op jit(solution)/shard_map/all_to_all | solution.py:97
  73.4 12.1 %all-to-all-done.1 = bf16[32,48,128]{2,1,0:T(8,128)(2,1)S(1)} async-done(((bf16[32,48,128]{2,1,0:T(8,128)(2,1)}), bf16[32,48,128]{2,1,0:T(8,128)(2,1)S(1)}, u32[]{:S(2)}, u32[]{:S(2)}) %all-to-all-start.1) | async-done | bytes 393248 | tf_op jit(solution)/shard_map/all_to_all | solution.py:97
  86.8 3.1 %fusion.22 = bf16[1,2,64,1536]{3,2,1,0:T(8,128)(2,1)S(1)} fusion(bf16[2,64,1536]{2,1,0:T(8,128)(2,1)S(1)} %dot_general.19, bf16[1536,1536]{1,0:T(8,128)(2,1)} %param.15, bf16[2,64,1536]{2,1,0:T(8,128)(2,1)S(1)} %copy-done.1, f32[2,64]{1,0:T(2,128)S(1)} %compare_convert_fusion), kind=kOutput, calls=%fused_computation.50 | convolution fusion | flops 604766208 | bytes 5898752 | tf_op jit(solution)/shard_map/dot_general | solution.py:175
  90.7 4.3 %collective-permute-start = (bf16[2,2,15,1536]{3,2,1,0:T(8,128)(2,1)}, bf16[2,2,15,1536]{3,2,1,0:T(8,128)(2,1)S(1)}, u32[]{:S(2)}, u32[]{:S(2)}) collective-permute-start(bf16[2,2,15,1536]{3,2,1,0:T(8,128)(2,1)} %get-tuple-element.75), channel_id=1, source_target_pairs={{0,1},{1,2},{2,3},{3,4},{4,5},{5,6},{6,7},{7,8},{8,9},{9,10},{10,1... | collective-permute-start | bytes 552968 | tf_op jit(solution)/shard_map/ppermute | solution.py:21
  99.7 2.8 %collective-permute-done.1 = bf16[2,2,15,1536]{3,2,1,0:T(8,128)(2,1)S(1)} collective-permute-done((bf16[2,2,15,1536]{3,2,1,0:T(8,128)(2,1)S(1)}, bf16[2,2,15,1536]{3,2,1,0:T(8,128)(2,1)S(1)}, u32[]{:S(2)}, u32[]{:S(2)}) %collective-permute-start.1) | collective-permute-done | bytes 184352 | tf_op jit(solution)/shard_map/ppermute | solution.py:22
  103.0 4.0 %fusion.96 = bf16[2,64,1536]{2,1,0:T(8,128)(2,1)S(1)} fusion(f32[2,94,1536]{2,1,0:T(8,128)S(1)} %get-tuple-element.73, f32[1536]{0:T(1024)S(1)} %get-tuple-element.36, f32[1536]{0:T(1024)S(1)} %get-tuple-element.37, f32[1536]{0:T(1024)S(1)} %get-tuple-element.38, f32[1536]{0:T(1024)S(1)} %get-tuple-element.39, f32[1536]{0:T(1024)S(1)} %get-tuple-element.40, ...), kind=kLoop, calls=%fused_computation.154 | loop fusion | flops 12386304 | bytes 24963584 | tf_op jit(solution)/shard_map/convert_element_type | solution.py:200
  107.5 2.1 %fusion.92 = (f32[1536]{0:T(1024)S(1)}, f32[1536]{0:T(1024)S(1)}, f32[1536]{0:T(1024)S(1)}, f32[1536]{0:T(1024)S(1)}, f32[1536]{0:T(1024)S(1)}, /*index=5*/f32[1...) fusion(bf16[2,64,1536]{2,1,0:T(8,128)(2,1)S(1)} %copy-done, ...), kind=kLoop, calls=%fused_computation.148 | loop fusion | flops 10785792 | bytes 7581696 | tf_op jit(solution)/shard_map/reduce_sum | solution.py:192
  115.4 4.5 %fusion.93 = f32[1536,12,128]{2,0,1:T(8,128)} fusion(bf16[256,12,128]{0,2,1:T(8,128)(2,1)S(1)} %bitcast.65, bf16[2,256,1536]{1,2,0:T(8,128)(2,1)S(1)} %pad_maximum_fusion), kind=kOutput, calls=%fused_computation.150 | convolution fusion | flops 1207959552 | bytes 11010048 | tf_op jit(solution)/shard_map/ncl,nr->crl/dot_general | solution.py:62
  119.9 26.4 %gather_fusion = f32[11796,128]{1,0:T(8,128)} fusion(f32[18432,128]{1,0:T(8,128)} %bitcast.56, s32[12288]{0:T(1024)S(1)} %pad_clamp_fusion), kind=kCustom, calls=%fused_computation | custom fusion | bytes 12126288 | tf_op jit(solution)/shard_map/jit(_take)/gather | solution.py:44
  146.5 10.5 %select_reduce_fusion = f32[11796]{0:T(1024)S(1)} fusion(f32[11796,128]{1,0:T(8,128)} %gather_fusion, s32[11796]{0:T(1024)S(1)} %add_select_fusion.3, pred[11796]{0:T(1024)(128)(4,1)S(1)} %copy-done.38), kind=kLoop, calls=%fused_computation.40 | loop fusion | flops 6027756 | bytes 6145716 | tf_op jit(solution)/shard_map/reduce_sum | solution.py:47
  158.4 2.9 %collective-permute-done.3 = f32[12272]{0:T(1024)S(1)} collective-permute-done((f32[12272]{0:T(1024)S(1)}, f32[12272]{0:T(1024)S(1)}, u32[]{:S(2)}, u32[]{:S(2)}) %collective-permute-start.3) | collective-permute-done | bytes 49120 | tf_op jit(solution)/shard_map/ppermute | solution.py:80
  161.7 5.3 %collective-permute-done.4 = f32[12272]{0:T(1024)S(1)} collective-permute-done((f32[12272]{0:T(1024)S(1)}, f32[12272]{0:T(1024)S(1)}, u32[]{:S(2)}, u32[]{:S(2)}) %collective-permute-start.4) | collective-permute-done | bytes 49120 | tf_op jit(solution)/shard_map/ppermute | solution.py:80
  167.6 3.5 %collective-permute-done.5 = f32[12272]{0:T(1024)S(1)} collective-permute-done((f32[12272]{0:T(1024)S(1)}, f32[12272]{0:T(1024)S(1)}, u32[]{:S(2)}, u32[]{:S(2)}) %collective-permute-start.5) | collective-permute-done | bytes 49120 | tf_op jit(solution)/shard_map/ppermute | solution.py:80
  172.2 4.6 %collective-permute-done.6 = f32[12272]{0:T(1024)S(1)} collective-permute-done((f32[12272]{0:T(1024)S(1)}, f32[12272]{0:T(1024)S(1)}, u32[]{:S(2)}, u32[]{:S(2)}) %collective-permute-start.6) | collective-permute-done | bytes 49120 | tf_op jit(solution)/shard_map/ppermute | solution.py:80
  178.2 6.6 %collective-permute-done.7 = f32[12272]{0:T(1024)S(1)} collective-permute-done((f32[12272]{0:T(1024)S(1)}, f32[12272]{0:T(1024)S(1)}, u32[]{:S(2)}, u32[]{:S(2)}) %collective-permute-start.7) | collective-permute-done | bytes 49120 | tf_op jit(solution)/shard_map/ppermute | solution.py:80
  185.4 3.6 %collective-permute-done.8 = f32[12272]{0:T(1024)S(1)} collective-permute-done((f32[12272]{0:T(1024)S(1)}, f32[12272]{0:T(1024)S(1)}, u32[]{:S(2)}, u32[]{:S(2)}) %collective-permute-start.8) | collective-permute-done | bytes 49120 | tf_op jit(solution)/shard_map/ppermute | solution.py:80
  190.9 3.9 %fusion.61 = bf16[2,64,1536]{2,1,0:T(8,128)(2,1)} fusion(f32[1536]{0:T(1024)S(1)} %get-tuple-element.36, f32[1536]{0:T(1024)S(1)} %get-tuple-element.37, f32[1536]{0:T(1024)S(1)} %get-tuple-element.38, f32[1536]{0:T(1024)S(1)} %get-tuple-element.39, f32[1536]{0:T(1024)S(1)} %get-tuple-element.40, f32[1536]{0:T(1024)S(1)} %get-tuple-element.41, ...), kind=kLoop, calls=%fused_computation.117 | loop fusion | flops 18284544 | bytes 12773376 | tf_op jit(solution)/shard_map/convert_element_type | solution.py:193
  195.1 2.4 %fusion.16 = bf16[2,64,1536]{2,1,0:T(8,128)(2,1)} fusion(bf16[2,64,1536]{2,1,0:T(8,128)(2,1)S(1)} %fusion.96, bf16[1536,1536]{1,0:T(8,128)(2,1)S(1)} %bitcast.58), kind=kOutput, calls=%fused_computation.48 | convolution fusion | flops 604176384 | bytes 5505024 | tf_op jit(solution)/shard_map/dot_general | solution.py:202
  (188 shorter events, 34.0 us)
Async XLA Ops:
  8.7 42.7 %all-to-all-start = ((bf16[32,144,128]{2,1,0:T(8,128)(2,1)}), bf16[32,144,128]{2,1,0:T(8,128)(2,1)S(1)}, u32[]{:S(2)}, u32[]{:S(2)}) async-start(bf16[32,144,128]{2,1,0:T(8,128)(2,1)} %reshape_reshape.13), calls=%async_computation | async-start | bytes 2359296 | tf_op jit(solution)/shard_map/all_to_all | solution.py:97
  21.5 65.3 %copy-start.39 = (f32[2,64]{1,0:T(2,128)}, f32[2,64]{1,0:T(2,128)S(1)}, u32[]{:S(2)}) copy-start(f32[2,64]{1,0:T(2,128)S(1)} %compare_convert_fusion) | copy-start | bytes 1540
  66.4 19.1 %all-to-all-start.1 = ((bf16[32,48,128]{2,1,0:T(8,128)(2,1)}), bf16[32,48,128]{2,1,0:T(8,128)(2,1)S(1)}, u32[]{:S(2)}, u32[]{:S(2)}) async-start(bf16[32,48,128]{2,1,0:T(8,128)(2,1)} %reshape_reshape.14), calls=%async_computation.1 | async-start | bytes 786432 | tf_op jit(solution)/shard_map/all_to_all | solution.py:97
  90.7 9.0 %collective-permute-start = (bf16[2,2,15,1536]{3,2,1,0:T(8,128)(2,1)}, bf16[2,2,15,1536]{3,2,1,0:T(8,128)(2,1)S(1)}, u32[]{:S(2)}, u32[]{:S(2)}) collective-permute-start(bf16[2,2,15,1536]{3,2,1,0:T(8,128)(2,1)} %get-tuple-element.75), channel_id=1, source_target_pairs={{0,1},{1,2},{2,3},{3,4},{4,5},{5,6},{6,7},{7,8},{8,9},{9,10},{10,1... | collective-permute-start | bytes 552968 | tf_op jit(solution)/shard_map/ppermute | solution.py:21
  95.0 7.6 %collective-permute-start.1 = (bf16[2,2,15,1536]{3,2,1,0:T(8,128)(2,1)S(1)}, bf16[2,2,15,1536]{3,2,1,0:T(8,128)(2,1)S(1)}, u32[]{:S(2)}, u32[]{:S(2)}) collective-permute-start(bf16[2,2,15,1536]{3,2,1,0:T(8,128)(2,1)S(1)} %get-tuple-element.76), channel_id=1, source_target_pairs={{1,0},{2,1},{3,2},{4,3},{5,4},{6,5},{7,6},{8,7},{9,8},{10,9},{11,1... | collective-permute-start | bytes 552968 | tf_op jit(solution)/shard_map/ppermute | solution.py:22
  107.4 6.6 %collective-permute-start.2 = (bf16[2,128,1536]{1,2,0:T(8,128)(2,1)S(1)}, bf16[2,128,1536]{1,2,0:T(8,128)(2,1)}, u32[]{:S(2)}, u32[]{:S(2)}) collective-permute-start(bf16[2,128,1536]{1,2,0:T(8,128)(2,1)S(1)} %pad_maximum_fusion.2), channel_id=1, source_target_pairs={{0,32},{32,0},{64,96},{96,64},{128,160},{160,128},{192,224},{224,1... | collective-permute-start | bytes 2359304 | tf_op jit(solution)/shard_map/ppermute | solution.py:57
  146.3 44.4 %copy-start.5 = (f32[1536]{0:T(1024)S(1)}, f32[1536]{0:T(1024)}, u32[]{:S(2)}) copy-start(f32[1536]{0:T(1024)} %copy-done.4) | copy-start | bytes 18436
  146.3 44.4 %copy-start.7 = (f32[1536]{0:T(1024)S(1)}, f32[1536]{0:T(1024)}, u32[]{:S(2)}) copy-start(f32[1536]{0:T(1024)} %copy-done.6) | copy-start | bytes 18436
  146.3 44.4 %copy-start.9 = (f32[1536]{0:T(1024)S(1)}, f32[1536]{0:T(1024)}, u32[]{:S(2)}) copy-start(f32[1536]{0:T(1024)} %copy-done.8) | copy-start | bytes 18436
  146.3 44.4 %copy-start.11 = (f32[1536]{0:T(1024)S(1)}, f32[1536]{0:T(1024)}, u32[]{:S(2)}) copy-start(f32[1536]{0:T(1024)} %copy-done.10) | copy-start | bytes 18436
  146.3 44.4 %copy-start.13 = (f32[1536]{0:T(1024)S(1)}, f32[1536]{0:T(1024)}, u32[]{:S(2)}) copy-start(f32[1536]{0:T(1024)} %copy-done.12) | copy-start | bytes 18436
  146.3 44.4 %copy-start.15 = (f32[1536]{0:T(1024)S(1)}, f32[1536]{0:T(1024)}, u32[]{:S(2)}) copy-start(f32[1536]{0:T(1024)} %copy-done.14) | copy-start | bytes 18436
  146.3 44.4 %copy-start.17 = (f32[1536]{0:T(1024)S(1)}, f32[1536]{0:T(1024)}, u32[]{:S(2)}) copy-start(f32[1536]{0:T(1024)} %get-tuple-element.49) | copy-start | bytes 18436
  146.3 44.4 %copy-start.19 = (f32[1536]{0:T(1024)S(1)}, f32[1536]{0:T(1024)}, u32[]{:S(2)}) copy-start(f32[1536]{0:T(1024)} %get-tuple-element.50) | copy-start | bytes 18436
  146.3 44.4 %copy-start.21 = (f32[1536]{0:T(1024)S(1)}, f32[1536]{0:T(1024)}, u32[]{:S(2)}) copy-start(f32[1536]{0:T(1024)} %get-tuple-element.51) | copy-start | bytes 18436
  146.4 44.4 %copy-start.23 = (f32[1536]{0:T(1024)S(1)}, f32[1536]{0:T(1024)}, u32[]{:S(2)}) copy-start(f32[1536]{0:T(1024)} %get-tuple-element.52) | copy-start | bytes 18436
  157.1 4.2 %collective-permute-start.3 = (f32[12272]{0:T(1024)S(1)}, f32[12272]{0:T(1024)S(1)}, u32[]{:S(2)}, u32[]{:S(2)}) collective-permute-start(f32[12272]{0:T(1024)S(1)} %pad_maximum_fusion.5), channel_id=1, source_target_pairs={{0,64},{32,96},{64,0},{96,32},{128,192},{160,224},{192,128},{224,1... | collective-permute-start | bytes 147272 | tf_op jit(solution)/shard_map/ppermute | solution.py:80
  161.4 5.6 %collective-permute-start.4 = (f32[12272]{0:T(1024)S(1)}, f32[12272]{0:T(1024)S(1)}, u32[]{:S(2)}, u32[]{:S(2)}) collective-permute-start(f32[12272]{0:T(1024)S(1)} %fusion.144), channel_id=1, source_target_pairs={{0,128},{32,160},{64,192},{96,224},{128,0},{160,32},{192,64},{224,... | collective-permute-start | bytes 147272 | tf_op jit(solution)/shard_map/ppermute | solution.py:80
  167.0 4.2 %collective-permute-start.5 = (f32[12272]{0:T(1024)S(1)}, f32[12272]{0:T(1024)S(1)}, u32[]{:S(2)}, u32[]{:S(2)}) collective-permute-start(f32[12272]{0:T(1024)S(1)} %add.345), channel_id=1, source_target_pairs={{0,1},{1,0},{2,3},{3,2},{4,5},{5,4},{6,7},{7,6},{8,9},{9,8},{10,11... | collective-permute-start | bytes 147272 | tf_op jit(solution)/shard_map/ppermute | solution.py:80
  171.2 5.6 %collective-permute-start.6 = (f32[12272]{0:T(1024)S(1)}, f32[12272]{0:T(1024)S(1)}, u32[]{:S(2)}, u32[]{:S(2)}) collective-permute-start(f32[12272]{0:T(1024)S(1)} %add.346), channel_id=1, source_target_pairs={{0,2},{1,3},{2,0},{3,1},{4,6},{5,7},{6,4},{7,5},{8,10},{9,11},{10,... | collective-permute-start | bytes 147272 | tf_op jit(solution)/shard_map/ppermute | solution.py:80
  176.8 8.1 %collective-permute-start.7 = (f32[12272]{0:T(1024)S(1)}, f32[12272]{0:T(1024)S(1)}, u32[]{:S(2)}, u32[]{:S(2)}) collective-permute-start(f32[12272]{0:T(1024)S(1)} %add.347), channel_id=1, source_target_pairs={{0,4},{1,5},{2,6},{3,7},{4,0},{5,1},{6,2},{7,3},{8,12},{9,13},{10,... | collective-permute-start | bytes 147272 | tf_op jit(solution)/shard_map/ppermute | solution.py:80
  184.9 4.2 %collective-permute-start.8 = (f32[12272]{0:T(1024)S(1)}, f32[12272]{0:T(1024)S(1)}, u32[]{:S(2)}, u32[]{:S(2)}) collective-permute-start(f32[12272]{0:T(1024)S(1)} %add.348), channel_id=1, source_target_pairs={{0,8},{1,9},{2,10},{3,11},{4,12},{5,13},{6,14},{7,15},{8,0},{9,1},... | collective-permute-start | bytes 147272 | tf_op jit(solution)/shard_map/ppermute | solution.py:80
  189.1 5.9 %collective-permute-start.9 = (f32[12272]{0:T(1024)S(1)}, f32[12272]{0:T(1024)S(1)}, u32[]{:S(2)}, u32[]{:S(2)}) collective-permute-start(f32[12272]{0:T(1024)S(1)} %add.349), channel_id=1, source_target_pairs={{0,16},{1,17},{2,18},{3,19},{4,20},{5,21},{6,22},{7,23},{8,24},{9,... | collective-permute-start | bytes 147272 | tf_op jit(solution)/shard_map/ppermute | solution.py:80
  195.0 2.5 %collective-permute-start.10 = (f32[12272]{0:T(1024)S(1)}, f32[12272]{0:T(1024)S(1)}, u32[]{:S(2)}, u32[]{:S(2)}) collective-permute-start(f32[12272]{0:T(1024)S(1)} %add.350), channel_id=1, source_target_pairs={{0,32},{32,0},{64,96},{96,64},{128,160},{160,128},{192,224},{224,1... | collective-permute-start | bytes 147272 | tf_op jit(solution)/shard_map/ppermute | solution.py:211
  (34 other events, 799.6 us)
